TPU v7x, 32 devices: a whole 2x2x4 slice. The times are simulated.
32 devices in a mesh: tile: 4 (over x, core), mem: 8 (over z, y).
Axes of the slice: x: 2, y: 2, z: 4, core: 2. Of those that a mesh axis runs over, the one named last changes fastest.
Arguments:
- perturbations: bfloat16 [32, 2, 16, 16, 512], P('mem', None, 'tile'), may hold values from -3 to 3
- innovations: float32 [4, 32768], P('tile', 'mem'), may hold values from -6 to 6
- obs_weight: float32 [4, 32768], P('tile', 'mem'), may hold values from 0.4 to 4
- obs_cell: int32 [4, 32768], P('tile', 'mem'), may hold values from 0 to 8191
- row_start: int32 [16], P('tile'), may hold values from 0 to 511
- row_length: int32 [16], P('tile'), may hold values from 256 to 512
- lat_rate: float32 [16], replicated, may hold values from 0.3 to 0.4
- lon_rate: float32 [16], replicated, may hold values from 0.02 to 0.1
Outputs:
- control: float32 [32, 16, 16, 512], P('mem', 'tile')
- increment: float32 [2, 16, 8192], P(None, 'tile', 'mem')
All inputs are finite; a program needn't handle non-finite values.
Results may differ from a plain program's by a relative error of at most 0.0003.
Values sent between devices are 32-bit elements; how exact they have to be, the bound alone decides.
No kernel may reach another device: no remote copies, remote signals or barrier semaphores. Data moves between devices by JAX's collectives and lax.ppermute only.
A program may use at most 64 MiB of HBM per device.

v0:
```python
import jax
import jax.numpy as jnp
from jax import lax
from jax.sharding import PartitionSpec as P

ITERS = 2
STEPS = 8


def row_mask(starts, lengths, nlon):
    lon = lax.broadcasted_iota(jnp.int32, (starts.shape[0], nlon), 1)
    rel = (lon - starts[:, None]) % nlon
    return jnp.where(rel < lengths[:, None], 1.0, 0.0).astype(jnp.float32)[:, None, :]


def diffuse_step(field, mask, lat_rate, lon_rate):
    zero = jnp.zeros_like(field[:, :1])
    north = jnp.concatenate([field[:, 1:], zero], axis=1)
    south = jnp.concatenate([zero, field[:, :-1]], axis=1)
    east = jnp.roll(field, -1, axis=3)
    west = jnp.roll(field, 1, axis=3)
    lat_term = north + south - 2.0 * field
    lon_term = east + west - 2.0 * field
    return mask * (
        field + lat_rate[:, None, None, None] * lat_term + lon_rate[:, None, None, None] * lon_term
    )


def global_sum(value):
    axes = ("tile", "mem")
    count = lax.axis_size(axes)
    value = jnp.asarray(value, jnp.float32)
    spread = jnp.broadcast_to(value, (count,) + value.shape)
    return jnp.sum(lax.all_to_all(spread, axes, 0, 0, tiled=True), axis=0)


def add_at_cells(cells, values, size):
    lanes = 128
    count, kinds = values.shape
    high = lax.broadcasted_iota(jnp.int32, (count, size // lanes), 1) == (cells // lanes)[:, None]
    low = lax.broadcasted_iota(jnp.int32, (count, lanes), 1) == (cells % lanes)[:, None]
    spread = values[:, :, None] * low.astype(jnp.float32)[:, None, :]
    summed = jnp.dot(
        high.astype(jnp.float32).T,
        spread.reshape(count, kinds * lanes),
        precision=lax.Precision.HIGHEST,
        preferred_element_type=jnp.float32,
    )
    return summed.reshape(size // lanes, kinds, lanes).transpose(0, 2, 1).reshape(size, kinds)


def gather_rows(block, dim):
    count = lax.axis_size("tile")
    shape = block.shape
    copies = jnp.broadcast_to(
        jnp.expand_dims(block, dim), shape[:dim] + (count,) + shape[dim:]
    )
    joined = lax.all_to_all(copies, "tile", dim, dim, tiled=True)
    return joined.reshape(shape[:dim] + (count * shape[dim],) + shape[dim + 1 :])


def gather_rows_by_permutes(block, dim):
    count = lax.axis_size("tile")
    me = lax.axis_index("tile")
    pieces = [block] + [
        lax.ppermute(block, "tile", [(i, (i + k) % count) for i in range(count)])
        for k in range(1, count)
    ]
    by_offset = jnp.stack([pieces[(count - q) % count] for q in range(count)], axis=dim)
    ordered = jnp.roll(by_offset, me, axis=dim)
    shape = block.shape
    return ordered.reshape(shape[:dim] + (count * shape[dim],) + shape[dim + 1 :])


def reduce_rows_by_permutes(block, dim):
    count = lax.axis_size("tile")
    me = lax.axis_index("tile")
    share = block.shape[dim] // count
    total = lax.dynamic_slice_in_dim(block, me * share, share, axis=dim)
    for k in range(1, count):
        piece = lax.dynamic_slice_in_dim(block, ((me + k) % count) * share, share, axis=dim)
        total = total + lax.ppermute(piece, "tile", [(i, (i + k) % count) for i in range(count)])
    return total


def sum_over_tile_by_permutes(block):
    count = lax.axis_size("tile")
    total = block
    for k in range(1, count):
        total = total + lax.ppermute(block, "tile", [(i, (i + k) % count) for i in range(count)])
    return total


def reduce_rows(block, dim):
    count = lax.axis_size("tile")
    shape = block.shape
    parts = block.reshape(shape[:dim] + (count, shape[dim] // count) + shape[dim + 1 :])
    received = lax.all_to_all(parts, "tile", dim, dim, tiled=True)
    return jnp.sum(received, axis=dim)


def body(
    perturbations, innovations, obs_weight, obs_cell, row_start, row_length, lat_rate, lon_rate
):
    slots = perturbations.shape[1]
    lat_rows = perturbations.shape[2]
    levels = perturbations.shape[3]
    nlon = perturbations.shape[4]
    groups = lax.axis_size("mem")
    own_levels = levels // groups
    shard_cols = own_levels * nlon
    first = lax.axis_index("mem") * own_levels
    lat_own = lax.dynamic_slice_in_dim(lat_rate, first, own_levels)
    lon_own = lax.dynamic_slice_in_dim(lon_rate, first, own_levels)

    tiles = lax.axis_size("tile")
    local_members = perturbations.shape[0]
    share = local_members // tiles
    if share and local_members % tiles == 0:
        sent = perturbations.astype(jnp.float32).reshape(
            tiles, share, slots, lat_rows, groups, own_levels, nlon
        )
        sent = sent.transpose(0, 4, 2, 5, 3, 1, 6).reshape(
            tiles * groups, slots, own_levels, lat_rows, share, nlon
        )
        got = lax.all_to_all(sent, ("tile", "mem"), 0, 0, tiled=True)
        pert = got.reshape(tiles, groups, slots, own_levels, lat_rows, share, nlon)
        pert = pert.transpose(2, 3, 0, 4, 1, 5, 6).reshape(
            slots, own_levels, tiles * lat_rows, groups * share, nlon
        )
    else:
        pert = lax.all_to_all(
            perturbations.astype(jnp.float32).transpose(1, 3, 2, 0, 4),
            "mem",
            split_axis=1,
            concat_axis=3,
            tiled=True,
        )
        pert = lax.all_to_all(pert, "tile", split_axis=3, concat_axis=2, tiled=True)

    def smooth(field):
        current = mask * field
        return lax.fori_loop(
            0, STEPS, lambda inner, now: diffuse_step(now, mask, lat_own, lon_own), current, unroll=4
        )

    def forward(control):
        smoothed = smooth(control)
        return sum_over_tile_by_permutes(jnp.sum(pert * smoothed[None], axis=3))

    def adjoint(gradient):
        return smooth(jnp.sum(pert * gradient[:, :, :, None], axis=0))

    def to_output(control):
        if share and local_members % tiles == 0:
            sent = control.reshape(own_levels, tiles, lat_rows, groups, share, nlon)
            sent = sent.transpose(1, 3, 0, 2, 4, 5).reshape(
                tiles * groups, own_levels, lat_rows, share, nlon
            )
            got = lax.all_to_all(sent, ("tile", "mem"), 0, 0, tiled=True)
            control = got.reshape(tiles, groups, own_levels, lat_rows, share, nlon)
            control = control.transpose(0, 4, 3, 1, 2, 5).reshape(
                tiles * share, lat_rows, levels, nlon
            )
        else:
            control = lax.all_to_all(control, "tile", split_axis=1, concat_axis=2, tiled=True)
            control = lax.all_to_all(control, "mem", split_axis=2, concat_axis=0, tiled=True)
            control = control.transpose(2, 1, 0, 3)
        return control

    local_cells = obs_cell[0]
    innov = innovations[0]
    weight = obs_weight[0]
    size = slots * lat_rows * shard_cols
    state_shape = (slots, own_levels, lat_rows, nlon)
    gathered = add_at_cells(local_cells, jnp.stack([weight * innov, weight], axis=1), size)
    gathered = gathered.reshape(slots, lat_rows, own_levels, nlon, 2).transpose(4, 0, 2, 1, 3)

    tables = jnp.zeros((lat_rows, nlon), jnp.float32)
    tables = tables.at[:, 0].set(row_start.astype(jnp.float32))
    tables = tables.at[:, 1].set(row_length.astype(jnp.float32))
    payload = jnp.concatenate(
        [gathered.reshape(2 * slots * own_levels, lat_rows, nlon), tables[None]], axis=0
    )
    payload = gather_rows_by_permutes(payload, 1)
    tables = payload[-1, :, :2].astype(jnp.int32)
    mask = row_mask(tables[:, 0], tables[:, 1], nlon)
    both = payload[:-1].reshape(2, slots, own_levels, tiles * lat_rows, nlon)
    first_grad, obs_diag = both[0], both[1]
    me = lax.axis_index("tile")

    residual = adjoint(first_grad)
    direction = residual
    control = jnp.zeros_like(residual)
    increment = jnp.zeros(state_shape, jnp.float32)
    norm_now = None
    for step in range(ITERS):
        state = forward(direction)
        image = direction + adjoint(obs_diag * state)
        if norm_now is None:
            sums = global_sum(jnp.stack([jnp.sum(residual * residual), jnp.sum(direction * image)]))
            norm_now, curvature = sums[0], sums[1]
        else:
            curvature = global_sum(jnp.sum(direction * image))
        alpha = norm_now / curvature
        control = control + alpha * direction
        own_state = lax.dynamic_slice_in_dim(state, me * lat_rows, lat_rows, axis=2)
        increment = increment + alpha * own_state
        if step + 1 < ITERS:
            residual = residual - alpha * image
            norm_next = global_sum(jnp.sum(residual * residual))
            direction = residual + norm_next / norm_now * direction
            norm_now = norm_next
    control = to_output(control)
    increment = increment.transpose(0, 2, 1, 3).reshape(slots, lat_rows, shard_cols)
    return (control, increment)


def solution(mesh):
    return jax.shard_map(
        body,
        mesh=mesh,
        in_specs=(
            P("mem", None, "tile", None, None),
            P("tile", "mem"),
            P("tile", "mem"),
            P("tile", "mem"),
            P("tile"),
            P("tile"),
            P(),
            P(),
        ),
        out_specs=(P("mem", "tile", None, None), P(None, "tile", "mem")),
        check_vma=False,
    )
```

profile of v0, /device:TPU:0, one launch (start us, length us, event | category | flops | bytes accessed | tf_op | source)
XLA Modules:
  0.0 162.3 jit_solution(13633752903672514449)
XLA Ops:
  0.6 0.6 compare_reduce_fusion.1
  1.3 0.6 compare_reduce_fusion
  1.9 0.7 add_select_fusion.7
  3.0 2.5 %fusion.126 = f32[64,128,2]{1,0,2:T(8,128)S(1)} fusion(f32[4096,128]{0,1:T(8,128)S(1)} %fusion.125, f32[4096,2]{0,1:T(2,128)S(1)} %pad_maximum_fusion.1, s32[4096]{0:T(1024)S(1)} %get-tuple-element.447), kind=kOutput, calls=%fused_computation.157 | convolution fusion | flops 806617088 | bytes 2211840 | tf_op jit(solution)/shard_map/dot_general | solution.py:43
  5.6 0.7 fusion.146
  6.3 0.6 fusion.147
  7.2 2.4 %collective-permute-start = (f32[9,4,512]{2,1,0:T(4,128)S(1)}, f32[9,4,512]{2,1,0:T(4,128)S(1)}, u32[]{:S(2)}, u32[]{:S(2)}) collective-permute-start(f32[9,4,512]{2,1,0:T(4,128)S(1)} %pad_maximum_fusion), channel_id=1, source_target_pairs={{0,24},{8,0},{16,8},{24,16},{1,25},{9,1},{17,9},{25,17},{2,26},{10... | collective-permute-start | bytes 221192 | tf_op jit(solution)/shard_map/ppermute | solution.py:66
  9.6 0.6 collective-permute-start.1
  10.4 0.4 copy.180
  10.9 0.6 copy.237
  11.5 1.7 %copy.182 = f32[32,2,2,4,1,512]{5,3,2,1,4,0:T(4,128)} copy(f32[32,2,2,4,1,512]{5,0,3,2,1,4:T(8,128)S(1)} %bitcast.108) | data formatting | bytes 2097152 | tf_op jit(solution)/shard_map/reshape | solution.py:123
  13.2 6.1 %all-to-all-start = ((f32[32,2,2,4,1,512]{5,3,2,1,4,0:T(4,128)}), f32[32,2,2,4,1,512]{5,3,2,1,4,0:T(4,128)S(1)}, u32[]{:S(2)}, u32[]{:S(2)}) async-start(f32[32,2,2,4,1,512]{5,3,2,1,4,0:T(4,128)} %copy.182), calls=%async_computation | async-start | bytes 2097152 | tf_op jit(solution)/shard_map/all_to_all | solution.py:126
  20.2 26.5 %all-to-all-done = f32[32,2,2,4,1,512]{5,3,2,1,4,0:T(4,128)S(1)} async-done(((f32[32,2,2,4,1,512]{5,3,2,1,4,0:T(4,128)}), f32[32,2,2,4,1,512]{5,3,2,1,4,0:T(4,128)S(1)}, u32[]{:S(2)}, u32[]{:S(2)}) %all-to-all-start) | async-done | bytes 1048608 | tf_op jit(solution)/shard_map/all_to_all | solution.py:126
  46.7 0.7 fusion.129
  47.5 6.9 %while.57 = (s32[]{:T(128)}, f32[2,16,8,512]{3,2,1,0:T(8,128)S(1)}, f32[2]{0:T(128)S(1)}, f32[2]{0:T(128)S(1)}, s32[16]{0:T(128)S(1)}, /*index=5*/s32[16]{0:T(128)S(1)}, s32[]{:T(128)}) while((s32[]{:T(128)}, f32[2,16,8,512]{3,2,1,0:T(8,128)S(1)}, f32[2]{0:T(128)S(1)}, f32[2]{0:T(128)S(1)}, s32[16]{0:T(128)S(1)}, ...), condition=%wide.region_4.5_spmd.clone, body=%wide.region_3.4_spmd.clone.sunk | while | flops 6406146 | bytes 28737804 | solution.py:143
  48.0 0.4 fusion.302
  48.8 0.4 fusion.306
  49.7 0.4 fusion.310
  50.5 0.4 fusion.314
  51.4 0.4 fusion.302
  52.3 0.4 fusion.306
  53.1 0.4 fusion.310
  54.4 6.8 %while.58 = (s32[]{:T(128)}, f32[2,16,8,512]{3,2,1,0:T(8,128)S(1)}, f32[2]{0:T(128)S(1)}, f32[2]{0:T(128)S(1)}, s32[16]{0:T(128)S(1)}, /*index=5*/s32[16]{0:T(128)S(1)}, s32[]{:T(128)}) while((s32[]{:T(128)}, f32[2,16,8,512]{3,2,1,0:T(8,128)S(1)}, f32[2]{0:T(128)S(1)}, f32[2]{0:T(128)S(1)}, s32[16]{0:T(128)S(1)}, ...), condition=%wide.region_7.8_spmd.clone, body=%wide.region_6.7_spmd.clone.sunk | while | flops 6406146 | bytes 28737804 | solution.py:143
  54.9 0.4 fusion.319
  58.4 0.4 fusion.319
  61.3 0.9 fusion.130
  62.4 0.8 collective-permute-start.4
  63.2 1.2 collective-permute-start.5
  64.4 3.1 %collective-permute-done.3 = f32[2,2,16,512]{3,2,1,0:T(8,128)S(1)} collective-permute-done((f32[2,2,16,512]{3,2,1,0:T(8,128)S(1)}, f32[2,2,16,512]{3,2,1,0:T(8,128)S(1)}, u32[]{:S(2)}, u32[]{:S(2)}) %collective-permute-start.3) | collective-permute-done | bytes 131104 | tf_op jit(solution)/shard_map/ppermute | solution.py:90
  67.5 1.2 collective-permute-done.4
  69.2 0.7 fusion.131
  70.0 6.8 %while.59 = (s32[]{:T(128)}, f32[2,16,8,512]{3,2,1,0:T(8,128)S(1)}, f32[2]{0:T(128)S(1)}, f32[2]{0:T(128)S(1)}, s32[16]{0:T(128)S(1)}, /*index=5*/s32[16]{0:T(128)S(1)}, s32[]{:T(128)}) while((s32[]{:T(128)}, f32[2,16,8,512]{3,2,1,0:T(8,128)S(1)}, f32[2]{0:T(128)S(1)}, f32[2]{0:T(128)S(1)}, s32[16]{0:T(128)S(1)}, ...), condition=%wide.region_11.12_spmd.clone, body=%wide.region_10.11_spmd.clone.sunk | while | flops 6406146 | bytes 28737804 | solution.py:143
  70.5 0.4 fusion.336
  73.9 0.4 fusion.336
  76.8 0.8 multiply_reduce_fusion.2
  77.6 1.4 pad_maximum_fusion.2
  79.0 10.6 %all_to_all.28 = f32[32,1,2]{2,1,0:T(1,128)S(1)} all-to-all(f32[32,1,2]{2,1,0:T(1,128)S(1)} %broadcast_in_dim.30), channel_id=1, replica_groups=mesh['tile'=4,'mem'=8] {'tile','mem'}, dimensions={0} | all-to-all | bytes 512 | tf_op jit(solution)/shard_map/all_to_all | solution.py:34
  89.6 0.6 fusion.210
  91.5 0.8 multiply_reduce_fusion
  92.3 1.2 broadcast_in_dim.31
  93.6 2.5 %all-to-all-start.2 = ((f32[32,1,1]{2,1,0:T(1,128)}), f32[32,1,1]{2,1,0:T(1,128)S(1)}, u32[]{:S(2)}, u32[]{:S(2)}) async-start(f32[32,1,1]{2,1,0:T(1,128)} %broadcast_in_dim.31), calls=%async_computation.2 | async-start | bytes 32768 | tf_op jit(solution)/shard_map/all_to_all | solution.py:34
  96.1 7.0 %all-to-all-done.2 = f32[32,1,1]{2,1,0:T(1,128)S(1)} async-done(((f32[32,1,1]{2,1,0:T(1,128)}), f32[32,1,1]{2,1,0:T(1,128)S(1)}, u32[]{:S(2)}, u32[]{:S(2)}) %all-to-all-start.2) | async-done | bytes 160 | tf_op jit(solution)/shard_map/all_to_all | solution.py:34
  103.2 0.6 reduce_sum.128
  105.3 6.8 %while.60 = (s32[]{:T(128)}, f32[2,16,8,512]{3,2,1,0:T(8,128)S(1)}, f32[2]{0:T(128)S(1)}, f32[2]{0:T(128)S(1)}, s32[16]{0:T(128)S(1)}, /*index=5*/s32[16]{0:T(128)S(1)}, s32[]{:T(128)}) while((s32[]{:T(128)}, f32[2,16,8,512]{3,2,1,0:T(8,128)S(1)}, f32[2]{0:T(128)S(1)}, f32[2]{0:T(128)S(1)}, s32[16]{0:T(128)S(1)}, ...), condition=%wide.region_17.18_spmd.clone, body=%wide.region_16.17_spmd.clone.sunk | while | flops 6406146 | bytes 28737804 | solution.py:143
  105.8 0.4 fusion.353
  109.2 0.4 fusion.353
  112.1 0.9 fusion.132
  113.2 0.7 collective-permute-start.7
  113.9 1.4 collective-permute-start.8
  115.3 3.1 %collective-permute-done.6 = f32[2,2,16,512]{3,2,1,0:T(8,128)S(1)} collective-permute-done((f32[2,2,16,512]{3,2,1,0:T(8,128)S(1)}, f32[2,2,16,512]{3,2,1,0:T(8,128)S(1)}, u32[]{:S(2)}, u32[]{:S(2)}) %collective-permute-start.6) | collective-permute-done | bytes 131104 | tf_op jit(solution)/shard_map/ppermute | solution.py:90
  118.4 1.2 collective-permute-done.7
  120.1 0.7 fusion.133
  120.9 6.8 %while.61 = (s32[]{:T(128)}, f32[2,16,8,512]{3,2,1,0:T(8,128)S(1)}, f32[2]{0:T(128)S(1)}, f32[2]{0:T(128)S(1)}, s32[16]{0:T(128)S(1)}, /*index=5*/s32[16]{0:T(128)S(1)}, s32[]{:T(128)}) while((s32[]{:T(128)}, f32[2,16,8,512]{3,2,1,0:T(8,128)S(1)}, f32[2]{0:T(128)S(1)}, f32[2]{0:T(128)S(1)}, s32[16]{0:T(128)S(1)}, ...), condition=%wide.region_21.22_spmd.clone, body=%wide.region_20.21_spmd.clone.sunk | while | flops 6406146 | bytes 28737804 | solution.py:143
  121.4 0.4 fusion.370
  124.8 0.4 fusion.370
  127.7 0.8 fusion.136
  128.5 0.7 broadcast_in_dim.32
  129.2 9.2 %all_to_all.29 = f32[32,1,1]{2,1,0:T(1,128)S(1)} all-to-all(f32[32,1,1]{2,1,0:T(1,128)S(1)} %broadcast_in_dim.32), channel_id=1, replica_groups=mesh['tile'=4,'mem'=8] {'tile','mem'}, dimensions={0} | all-to-all | bytes 256 | tf_op jit(solution)/shard_map/all_to_all | solution.py:34
  138.4 0.6 reduce_sum.134
  140.6 1.1 copy.208
  141.7 2.6 %all-to-all-start.4 = ((f32[32,2,4,1,512]{4,2,1,3,0:T(4,128)}), f32[32,2,4,1,512]{4,2,1,3,0:T(4,128)S(1)}, u32[]{:S(2)}, u32[]{:S(2)}) async-start(f32[32,2,4,1,512]{4,2,1,3,0:T(4,128)} %copy.208), calls=%async_computation.4 | async-start | bytes 1048576 | tf_op jit(solution)/shard_map/all_to_all | solution.py:160
  144.3 0.6 multiply_add_fusion.2
  144.9 15.7 %all-to-all-done.4 = f32[32,2,4,1,512]{4,2,1,3,0:T(4,128)S(1)} async-done(((f32[32,2,4,1,512]{4,2,1,3,0:T(4,128)}), f32[32,2,4,1,512]{4,2,1,3,0:T(4,128)S(1)}, u32[]{:S(2)}, u32[]{:S(2)}) %all-to-all-start.4) | async-done | bytes 524320 | tf_op jit(solution)/shard_map/all_to_all | solution.py:160
  161.3 1.0 copy.211
  (232 shorter events, 31.6 us)
Async XLA Ops:
  0.6 2.3 %copy-start.2 = (f32[1,4096]{1,0:T(1,128)S(1)}, f32[1,4096]{1,0:T(1,128)}, u32[]{:S(2)}) copy-start(f32[1,4096]{1,0:T(1,128)} %param.23) | copy-start | bytes 49156
  0.6 2.3 %copy-start.1 = (f32[1,4096]{1,0:T(1,128)S(1)}, f32[1,4096]{1,0:T(1,128)}, u32[]{:S(2)}) copy-start(f32[1,4096]{1,0:T(1,128)} %param.24) | copy-start | bytes 49156
  2.7 2.9 %copy-start.3 = (s32[4]{0:T(128)S(1)}, s32[4]{0:T(128)}, u32[]{:S(2)}) copy-start(s32[4]{0:T(128)} %param.26) | copy-start | bytes 52
  2.7 3.6 %copy-start.4 = (s32[4]{0:T(128)S(1)}, s32[4]{0:T(128)}, u32[]{:S(2)}) copy-start(s32[4]{0:T(128)} %param.27) | copy-start | bytes 52
  2.7 7.8 %copy-start = (bf16[4,2,4,16,512]{4,3,2,1,0:T(8,128)(2,1)S(1)}, bf16[4,2,4,16,512]{4,3,2,1,0:T(8,128)(2,1)}, u32[]{:S(2)}) copy-start(bf16[4,2,4,16,512]{4,3,2,1,0:T(8,128)(2,1)} %param.22) | copy-start | bytes 1572868
  7.2 12.3 %collective-permute-start = (f32[9,4,512]{2,1,0:T(4,128)S(1)}, f32[9,4,512]{2,1,0:T(4,128)S(1)}, u32[]{:S(2)}, u32[]{:S(2)}) collective-permute-start(f32[9,4,512]{2,1,0:T(4,128)S(1)} %pad_maximum_fusion), channel_id=1, source_target_pairs={{0,24},{8,0},{16,8},{24,16},{1,25},{9,1},{17,9},{25,17},{2,26},{10... | collective-permute-start | bytes 221192 | tf_op jit(solution)/shard_map/ppermute | solution.py:66
  9.6 9.9 %collective-permute-start.1 = (f32[9,4,512]{2,1,0:T(4,128)S(1)}, f32[9,4,512]{2,1,0:T(4,128)S(1)}, u32[]{:S(2)}, u32[]{:S(2)}) collective-permute-start(f32[9,4,512]{2,1,0:T(4,128)S(1)} %pad_maximum_fusion), channel_id=1, source_target_pairs={{0,16},{8,24},{16,0},{24,8},{1,17},{9,25},{17,1},{25,9},{2,18},{10... | collective-permute-start | bytes 221192 | tf_op jit(solution)/shard_map/ppermute | solution.py:66
  10.3 9.3 %collective-permute-start.2 = (f32[9,4,512]{2,1,0:T(4,128)S(1)}, f32[9,4,512]{2,1,0:T(4,128)S(1)}, u32[]{:S(2)}, u32[]{:S(2)}) collective-permute-start(f32[9,4,512]{2,1,0:T(4,128)S(1)} %pad_maximum_fusion), channel_id=1, source_target_pairs={{0,8},{8,16},{16,24},{24,0},{1,9},{9,17},{17,25},{25,1},{2,10},{10... | collective-permute-start | bytes 221192 | tf_op jit(solution)/shard_map/ppermute | solution.py:66
  11.5 7.8 %copy-start.5 = (f32[16]{0:T(128)S(1)}, f32[16]{0:T(128)}, u32[]{:S(2)}) copy-start(f32[16]{0:T(128)} %param.28) | copy-start | bytes 196
  11.5 7.9 %copy-start.6 = (f32[16]{0:T(128)S(1)}, f32[16]{0:T(128)}, u32[]{:S(2)}) copy-start(f32[16]{0:T(128)} %param.29) | copy-start | bytes 196
  13.2 33.5 %all-to-all-start = ((f32[32,2,2,4,1,512]{5,3,2,1,4,0:T(4,128)}), f32[32,2,2,4,1,512]{5,3,2,1,4,0:T(4,128)S(1)}, u32[]{:S(2)}, u32[]{:S(2)}) async-start(f32[32,2,2,4,1,512]{5,3,2,1,4,0:T(4,128)} %copy.182), calls=%async_computation | async-start | bytes 2097152 | tf_op jit(solution)/shard_map/all_to_all | solution.py:126
  62.3 5.2 %collective-permute-start.3 = (f32[2,2,16,512]{3,2,1,0:T(8,128)S(1)}, f32[2,2,16,512]{3,2,1,0:T(8,128)S(1)}, u32[]{:S(2)}, u32[]{:S(2)}) collective-permute-start(f32[2,2,16,512]{3,2,1,0:T(8,128)S(1)} %copy.191), channel_id=1, source_target_pairs={{0,8},{8,16},{16,24},{24,0},{1,9},{9,17},{17,25},{25,1},{2,10},{10... | collective-permute-start | bytes 393224 | tf_op jit(solution)/shard_map/ppermute | solution.py:90
  62.4 6.4 %collective-permute-start.4 = (f32[2,2,16,512]{3,2,1,0:T(8,128)S(1)}, f32[2,2,16,512]{3,2,1,0:T(8,128)S(1)}, u32[]{:S(2)}, u32[]{:S(2)}) collective-permute-start(f32[2,2,16,512]{3,2,1,0:T(8,128)S(1)} %copy.191), channel_id=1, source_target_pairs={{0,16},{8,24},{16,0},{24,8},{1,17},{9,25},{17,1},{25,9},{2,18},{10... | collective-permute-start | bytes 393224 | tf_op jit(solution)/shard_map/ppermute | solution.py:90
  63.2 5.8 %collective-permute-start.5 = (f32[2,2,16,512]{3,2,1,0:T(8,128)S(1)}, f32[2,2,16,512]{3,2,1,0:T(8,128)S(1)}, u32[]{:S(2)}, u32[]{:S(2)}) collective-permute-start(f32[2,2,16,512]{3,2,1,0:T(8,128)S(1)} %copy.191), channel_id=1, source_target_pairs={{0,24},{8,0},{16,8},{24,16},{1,25},{9,1},{17,9},{25,17},{2,26},{10... | collective-permute-start | bytes 393224 | tf_op jit(solution)/shard_map/ppermute | solution.py:90
  93.6 9.6 %all-to-all-start.2 = ((f32[32,1,1]{2,1,0:T(1,128)}), f32[32,1,1]{2,1,0:T(1,128)S(1)}, u32[]{:S(2)}, u32[]{:S(2)}) async-start(f32[32,1,1]{2,1,0:T(1,128)} %broadcast_in_dim.31), calls=%async_computation.2 | async-start | bytes 32768 | tf_op jit(solution)/shard_map/all_to_all | solution.py:34
  113.2 5.2 %collective-permute-start.6 = (f32[2,2,16,512]{3,2,1,0:T(8,128)S(1)}, f32[2,2,16,512]{3,2,1,0:T(8,128)S(1)}, u32[]{:S(2)}, u32[]{:S(2)}) collective-permute-start(f32[2,2,16,512]{3,2,1,0:T(8,128)S(1)} %copy.201), channel_id=1, source_target_pairs={{0,8},{8,16},{16,24},{24,0},{1,9},{9,17},{17,25},{25,1},{2,10},{10... | collective-permute-start | bytes 393224 | tf_op jit(solution)/shard_map/ppermute | solution.py:90
  113.2 6.4 %collective-permute-start.7 = (f32[2,2,16,512]{3,2,1,0:T(8,128)S(1)}, f32[2,2,16,512]{3,2,1,0:T(8,128)S(1)}, u32[]{:S(2)}, u32[]{:S(2)}) collective-permute-start(f32[2,2,16,512]{3,2,1,0:T(8,128)S(1)} %copy.201), channel_id=1, source_target_pairs={{0,16},{8,24},{16,0},{24,8},{1,17},{9,25},{17,1},{25,9},{2,18},{10... | collective-permute-start | bytes 393224 | tf_op jit(solution)/shard_map/ppermute | solution.py:90
  113.9 6.0 %collective-permute-start.8 = (f32[2,2,16,512]{3,2,1,0:T(8,128)S(1)}, f32[2,2,16,512]{3,2,1,0:T(8,128)S(1)}, u32[]{:S(2)}, u32[]{:S(2)}) collective-permute-start(f32[2,2,16,512]{3,2,1,0:T(8,128)S(1)} %copy.201), channel_id=1, source_target_pairs={{0,24},{8,0},{16,8},{24,16},{1,25},{9,1},{17,9},{25,17},{2,26},{10... | collective-permute-start | bytes 393224 | tf_op jit(solution)/shard_map/ppermute | solution.py:90
  141.7 19.0 %all-to-all-start.4 = ((f32[32,2,4,1,512]{4,2,1,3,0:T(4,128)}), f32[32,2,4,1,512]{4,2,1,3,0:T(4,128)S(1)}, u32[]{:S(2)}, u32[]{:S(2)}) async-start(f32[32,2,4,1,512]{4,2,1,3,0:T(4,128)} %copy.208), calls=%async_computation.4 | async-start | bytes 1048576 | tf_op jit(solution)/shard_map/all_to_all | solution.py:160
where the time goes:
time: 163 us; the launch traced here: 162 us
  waiting for transfers between devices  58.5 us (36%)
  other arithmetic  30.2 us (19%)
  local copies, waits for them, and re-layouts  26.3 us (16%)
  blocking collectives  19.8 us (12%)
  starting transfers between devices  18.7 us (11%)
  between operations  5.22 us (3%)
  matrix products  2.47 us (2%)
    all_to_all x1, waiting for transfers between devices, body(): got = lax.all_to_all(sent, ('tile', 'mem'), 0, 0, tiled=True)  26.5 us
    all_to_all x2, blocking collectives, global_sum(): return jnp.sum(lax.all_to_all(spread, axes, 0, 0, tiled=True), axis=0)  19.8 us
    all_to_all x1, waiting for transfers between devices, to_output(): got = lax.all_to_all(sent, ('tile', 'mem'), 0, 0, tiled=True)  15.7 us
    mul x40, other arithmetic, diffuse_step(): mask * (field + lat_rate[:, None, None, None] * lat_term + lon_rate[:, No...  15.5 us
    slice x80, local copies, waits for them, and re-layouts, diffuse_step(): west = jnp.roll(field, 1, axis=3)  12.2 us
    ppermute x6, waiting for transfers between devices, sum_over_tile_by_permutes(): lax.ppermute(block, 'tile', [(i, (i + k) % count) for i in range(count)])  9.25 us
    all_to_all x1, waiting for transfers between devices, global_sum(): return jnp.sum(lax.all_to_all(spread, axes, 0, 0, tiled=True), axis=0)  7.04 us
    all_to_all x1, starting transfers between devices, body(): got = lax.all_to_all(sent, ('tile', 'mem'), 0, 0, tiled=True)  6.12 us
  transfers between devices with their start and end apart: 12, of which 9 were waited for; matrix products, arithmetic and copies ran while one was open for 3% of the time, Pallas kernels for 0%

commit v1 on v0

--- a/solution.py
+++ b/solution.py
@@ -1,6 +1,8 @@
 import jax
 import jax.numpy as jnp
 from jax import lax
+from jax.experimental import pallas as pl
+from jax.experimental.pallas import tpu as pltpu
 from jax.sharding import PartitionSpec as P
 
 ITERS = 2
@@ -24,6 +26,42 @@
     return mask * (
         field + lat_rate[:, None, None, None] * lat_term + lon_rate[:, None, None, None] * lon_term
     )
+
+
+def smooth_kernel(rates_ref, mask_ref, field_ref, out_ref):
+    levels, rows, members, nlon = field_ref.shape
+    mask = mask_ref[...]
+    zero = jnp.zeros((1, members, nlon), jnp.float32)
+    for level in range(levels):
+        lat = rates_ref[0, level]
+        lon = rates_ref[1, level]
+        now = mask * field_ref[level]
+        for inner in range(STEPS):
+            north = jnp.concatenate([now[1:], zero], axis=0)
+            south = jnp.concatenate([zero, now[:-1]], axis=0)
+            east = pltpu.roll(now, nlon - 1, 2)
+            west = pltpu.roll(now, 1, 2)
+            lat_term = north + south - 2.0 * now
+            lon_term = east + west - 2.0 * now
+            now = mask * (now + lat * lat_term + lon * lon_term)
+        out_ref[level] = now
+
+
+def smooth_in_vmem(field, mask, lat_rate, lon_rate):
+    size = field.size
+    return pl.pallas_call(
+        smooth_kernel,
+        out_shape=jax.ShapeDtypeStruct(field.shape, jnp.float32),
+        in_specs=[
+            pl.BlockSpec(memory_space=pltpu.SMEM),
+            pl.BlockSpec(memory_space=pltpu.VMEM),
+            pl.BlockSpec(memory_space=pltpu.VMEM),
+        ],
+        out_specs=pl.BlockSpec(memory_space=pltpu.VMEM),
+        cost_estimate=pl.CostEstimate(
+            flops=14 * STEPS * size, bytes_accessed=8 * size, transcendentals=0
+        ),
+    )(jnp.stack([lat_rate, lon_rate]), mask, field)
 
 
 def global_sum(value):
@@ -139,10 +177,7 @@
         pert = lax.all_to_all(pert, "tile", split_axis=3, concat_axis=2, tiled=True)
 
     def smooth(field):
-        current = mask * field
-        return lax.fori_loop(
-            0, STEPS, lambda inner, now: diffuse_step(now, mask, lat_own, lon_own), current, unroll=4
-        )
+        return smooth_in_vmem(field, mask, lat_own, lon_own)
 
     def forward(control):
         smoothed = smooth(control)

time: 163 us -> 160 us (0.982)
  Pallas kernels: 0 us -> 25.8 us
  local copies, waits for them, and re-layouts: 26.3 us -> 11.3 us
  other arithmetic: 30.2 us -> 19.8 us
  blocking collectives: 19.8 us -> 28.6 us
  waiting for transfers between devices: 58.5 us -> 50.2 us
  starting transfers between devices: 18.7 us -> 16.1 us
    pallas_call x0 -> x5, Pallas kernels: none -> 25.8 us  [smooth_in_vmem(): pl.pallas_call(smooth_kernel, out_shape=jax.ShapeDtypeStruct(field.shape,...]
    slice x120 -> x1, local copies, waits for them, and re-layouts: 16.8 us -> 0.01 us  [body(): mask = row_mask(tables[:, 0], tables[:, 1], nlon)]
    mul x45 -> x0, other arithmetic: 15.9 us -> none  [the longest x40 15.5 us: diffuse_step(): mask * (field + lat_rate[:, None, None, None] * lat_term + lon_rate[:, No...]
    all_to_all x2 -> x3, blocking collectives: 19.8 us -> 28.6 us  [global_sum(): return jnp.sum(lax.all_to_all(spread, axes, 0, 0, tiled=True), axis=0)]
    all_to_all x1 -> x0, waiting for transfers between devices: 7.04 us -> none  [global_sum(): return jnp.sum(lax.all_to_all(spread, axes, 0, 0, tiled=True), axis=0)]
    all_to_all x1 -> x0, starting transfers between devices: 2.54 us -> none  [global_sum(): return jnp.sum(lax.all_to_all(spread, axes, 0, 0, tiled=True), axis=0)]
    reduce_sum x3, local copies, waits for them, and re-layouts: 0.11 us -> 2.51 us  [adjoint(): return smooth(jnp.sum(pert * gradient[:, :, :, None], axis=0))]
    reduce_sum x2, other arithmetic: 1.81 us -> 3.8 us  [forward(): return sum_over_tile_by_permutes(jnp.sum(pert * smoothed[None], axis=3))]
  transfers between devices with their start and end apart: 12 -> 11, of which waited for: 9 -> 8; matrix products, arithmetic and copies ran while one was open for 3% -> 3% of each run, Pallas kernels for 0% -> 0%
where the time goes in v1:
time: 160 us; the launch traced here: 159 us
  waiting for transfers between devices  50.2 us (31%)
  blocking collectives  28.6 us (18%)
  Pallas kernels  25.8 us (16%)
  other arithmetic  19.8 us (12%)
  starting transfers between devices  16.1 us (10%)
  local copies, waits for them, and re-layouts  11.3 us (7%)
  between operations  5.07 us (3%)
  matrix products  2.48 us (2%)
    all_to_all x3, blocking collectives, global_sum(): return jnp.sum(lax.all_to_all(spread, axes, 0, 0, tiled=True), axis=0)  28.6 us
    pallas_call x5, Pallas kernels, smooth_in_vmem(): pl.pallas_call(smooth_kernel, out_shape=jax.ShapeDtypeStruct(field.shape,...  25.8 us
    all_to_all x1, waiting for transfers between devices, body(): got = lax.all_to_all(sent, ('tile', 'mem'), 0, 0, tiled=True)  25.3 us
    all_to_all x1, waiting for transfers between devices, to_output(): got = lax.all_to_all(sent, ('tile', 'mem'), 0, 0, tiled=True)  15.7 us
    ppermute x6, waiting for transfers between devices, sum_over_tile_by_permutes(): lax.ppermute(block, 'tile', [(i, (i + k) % count) for i in range(count)])  9.25 us
    all_to_all x1, starting transfers between devices, body(): got = lax.all_to_all(sent, ('tile', 'mem'), 0, 0, tiled=True)  6.12 us
    ppermute x6, starting transfers between devices, sum_over_tile_by_permutes(): lax.ppermute(block, 'tile', [(i, (i + k) % count) for i in range(count)])  4.16 us
    reduce_sum x2, other arithmetic, forward(): return sum_over_tile_by_permutes(jnp.sum(pert * smoothed[None], axis=3))  3.8 us
  transfers between devices with their start and end apart: 11, of which 8 were waited for; matrix products, arithmetic and copies ran while one was open for 3% of the time, Pallas kernels for 0%

profile of v1, /device:TPU:0, one launch (start us, length us, event | category | flops | bytes accessed | tf_op | source)
XLA Modules:
  0.0 159.4 jit_solution(6561095827602991924)
XLA Ops:
  0.6 0.6 compare_reduce_fusion.1
  1.3 0.6 compare_reduce_fusion
  1.9 0.7 add_select_fusion.1
  2.7 0.2 fusion.5
  3.0 2.5 %fusion.6 = f32[64,128,2]{1,0,2:T(8,128)S(1)} fusion(f32[4096,128]{0,1:T(8,128)S(1)} %fusion.5, f32[4096,2]{0,1:T(2,128)S(1)} %pad_maximum_fusion.1, s32[4096]{0:T(1024)S(1)} %get-tuple-element.47), kind=kOutput, calls=%fused_computation.7 | convolution fusion | flops 806617088 | bytes 2211840 | tf_op jit(solution)/shard_map/dot_general | solution.py:81
  5.6 0.7 fusion.21
  6.3 0.6 fusion.22
  7.2 2.4 %collective-permute-start = (f32[9,4,512]{2,1,0:T(4,128)S(1)}, f32[9,4,512]{2,1,0:T(4,128)S(1)}, u32[]{:S(2)}, u32[]{:S(2)}) collective-permute-start(f32[9,4,512]{2,1,0:T(4,128)S(1)} %pad_maximum_fusion), channel_id=1, source_target_pairs={{0,24},{8,0},{16,8},{24,16},{1,25},{9,1},{17,9},{25,17},{2,26},{10... | collective-permute-start | bytes 221192 | tf_op jit(solution)/shard_map/ppermute | solution.py:104
  9.6 0.6 collective-permute-start.1
  10.3 0.2 collective-permute-start.2
  10.4 0.4 copy.184
  10.9 0.6 copy.241
  11.5 1.7 %copy.186 = f32[32,2,2,4,1,512]{5,3,2,1,4,0:T(4,128)} copy(f32[32,2,2,4,1,512]{5,0,3,2,1,4:T(8,128)S(1)} %bitcast.110) | data formatting | bytes 2097152 | tf_op jit(solution)/shard_map/reshape | solution.py:161
  13.2 6.1 %all-to-all-start = ((f32[32,2,2,4,1,512]{5,3,2,1,4,0:T(4,128)}), f32[32,2,2,4,1,512]{5,3,2,1,4,0:T(4,128)S(1)}, u32[]{:S(2)}, u32[]{:S(2)}) async-start(f32[32,2,2,4,1,512]{5,3,2,1,4,0:T(4,128)} %copy.186), calls=%async_computation | async-start | bytes 2097152 | tf_op jit(solution)/shard_map/all_to_all | solution.py:164
  19.5 0.6 pad_maximum_fusion.2.rates_ref
  20.4 0.1 reshape.314
  20.6 0.8 compare_select_fusion.2.mask_ref
  21.4 25.3 %all-to-all-done = f32[32,2,2,4,1,512]{5,3,2,1,4,0:T(4,128)S(1)} async-done(((f32[32,2,2,4,1,512]{5,3,2,1,4,0:T(4,128)}), f32[32,2,2,4,1,512]{5,3,2,1,4,0:T(4,128)S(1)}, u32[]{:S(2)}, u32[]{:S(2)}) %all-to-all-start) | async-done | bytes 1048608 | tf_op jit(solution)/shard_map/all_to_all | solution.py:164
  46.7 0.7 fusion.9
  47.4 0.8 copy.190
  48.2 5.2 %shard_map.95.field_ref = f32[2,16,8,512]{3,2,1,0:T(8,128)} custom-call(f32[2,2]{1,0:T(2,128)} %pad_maximum_fusion.2.rates_ref, f32[16,1,512]{2,1,0:T(1,128)} %compare_select_fusion.2.mask_ref, f32[2,16,8,512]{3,2,1,0:T(8,128)} %bitcast.113), custom_call_target="tpu_custom_call" | custom-call | flops 14680064 | bytes 1048576 | tf_op jit(solution)/shard_map/pallas_call | solution.py:52
  53.4 5.2 %shard_map.96 = f32[2,16,8,512]{3,2,1,0:T(8,128)} custom-call(f32[2,2]{1,0:T(2,128)} %pad_maximum_fusion.2.rates_ref, f32[16,1,512]{2,1,0:T(1,128)} %compare_select_fusion.2.mask_ref, f32[2,16,8,512]{3,2,1,0:T(8,128)} %shard_map.95.field_ref), custom_call_target="tpu_custom_call" | custom-call | flops 14680064 | bytes 1048576 | tf_op jit(solution)/shard_map/pallas_call | solution.py:52
  58.5 1.9 %fusion.10 = f32[2,2,4,4,512]{4,2,3,1,0:T(4,128)S(1)} fusion(f32[4,8,2,2,4,1,512]{6,4,3,2,1,0,5:T(4,128)S(1)} %bitcast.106, f32[2,4,4,8,512]{4,3,2,1,0:T(8,128)} %bitcast.115), kind=kLoop, calls=%fused_computation.14 | loop fusion | flops 491520 | bytes 1703936 | tf_op jit(solution)/shard_map/reduce_sum | solution.py:184
  60.4 0.1 copy.193
  60.6 0.8 collective-permute-start.4
  61.5 1.2 collective-permute-start.5
  62.7 3.1 %collective-permute-done.3 = f32[2,2,16,512]{3,2,1,0:T(8,128)S(1)} collective-permute-done((f32[2,2,16,512]{3,2,1,0:T(8,128)S(1)}, f32[2,2,16,512]{3,2,1,0:T(8,128)S(1)}, u32[]{:S(2)}, u32[]{:S(2)}) %collective-permute-start.3) | collective-permute-done | bytes 131104 | tf_op jit(solution)/shard_map/ppermute | solution.py:128
  65.8 1.2 collective-permute-done.4
  67.0 0.3 collective-permute-done.5
  67.5 0.7 fusion.11
  68.1 0.8 copy.199
  69.0 5.2 %shard_map.97 = f32[2,16,8,512]{3,2,1,0:T(8,128)} custom-call(f32[2,2]{1,0:T(2,128)} %pad_maximum_fusion.2.rates_ref, f32[16,1,512]{2,1,0:T(1,128)} %compare_select_fusion.2.mask_ref, f32[2,16,8,512]{3,2,1,0:T(8,128)} %bitcast.114), custom_call_target="tpu_custom_call" | custom-call | flops 14680064 | bytes 1048576 | tf_op jit(solution)/shard_map/pallas_call | solution.py:52
  74.1 1.9 %multiply_reduce_fusion.2 = (f32[]{:T(128)}, f32[]{:T(128)}, f32[2,16,8,512]{3,2,1,0:T(8,128)S(1)}) fusion(f32[2,16,8,512]{3,2,1,0:T(8,128)S(1)} %copy-done, f32[2,16,8,512]{3,2,1,0:T(8,128)} %shard_map.97), kind=kLoop, calls=%fused_computation.30 | loop fusion | flops 655358 | bytes 1572872 | tf_op jit(solution)/shard_map/reduce_sum | solution.py:236
  76.0 1.4 pad_maximum_fusion.3
  77.4 10.6 %all_to_all.28 = f32[32,1,2]{2,1,0:T(1,128)S(1)} all-to-all(f32[32,1,2]{2,1,0:T(1,128)S(1)} %broadcast_in_dim.36), channel_id=1, replica_groups=mesh['tile'=4,'mem'=8] {'tile','mem'}, dimensions={0} | all-to-all | bytes 512 | tf_op jit(solution)/shard_map/all_to_all | solution.py:72
  88.1 0.6 fusion.25
  90.0 0.8 multiply_reduce_fusion
  90.8 0.7 broadcast_in_dim.37
  91.5 8.8 %all_to_all.29 = f32[32,1,1]{2,1,0:T(1,128)S(1)} all-to-all(f32[32,1,1]{2,1,0:T(1,128)S(1)} %broadcast_in_dim.37), channel_id=1, replica_groups=mesh['tile'=4,'mem'=8] {'tile','mem'}, dimensions={0} | all-to-all | bytes 256 | tf_op jit(solution)/shard_map/all_to_all | solution.py:72
  100.3 0.6 reduce_sum.128
  102.2 0.9 multiply_add_fusion.1.field_ref
  103.1 5.2 %shard_map.98 = f32[2,16,8,512]{3,2,1,0:T(8,128)} custom-call(f32[2,2]{1,0:T(2,128)} %pad_maximum_fusion.2.rates_ref, f32[16,1,512]{2,1,0:T(1,128)} %compare_select_fusion.2.mask_ref, f32[2,16,8,512]{3,2,1,0:T(8,128)} %multiply_add_fusion.1.field_ref), custom_call_target="tpu_custom_call" | custom-call | flops 14680064 | bytes 1048576 | tf_op jit(solution)/shard_map/pallas_call | solution.py:52
  108.3 1.9 %fusion.12 = f32[2,2,4,4,512]{4,2,3,1,0:T(4,128)S(1)} fusion(f32[4,8,2,2,4,1,512]{6,4,3,2,1,0,5:T(4,128)S(1)} %bitcast.108, f32[2,4,4,8,512]{4,3,2,1,0:T(8,128)} %bitcast.116), kind=kLoop, calls=%fused_computation.16 | loop fusion | flops 491520 | bytes 1703936 | tf_op jit(solution)/shard_map/reduce_sum | solution.py:184
  110.2 0.1 copy.203
  110.4 0.7 collective-permute-start.7
  111.0 1.4 collective-permute-start.8
  112.4 3.1 %collective-permute-done.6 = f32[2,2,16,512]{3,2,1,0:T(8,128)S(1)} collective-permute-done((f32[2,2,16,512]{3,2,1,0:T(8,128)S(1)}, f32[2,2,16,512]{3,2,1,0:T(8,128)S(1)}, u32[]{:S(2)}, u32[]{:S(2)}) %collective-permute-start.6) | collective-permute-done | bytes 131104 | tf_op jit(solution)/shard_map/ppermute | solution.py:128
  115.5 1.2 collective-permute-done.7
  116.8 0.3 collective-permute-done.8
  117.3 0.7 fusion.13
  117.9 0.8 copy.209
  118.8 5.2 %shard_map.99 = f32[2,16,8,512]{3,2,1,0:T(8,128)} custom-call(f32[2,2]{1,0:T(2,128)} %pad_maximum_fusion.2.rates_ref, f32[16,1,512]{2,1,0:T(1,128)} %compare_select_fusion.2.mask_ref, f32[2,16,8,512]{3,2,1,0:T(8,128)} %bitcast.112), custom_call_target="tpu_custom_call" | custom-call | flops 14680064 | bytes 1048576 | tf_op jit(solution)/shard_map/pallas_call | solution.py:52
  123.9 1.8 %fusion.16 = f32[]{:T(128)} fusion(f32[2,16,8,512]{3,2,1,0:T(8,128)S(1)} %copy-done.1, f32[2,16,8,512]{3,2,1,0:T(8,128)} %shard_map.99), kind=kLoop, calls=%fused_computation.22 | loop fusion | flops 393215 | bytes 1048580 | tf_op jit(solution)/shard_map/reduce_sum | solution.py:239
  125.7 0.7 broadcast_in_dim.38
  126.4 9.2 %all_to_all.30 = f32[32,1,1]{2,1,0:T(1,128)S(1)} all-to-all(f32[32,1,1]{2,1,0:T(1,128)S(1)} %broadcast_in_dim.38), channel_id=1, replica_groups=mesh['tile'=4,'mem'=8] {'tile','mem'}, dimensions={0} | all-to-all | bytes 256 | tf_op jit(solution)/shard_map/all_to_all | solution.py:72
  135.6 0.6 reduce_sum.134
  137.5 0.1 multiply_add_fusion
  137.7 1.1 copy.212
  138.8 2.6 %all-to-all-start.4 = ((f32[32,2,4,1,512]{4,2,1,3,0:T(4,128)}), f32[32,2,4,1,512]{4,2,1,3,0:T(4,128)S(1)}, u32[]{:S(2)}, u32[]{:S(2)}) async-start(f32[32,2,4,1,512]{4,2,1,3,0:T(4,128)} %copy.212), calls=%async_computation.4 | async-start | bytes 1048576 | tf_op jit(solution)/shard_map/all_to_all | solution.py:195
  141.4 0.6 multiply_add_fusion.2
  142.1 15.7 %all-to-all-done.4 = f32[32,2,4,1,512]{4,2,1,3,0:T(4,128)S(1)} async-done(((f32[32,2,4,1,512]{4,2,1,3,0:T(4,128)}), f32[32,2,4,1,512]{4,2,1,3,0:T(4,128)S(1)}, u32[]{:S(2)}, u32[]{:S(2)}) %all-to-all-start.4) | async-done | bytes 524320 | tf_op jit(solution)/shard_map/all_to_all | solution.py:195
  157.8 0.3 copy.242
  158.1 0.3 copy.214
  158.4 1.0 copy.215
  (61 shorter events, 1.6 us)
Async XLA Ops:
  0.6 2.3 %copy-start.4 = (f32[1,4096]{1,0:T(1,128)S(1)}, f32[1,4096]{1,0:T(1,128)}, u32[]{:S(2)}) copy-start(f32[1,4096]{1,0:T(1,128)} %param.13) | copy-start | bytes 49156
  0.6 2.3 %copy-start.3 = (f32[1,4096]{1,0:T(1,128)S(1)}, f32[1,4096]{1,0:T(1,128)}, u32[]{:S(2)}) copy-start(f32[1,4096]{1,0:T(1,128)} %param.14) | copy-start | bytes 49156
  2.7 2.9 %copy-start.7 = (s32[4]{0:T(128)S(1)}, s32[4]{0:T(128)}, u32[]{:S(2)}) copy-start(s32[4]{0:T(128)} %param.16) | copy-start | bytes 52
  2.7 3.7 %copy-start.8 = (s32[4]{0:T(128)S(1)}, s32[4]{0:T(128)}, u32[]{:S(2)}) copy-start(s32[4]{0:T(128)} %param.17) | copy-start | bytes 52
  2.7 7.8 %copy-start.2 = (bf16[4,2,4,16,512]{4,3,2,1,0:T(8,128)(2,1)S(1)}, bf16[4,2,4,16,512]{4,3,2,1,0:T(8,128)(2,1)}, u32[]{:S(2)}) copy-start(bf16[4,2,4,16,512]{4,3,2,1,0:T(8,128)(2,1)} %param.12) | copy-start | bytes 1572868
  7.2 12.8 %collective-permute-start = (f32[9,4,512]{2,1,0:T(4,128)S(1)}, f32[9,4,512]{2,1,0:T(4,128)S(1)}, u32[]{:S(2)}, u32[]{:S(2)}) collective-permute-start(f32[9,4,512]{2,1,0:T(4,128)S(1)} %pad_maximum_fusion), channel_id=1, source_target_pairs={{0,24},{8,0},{16,8},{24,16},{1,25},{9,1},{17,9},{25,17},{2,26},{10... | collective-permute-start | bytes 221192 | tf_op jit(solution)/shard_map/ppermute | solution.py:104
  9.6 10.4 %collective-permute-start.1 = (f32[9,4,512]{2,1,0:T(4,128)S(1)}, f32[9,4,512]{2,1,0:T(4,128)S(1)}, u32[]{:S(2)}, u32[]{:S(2)}) collective-permute-start(f32[9,4,512]{2,1,0:T(4,128)S(1)} %pad_maximum_fusion), channel_id=1, source_target_pairs={{0,16},{8,24},{16,0},{24,8},{1,17},{9,25},{17,1},{25,9},{2,18},{10... | collective-permute-start | bytes 221192 | tf_op jit(solution)/shard_map/ppermute | solution.py:104
  10.3 9.8 %collective-permute-start.2 = (f32[9,4,512]{2,1,0:T(4,128)S(1)}, f32[9,4,512]{2,1,0:T(4,128)S(1)}, u32[]{:S(2)}, u32[]{:S(2)}) collective-permute-start(f32[9,4,512]{2,1,0:T(4,128)S(1)} %pad_maximum_fusion), channel_id=1, source_target_pairs={{0,8},{8,16},{16,24},{24,0},{1,9},{9,17},{17,25},{25,1},{2,10},{10... | collective-permute-start | bytes 221192 | tf_op jit(solution)/shard_map/ppermute | solution.py:104
  11.5 7.9 %copy-start.5 = (f32[16]{0:T(128)S(1)}, f32[16]{0:T(128)}, u32[]{:S(2)}) copy-start(f32[16]{0:T(128)} %param.19) | copy-start | bytes 196
  11.5 7.9 %copy-start.6 = (f32[16]{0:T(128)S(1)}, f32[16]{0:T(128)}, u32[]{:S(2)}) copy-start(f32[16]{0:T(128)} %param.18) | copy-start | bytes 196
  13.2 33.5 %all-to-all-start = ((f32[32,2,2,4,1,512]{5,3,2,1,4,0:T(4,128)}), f32[32,2,2,4,1,512]{5,3,2,1,4,0:T(4,128)S(1)}, u32[]{:S(2)}, u32[]{:S(2)}) async-start(f32[32,2,2,4,1,512]{5,3,2,1,4,0:T(4,128)} %copy.186), calls=%async_computation | async-start | bytes 2097152 | tf_op jit(solution)/shard_map/all_to_all | solution.py:164
  60.6 5.2 %collective-permute-start.3 = (f32[2,2,16,512]{3,2,1,0:T(8,128)S(1)}, f32[2,2,16,512]{3,2,1,0:T(8,128)S(1)}, u32[]{:S(2)}, u32[]{:S(2)}) collective-permute-start(f32[2,2,16,512]{3,2,1,0:T(8,128)S(1)} %copy.195), channel_id=1, source_target_pairs={{0,8},{8,16},{16,24},{24,0},{1,9},{9,17},{17,25},{25,1},{2,10},{10... | collective-permute-start | bytes 393224 | tf_op jit(solution)/shard_map/ppermute | solution.py:128
  60.6 6.4 %collective-permute-start.4 = (f32[2,2,16,512]{3,2,1,0:T(8,128)S(1)}, f32[2,2,16,512]{3,2,1,0:T(8,128)S(1)}, u32[]{:S(2)}, u32[]{:S(2)}) collective-permute-start(f32[2,2,16,512]{3,2,1,0:T(8,128)S(1)} %copy.195), channel_id=1, source_target_pairs={{0,16},{8,24},{16,0},{24,8},{1,17},{9,25},{17,1},{25,9},{2,18},{10... | collective-permute-start | bytes 393224 | tf_op jit(solution)/shard_map/ppermute | solution.py:128
  61.5 5.8 %collective-permute-start.5 = (f32[2,2,16,512]{3,2,1,0:T(8,128)S(1)}, f32[2,2,16,512]{3,2,1,0:T(8,128)S(1)}, u32[]{:S(2)}, u32[]{:S(2)}) collective-permute-start(f32[2,2,16,512]{3,2,1,0:T(8,128)S(1)} %copy.195), channel_id=1, source_target_pairs={{0,24},{8,0},{16,8},{24,16},{1,25},{9,1},{17,9},{25,17},{2,26},{10... | collective-permute-start | bytes 393224 | tf_op jit(solution)/shard_map/ppermute | solution.py:128
  67.4 6.7 %copy-start = (f32[2,16,8,512]{3,2,1,0:T(8,128)S(1)}, f32[2,16,8,512]{3,2,1,0:T(8,128)}, u32[]{:S(2)}) copy-start(f32[2,16,8,512]{3,2,1,0:T(8,128)} %shard_map.95.field_ref) | copy-start | bytes 1572868
  110.3 5.2 %collective-permute-start.6 = (f32[2,2,16,512]{3,2,1,0:T(8,128)S(1)}, f32[2,2,16,512]{3,2,1,0:T(8,128)S(1)}, u32[]{:S(2)}, u32[]{:S(2)}) collective-permute-start(f32[2,2,16,512]{3,2,1,0:T(8,128)S(1)} %copy.205), channel_id=1, source_target_pairs={{0,8},{8,16},{16,24},{24,0},{1,9},{9,17},{17,25},{25,1},{2,10},{10... | collective-permute-start | bytes 393224 | tf_op jit(solution)/shard_map/ppermute | solution.py:128
  110.4 6.4 %collective-permute-start.7 = (f32[2,2,16,512]{3,2,1,0:T(8,128)S(1)}, f32[2,2,16,512]{3,2,1,0:T(8,128)S(1)}, u32[]{:S(2)}, u32[]{:S(2)}) collective-permute-start(f32[2,2,16,512]{3,2,1,0:T(8,128)S(1)} %copy.205), channel_id=1, source_target_pairs={{0,16},{8,24},{16,0},{24,8},{1,17},{9,25},{17,1},{25,9},{2,18},{10... | collective-permute-start | bytes 393224 | tf_op jit(solution)/shard_map/ppermute | solution.py:128
  111.0 6.0 %collective-permute-start.8 = (f32[2,2,16,512]{3,2,1,0:T(8,128)S(1)}, f32[2,2,16,512]{3,2,1,0:T(8,128)S(1)}, u32[]{:S(2)}, u32[]{:S(2)}) collective-permute-start(f32[2,2,16,512]{3,2,1,0:T(8,128)S(1)} %copy.205), channel_id=1, source_target_pairs={{0,24},{8,0},{16,8},{24,16},{1,25},{9,1},{17,9},{25,17},{2,26},{10... | collective-permute-start | bytes 393224 | tf_op jit(solution)/shard_map/ppermute | solution.py:128
  117.2 6.7 %copy-start.1 = (f32[2,16,8,512]{3,2,1,0:T(8,128)S(1)}, f32[2,16,8,512]{3,2,1,0:T(8,128)}, u32[]{:S(2)}) copy-start(f32[2,16,8,512]{3,2,1,0:T(8,128)} %multiply_add_fusion.1.field_ref) | copy-start | bytes 1572868
  138.8 19.0 %all-to-all-start.4 = ((f32[32,2,4,1,512]{4,2,1,3,0:T(4,128)}), f32[32,2,4,1,512]{4,2,1,3,0:T(4,128)S(1)}, u32[]{:S(2)}, u32[]{:S(2)}) async-start(f32[32,2,4,1,512]{4,2,1,3,0:T(4,128)} %copy.212), calls=%async_computation.4 | async-start | bytes 1048576 | tf_op jit(solution)/shard_map/all_to_all | solution.py:195

commit v2 on v0

--- a/solution.py
+++ b/solution.py
@@ -1,6 +1,8 @@
 import jax
 import jax.numpy as jnp
 from jax import lax
+from jax.experimental import pallas as pl
+from jax.experimental.pallas import tpu as pltpu
 from jax.sharding import PartitionSpec as P
 
 ITERS = 2
@@ -24,6 +26,58 @@
     return mask * (
         field + lat_rate[:, None, None, None] * lat_term + lon_rate[:, None, None, None] * lon_term
     )
+
+
+def smooth_level(rates_ref, mask, now, level):
+    rows, members, nlon = now.shape
+    lat = rates_ref[0, level]
+    lon = rates_ref[1, level]
+    zero = jnp.zeros((1, members, nlon), jnp.float32)
+    now = mask * now
+    for inner in range(STEPS):
+        north = jnp.concatenate([now[1:], zero], axis=0)
+        south = jnp.concatenate([zero, now[:-1]], axis=0)
+        east = pltpu.roll(now, nlon - 1, 2)
+        west = pltpu.roll(now, 1, 2)
+        lat_term = north + south - 2.0 * now
+        lon_term = east + west - 2.0 * now
+        now = mask * (now + lat * lat_term + lon * lon_term)
+    return now
+
+
+def adjoint_kernel(rates_ref, mask_ref, pert_ref, diag_ref, state_ref, out_ref):
+    slots, levels = pert_ref.shape[:2]
+    mask = mask_ref[...]
+    for level in range(levels):
+        field = None
+        for slot in range(slots):
+            grad = diag_ref[slot, level] * state_ref[slot, level]
+            term = pert_ref[slot, level] * grad[:, None, :]
+            field = term if field is None else field + term
+        out_ref[level] = smooth_level(rates_ref, mask, field, level)
+
+
+def forward_kernel(rates_ref, mask_ref, pert_ref, field_ref, out_ref):
+    slots, levels = pert_ref.shape[:2]
+    mask = mask_ref[...]
+    for level in range(levels):
+        smoothed = smooth_level(rates_ref, mask, field_ref[level], level)
+        for slot in range(slots):
+            out_ref[slot, level] = jnp.sum(pert_ref[slot, level] * smoothed, axis=1)
+
+
+def local_call(kernel, out_shape, rates, *arrays):
+    size = sum(a.size for a in arrays)
+    return pl.pallas_call(
+        kernel,
+        out_shape=jax.ShapeDtypeStruct(out_shape, jnp.float32),
+        in_specs=[pl.BlockSpec(memory_space=pltpu.SMEM)]
+        + [pl.BlockSpec(memory_space=pltpu.VMEM)] * len(arrays),
+        out_specs=pl.BlockSpec(memory_space=pltpu.VMEM),
+        cost_estimate=pl.CostEstimate(
+            flops=16 * STEPS * size, bytes_accessed=4 * size, transcendentals=0
+        ),
+    )(rates, *arrays)
 
 
 def global_sum(value):
@@ -138,18 +192,23 @@
         )
         pert = lax.all_to_all(pert, "tile", split_axis=3, concat_axis=2, tiled=True)
 
-    def smooth(field):
-        current = mask * field
-        return lax.fori_loop(
-            0, STEPS, lambda inner, now: diffuse_step(now, mask, lat_own, lon_own), current, unroll=4
-        )
+    rates = jnp.stack([lat_own, lon_own])
 
     def forward(control):
-        smoothed = smooth(control)
-        return sum_over_tile_by_permutes(jnp.sum(pert * smoothed[None], axis=3))
-
-    def adjoint(gradient):
-        return smooth(jnp.sum(pert * gradient[:, :, :, None], axis=0))
+        partial = local_call(
+            forward_kernel,
+            (slots, own_levels, control.shape[1], nlon),
+            rates,
+            mask,
+            pert,
+            control,
+        )
+        return sum_over_tile_by_permutes(partial)
+
+    def adjoint(diag, state):
+        return local_call(
+            adjoint_kernel, pert.shape[1:], rates, mask, pert, diag, state
+        )
 
     def to_output(control):
         if share and local_members % tiles == 0:
@@ -189,14 +248,14 @@
     first_grad, obs_diag = both[0], both[1]
     me = lax.axis_index("tile")
 
-    residual = adjoint(first_grad)
+    residual = adjoint(first_grad, jnp.ones_like(first_grad))
     direction = residual
     control = jnp.zeros_like(residual)
     increment = jnp.zeros(state_shape, jnp.float32)
     norm_now = None
     for step in range(ITERS):
         state = forward(direction)
-        image = direction + adjoint(obs_diag * state)
+        image = direction + adjoint(obs_diag, state)
         if norm_now is None:
             sums = global_sum(jnp.stack([jnp.sum(residual * residual), jnp.sum(direction * image)]))
             norm_now, curvature = sums[0], sums[1]

time: 163 us -> 159 us (0.975)
  Pallas kernels: 0 us -> 27.6 us
  local copies, waits for them, and re-layouts: 26.3 us -> 11.8 us
  other arithmetic: 30.2 us -> 18 us
  waiting for transfers between devices: 58.5 us -> 48.8 us
  blocking collectives: 19.8 us -> 28.4 us
  starting transfers between devices: 18.7 us -> 16 us
    pallas_call x0 -> x5, Pallas kernels: none -> 27.6 us  [local_call(): pl.pallas_call(kernel, out_shape=jax.ShapeDtypeStruct(out_shape, jnp.floa...]
    slice x120 -> x1, local copies, waits for them, and re-layouts: 16.8 us -> 0.01 us  [body(): mask = row_mask(tables[:, 0], tables[:, 1], nlon)]
    mul x47 -> x0, other arithmetic: 16 us -> none  [the longest x40 15.5 us: diffuse_step(): mask * (field + lat_rate[:, None, None, None] * lat_term + lon_rate[:, No...]
    all_to_all x2 -> x3, blocking collectives: 19.8 us -> 28.4 us  [global_sum(): return jnp.sum(lax.all_to_all(spread, axes, 0, 0, tiled=True), axis=0)]
    all_to_all x1 -> x0, waiting for transfers between devices: 7.04 us -> none  [global_sum(): return jnp.sum(lax.all_to_all(spread, axes, 0, 0, tiled=True), axis=0)]
    add x0 -> x3, other arithmetic: none -> 4.08 us  [the longest x2 3.18 us: sum_over_tile_by_permutes(): total + lax.ppermute(block, 'tile', [(i, (i + k) % count) for i in range(...]
    reduce_sum x5 -> x0, other arithmetic: 3.77 us -> none  [the longest x3 1.96 us: adjoint(): return smooth(jnp.sum(pert * gradient[:, :, :, None], axis=0))]
    all_to_all x1 -> x0, starting transfers between devices: 2.54 us -> none  [global_sum(): return jnp.sum(lax.all_to_all(spread, axes, 0, 0, tiled=True), axis=0)]
  transfers between devices with their start and end apart: 12 -> 11, of which waited for: 9 -> 8; matrix products, arithmetic and copies ran while one was open for 3% -> 5% of each run, Pallas kernels for 0% -> 0%
where the time goes in v2:
time: 159 us; the launch traced here: 158 us
  waiting for transfers between devices  48.8 us (31%)
  blocking collectives  28.4 us (18%)
  Pallas kernels  27.6 us (17%)
  other arithmetic  18 us (11%)
  starting transfers between devices  16 us (10%)
  local copies, waits for them, and re-layouts  11.8 us (7%)
  between operations  5.09 us (3%)
  matrix products  2.47 us (2%)
    all_to_all x3, blocking collectives, global_sum(): return jnp.sum(lax.all_to_all(spread, axes, 0, 0, tiled=True), axis=0)  28.4 us
    pallas_call x5, Pallas kernels, local_call(): pl.pallas_call(kernel, out_shape=jax.ShapeDtypeStruct(out_shape, jnp.floa...  27.6 us
    all_to_all x1, waiting for transfers between devices, body(): got = lax.all_to_all(sent, ('tile', 'mem'), 0, 0, tiled=True)  24.7 us
    all_to_all x1, waiting for transfers between devices, to_output(): got = lax.all_to_all(sent, ('tile', 'mem'), 0, 0, tiled=True)  14.8 us
    ppermute x6, waiting for transfers between devices, sum_over_tile_by_permutes(): lax.ppermute(block, 'tile', [(i, (i + k) % count) for i in range(count)])  9.25 us
    all_to_all x1, starting transfers between devices, body(): got = lax.all_to_all(sent, ('tile', 'mem'), 0, 0, tiled=True)  6.12 us
    ppermute x6, starting transfers between devices, sum_over_tile_by_permutes(): lax.ppermute(block, 'tile', [(i, (i + k) % count) for i in range(count)])  4.08 us
    ppermute x3, starting transfers between devices, gather_rows_by_permutes(): lax.ppermute(block, 'tile', [(i, (i + k) % count) for i in range(count)])  3.23 us
  transfers between devices with their start and end apart: 11, of which 8 were waited for; matrix products, arithmetic and copies ran while one was open for 5% of the time, Pallas kernels for 0%

profile of v2, /device:TPU:0, one launch (start us, length us, event | category | flops | bytes accessed | tf_op | source)
XLA Modules:
  0.0 158.1 jit_solution(6101123793561870079)
XLA Ops:
  0.6 0.6 compare_reduce_fusion.1
  1.3 0.6 compare_reduce_fusion
  1.9 0.7 add_select_fusion.1
  2.7 0.2 fusion.5
  3.0 2.5 %fusion.6 = f32[64,128,2]{1,0,2:T(8,128)S(1)} fusion(f32[4096,128]{0,1:T(8,128)S(1)} %fusion.5, f32[4096,2]{0,1:T(2,128)S(1)} %pad_maximum_fusion.1, s32[4096]{0:T(1024)S(1)} %get-tuple-element.41), kind=kOutput, calls=%fused_computation.7 | convolution fusion | flops 806617088 | bytes 2211840 | tf_op jit(solution)/shard_map/dot_general | solution.py:97
  5.6 0.7 fusion.16
  6.3 0.7 fusion.17
  7.0 0.1 copy.106
  7.1 2.4 %collective-permute-start = (f32[9,4,512]{2,1,0:T(4,128)S(1)}, f32[9,4,512]{2,1,0:T(4,128)S(1)}, u32[]{:S(2)}, u32[]{:S(2)}) collective-permute-start(f32[9,4,512]{2,1,0:T(4,128)S(1)} %pad_maximum_fusion), channel_id=1, source_target_pairs={{0,24},{8,0},{16,8},{24,16},{1,25},{9,1},{17,9},{25,17},{2,26},{10... | collective-permute-start | bytes 221192 | tf_op jit(solution)/shard_map/ppermute | solution.py:120
  9.5 0.6 collective-permute-start.1
  10.2 0.2 collective-permute-start.2
  10.3 0.4 copy.114
  10.8 0.6 copy.139
  11.4 1.7 %copy.116 = f32[32,2,2,4,1,512]{5,3,2,1,4,0:T(4,128)} copy(f32[32,2,2,4,1,512]{5,0,3,2,1,4:T(8,128)S(1)} %bitcast.95) | data formatting | bytes 2097152 | tf_op jit(solution)/shard_map/reshape | solution.py:177
  13.0 6.1 %all-to-all-start = ((f32[32,2,2,4,1,512]{5,3,2,1,4,0:T(4,128)}), f32[32,2,2,4,1,512]{5,3,2,1,4,0:T(4,128)S(1)}, u32[]{:S(2)}, u32[]{:S(2)}) async-start(f32[32,2,2,4,1,512]{5,3,2,1,4,0:T(4,128)} %copy.116), calls=%async_computation | async-start | bytes 2097152 | tf_op jit(solution)/shard_map/all_to_all | solution.py:180
  19.3 0.1 dynamic-slice_bitcast_fusion
  19.3 0.6 pad_maximum_fusion.2.rates_ref
  20.1 0.7 squeeze.25.diag_ref
  20.8 0.1 reshape.296
  20.9 0.1 copy.133
  21.0 0.8 compare_select_fusion.2.mask_ref
  21.8 24.7 %all-to-all-done = f32[32,2,2,4,1,512]{5,3,2,1,4,0:T(4,128)S(1)} async-done(((f32[32,2,2,4,1,512]{5,3,2,1,4,0:T(4,128)}), f32[32,2,2,4,1,512]{5,3,2,1,4,0:T(4,128)S(1)}, u32[]{:S(2)}, u32[]{:S(2)}) %all-to-all-start) | async-done | bytes 1048608 | tf_op jit(solution)/shard_map/all_to_all | solution.py:180
  46.6 0.6 copy.138
  47.2 1.1 copy.118
  48.3 0.7 broadcast_in_dim.35.state_ref
  48.9 5.4 %shard_map.95.field_ref = f32[2,16,8,512]{3,2,1,0:T(8,128)} custom-call(f32[2,2]{1,0:T(2,128)} %pad_maximum_fusion.2.rates_ref, f32[16,1,512]{2,1,0:T(1,128)} %compare_select_fusion.2.mask_ref, f32[2,2,16,8,512]{4,3,2,1,0:T(8,128)} %bitcast.90, f32[2,2,16,512]{3,2,1,0:T(8,128)} %squeeze.25.diag_ref, f32[2,2,16,512]{3,2,1,0:T(8,128)} %broadcast_in_dim.35.state_ref), custom_call_target="tpu_custom_call" | custom-call | flops 42991616 | bytes 1343488 | tf_op jit(solution)/shard_map/pallas_call | solution.py:71
  54.4 5.7 %shard_map.96 = f32[2,2,16,512]{3,2,1,0:T(8,128)} custom-call(f32[2,2]{1,0:T(2,128)} %pad_maximum_fusion.2.rates_ref, f32[16,1,512]{2,1,0:T(1,128)} %compare_select_fusion.2.mask_ref, f32[2,2,16,8,512]{4,3,2,1,0:T(8,128)} %bitcast.91, f32[2,16,8,512]{3,2,1,0:T(8,128)} %shard_map.95.field_ref), custom_call_target="tpu_custom_call" | custom-call | flops 51380224 | bytes 1605632 | tf_op jit(solution)/shard_map/pallas_call | solution.py:71
  60.0 0.9 collective-permute-start.4
  60.9 1.2 collective-permute-start.5
  62.0 0.7 squeeze.26.diag_ref
  62.7 2.7 %collective-permute-done.3 = f32[2,2,16,512]{3,2,1,0:T(8,128)S(1)} collective-permute-done((f32[2,2,16,512]{3,2,1,0:T(8,128)}, f32[2,2,16,512]{3,2,1,0:T(8,128)S(1)}, u32[]{:S(2)}, u32[]{:S(2)}) %collective-permute-start.3) | collective-permute-done | bytes 131104 | tf_op jit(solution)/shard_map/ppermute | solution.py:144
  65.5 1.1 collective-permute-done.4
  66.6 0.4 collective-permute-done.5
  67.0 1.6 %add_add_fusion.1.state_ref = f32[2,2,16,512]{3,2,1,0:T(8,128)} fusion(f32[2,2,16,512]{3,2,1,0:T(8,128)S(1)} %collective-permute-done.5, f32[2,2,16,512]{3,2,1,0:T(8,128)S(1)} %collective-permute-done.4, f32[2,2,16,512]{3,2,1,0:T(8,128)} %shard_map.96, f32[2,2,16,512]{3,2,1,0:T(8,128)S(1)} %collective-permute-done.3), kind=kLoop, calls=%fused_computation.27 | loop fusion | flops 98304 | bytes 655360 | tf_op jit(solution)/shard_map/add | solution.py:144
  68.6 5.4 %shard_map.97 = f32[2,16,8,512]{3,2,1,0:T(8,128)} custom-call(f32[2,2]{1,0:T(2,128)} %pad_maximum_fusion.2.rates_ref, f32[16,1,512]{2,1,0:T(1,128)} %compare_select_fusion.2.mask_ref, f32[2,2,16,8,512]{4,3,2,1,0:T(8,128)} %bitcast.92, f32[2,2,16,512]{3,2,1,0:T(8,128)} %squeeze.26.diag_ref, f32[2,2,16,512]{3,2,1,0:T(8,128)} %add_add_fusion.1.state_ref), custom_call_target="tpu_custom_call" | custom-call | flops 42991616 | bytes 1343488 | tf_op jit(solution)/shard_map/pallas_call | solution.py:71
  74.0 1.9 %multiply_reduce_fusion.2 = (f32[]{:T(128)}, f32[]{:T(128)}, f32[2,16,8,512]{3,2,1,0:T(8,128)S(1)}) fusion(f32[2,16,8,512]{3,2,1,0:T(8,128)S(1)} %copy-done, f32[2,16,8,512]{3,2,1,0:T(8,128)} %shard_map.97), kind=kLoop, calls=%fused_computation.21 | loop fusion | flops 655358 | bytes 1572872 | tf_op jit(solution)/shard_map/reduce_sum | solution.py:260
  75.9 1.4 pad_maximum_fusion.3
  77.3 10.4 %all_to_all.28 = f32[32,1,2]{2,1,0:T(1,128)S(1)} all-to-all(f32[32,1,2]{2,1,0:T(1,128)S(1)} %broadcast_in_dim.36), channel_id=1, replica_groups=mesh['tile'=4,'mem'=8] {'tile','mem'}, dimensions={0} | all-to-all | bytes 512 | tf_op jit(solution)/shard_map/all_to_all | solution.py:88
  87.8 0.6 fusion.18
  89.8 0.8 multiply_reduce_fusion
  90.6 0.7 broadcast_in_dim.37
  91.2 8.8 %all_to_all.29 = f32[32,1,1]{2,1,0:T(1,128)S(1)} all-to-all(f32[32,1,1]{2,1,0:T(1,128)S(1)} %broadcast_in_dim.37), channel_id=1, replica_groups=mesh['tile'=4,'mem'=8] {'tile','mem'}, dimensions={0} | all-to-all | bytes 256 | tf_op jit(solution)/shard_map/all_to_all | solution.py:88
  100.0 0.7 reduce_sum.67
  102.1 0.9 multiply_add_fusion.1.field_ref
  103.0 5.6 %shard_map.98 = f32[2,2,16,512]{3,2,1,0:T(8,128)} custom-call(f32[2,2]{1,0:T(2,128)} %pad_maximum_fusion.2.rates_ref, f32[16,1,512]{2,1,0:T(1,128)} %compare_select_fusion.2.mask_ref, f32[2,2,16,8,512]{4,3,2,1,0:T(8,128)} %bitcast.93, f32[2,16,8,512]{3,2,1,0:T(8,128)} %multiply_add_fusion.1.field_ref), custom_call_target="tpu_custom_call" | custom-call | flops 51380224 | bytes 1605632 | tf_op jit(solution)/shard_map/pallas_call | solution.py:71
  108.7 0.6 collective-permute-start.7
  109.3 1.4 collective-permute-start.8
  110.7 3.4 %collective-permute-done.6 = f32[2,2,16,512]{3,2,1,0:T(8,128)S(1)} collective-permute-done((f32[2,2,16,512]{3,2,1,0:T(8,128)}, f32[2,2,16,512]{3,2,1,0:T(8,128)S(1)}, u32[]{:S(2)}, u32[]{:S(2)}) %collective-permute-start.6) | collective-permute-done | bytes 131104 | tf_op jit(solution)/shard_map/ppermute | solution.py:144
  114.1 1.1 collective-permute-done.7
  115.2 0.5 collective-permute-done.8
  115.7 1.6 %add_add_fusion.state_ref = f32[2,2,16,512]{3,2,1,0:T(8,128)} fusion(f32[2,2,16,512]{3,2,1,0:T(8,128)S(1)} %collective-permute-done.8, f32[2,2,16,512]{3,2,1,0:T(8,128)S(1)} %collective-permute-done.7, f32[2,2,16,512]{3,2,1,0:T(8,128)} %shard_map.98, f32[2,2,16,512]{3,2,1,0:T(8,128)S(1)} %collective-permute-done.6), kind=kLoop, calls=%fused_computation.26 | loop fusion | flops 98304 | bytes 655360 | tf_op jit(solution)/shard_map/add | solution.py:144
  117.3 5.4 %shard_map.99 = f32[2,16,8,512]{3,2,1,0:T(8,128)} custom-call(f32[2,2]{1,0:T(2,128)} %pad_maximum_fusion.2.rates_ref, f32[16,1,512]{2,1,0:T(1,128)} %compare_select_fusion.2.mask_ref, f32[2,2,16,8,512]{4,3,2,1,0:T(8,128)} %bitcast.94, f32[2,2,16,512]{3,2,1,0:T(8,128)} %squeeze.26.diag_ref, f32[2,2,16,512]{3,2,1,0:T(8,128)} %add_add_fusion.state_ref), custom_call_target="tpu_custom_call" | custom-call | flops 42991616 | bytes 1343488 | tf_op jit(solution)/shard_map/pallas_call | solution.py:71
  122.7 1.8 %fusion.11 = f32[]{:T(128)} fusion(f32[2,16,8,512]{3,2,1,0:T(8,128)S(1)} %copy-done.1, f32[2,16,8,512]{3,2,1,0:T(8,128)} %shard_map.99), kind=kLoop, calls=%fused_computation.13 | loop fusion | flops 393215 | bytes 1048580 | tf_op jit(solution)/shard_map/reduce_sum | solution.py:263
  124.5 0.7 broadcast_in_dim.38
  125.2 9.1 %all_to_all.30 = f32[32,1,1]{2,1,0:T(1,128)S(1)} all-to-all(f32[32,1,1]{2,1,0:T(1,128)S(1)} %broadcast_in_dim.38), channel_id=1, replica_groups=mesh['tile'=4,'mem'=8] {'tile','mem'}, dimensions={0} | all-to-all | bytes 256 | tf_op jit(solution)/shard_map/all_to_all | solution.py:88
  134.3 0.6 reduce_sum.69
  136.3 0.1 multiply_add_fusion
  136.4 1.1 copy.123
  137.5 2.6 %all-to-all-start.4 = ((f32[32,2,4,1,512]{4,2,1,3,0:T(4,128)}), f32[32,2,4,1,512]{4,2,1,3,0:T(4,128)S(1)}, u32[]{:S(2)}, u32[]{:S(2)}) async-start(f32[32,2,4,1,512]{4,2,1,3,0:T(4,128)} %copy.123), calls=%async_computation.4 | async-start | bytes 1048576 | tf_op jit(solution)/shard_map/all_to_all | solution.py:219
  140.2 1.5 multiply_add_fusion.2
  141.7 14.8 %all-to-all-done.4 = f32[32,2,4,1,512]{4,2,1,3,0:T(4,128)S(1)} async-done(((f32[32,2,4,1,512]{4,2,1,3,0:T(4,128)}), f32[32,2,4,1,512]{4,2,1,3,0:T(4,128)S(1)}, u32[]{:S(2)}, u32[]{:S(2)}) %all-to-all-start.4) | async-done | bytes 524320 | tf_op jit(solution)/shard_map/all_to_all | solution.py:219
  156.5 0.3 copy.140
  156.8 0.3 copy.125
  157.2 1.0 copy.126
  (45 shorter events, 0.5 us)
Async XLA Ops:
  0.6 2.3 %copy-start.4 = (f32[1,4096]{1,0:T(1,128)S(1)}, f32[1,4096]{1,0:T(1,128)}, u32[]{:S(2)}) copy-start(f32[1,4096]{1,0:T(1,128)} %param.13) | copy-start | bytes 49156
  0.6 2.3 %copy-start.3 = (f32[1,4096]{1,0:T(1,128)S(1)}, f32[1,4096]{1,0:T(1,128)}, u32[]{:S(2)}) copy-start(f32[1,4096]{1,0:T(1,128)} %param.14) | copy-start | bytes 49156
  2.7 2.9 %copy-start.7 = (s32[4]{0:T(128)S(1)}, s32[4]{0:T(128)}, u32[]{:S(2)}) copy-start(s32[4]{0:T(128)} %param.16) | copy-start | bytes 52
  2.7 3.6 %copy-start.8 = (s32[4]{0:T(128)S(1)}, s32[4]{0:T(128)}, u32[]{:S(2)}) copy-start(s32[4]{0:T(128)} %param.17) | copy-start | bytes 52
  2.9 7.4 %copy-start.2 = (bf16[4,2,4,16,512]{4,3,2,1,0:T(8,128)(2,1)S(1)}, bf16[4,2,4,16,512]{4,3,2,1,0:T(8,128)(2,1)}, u32[]{:S(2)}) copy-start(bf16[4,2,4,16,512]{4,3,2,1,0:T(8,128)(2,1)} %param.12) | copy-start | bytes 1572868
  7.1 12.8 %collective-permute-start = (f32[9,4,512]{2,1,0:T(4,128)S(1)}, f32[9,4,512]{2,1,0:T(4,128)S(1)}, u32[]{:S(2)}, u32[]{:S(2)}) collective-permute-start(f32[9,4,512]{2,1,0:T(4,128)S(1)} %pad_maximum_fusion), channel_id=1, source_target_pairs={{0,24},{8,0},{16,8},{24,16},{1,25},{9,1},{17,9},{25,17},{2,26},{10... | collective-permute-start | bytes 221192 | tf_op jit(solution)/shard_map/ppermute | solution.py:120
  9.5 10.4 %collective-permute-start.1 = (f32[9,4,512]{2,1,0:T(4,128)S(1)}, f32[9,4,512]{2,1,0:T(4,128)S(1)}, u32[]{:S(2)}, u32[]{:S(2)}) collective-permute-start(f32[9,4,512]{2,1,0:T(4,128)S(1)} %pad_maximum_fusion), channel_id=1, source_target_pairs={{0,16},{8,24},{16,0},{24,8},{1,17},{9,25},{17,1},{25,9},{2,18},{10... | collective-permute-start | bytes 221192 | tf_op jit(solution)/shard_map/ppermute | solution.py:120
  10.2 9.8 %collective-permute-start.2 = (f32[9,4,512]{2,1,0:T(4,128)S(1)}, f32[9,4,512]{2,1,0:T(4,128)S(1)}, u32[]{:S(2)}, u32[]{:S(2)}) collective-permute-start(f32[9,4,512]{2,1,0:T(4,128)S(1)} %pad_maximum_fusion), channel_id=1, source_target_pairs={{0,8},{8,16},{16,24},{24,0},{1,9},{9,17},{17,25},{25,1},{2,10},{10... | collective-permute-start | bytes 221192 | tf_op jit(solution)/shard_map/ppermute | solution.py:120
  11.4 7.9 %copy-start.5 = (f32[16]{0:T(128)S(1)}, f32[16]{0:T(128)}, u32[]{:S(2)}) copy-start(f32[16]{0:T(128)} %param.19) | copy-start | bytes 196
  11.4 7.9 %copy-start.6 = (f32[16]{0:T(128)S(1)}, f32[16]{0:T(128)}, u32[]{:S(2)}) copy-start(f32[16]{0:T(128)} %param.18) | copy-start | bytes 196
  13.0 33.5 %all-to-all-start = ((f32[32,2,2,4,1,512]{5,3,2,1,4,0:T(4,128)}), f32[32,2,2,4,1,512]{5,3,2,1,4,0:T(4,128)S(1)}, u32[]{:S(2)}, u32[]{:S(2)}) async-start(f32[32,2,2,4,1,512]{5,3,2,1,4,0:T(4,128)} %copy.116), calls=%async_computation | async-start | bytes 2097152 | tf_op jit(solution)/shard_map/all_to_all | solution.py:180
  54.4 19.7 %copy-start = (f32[2,16,8,512]{3,2,1,0:T(8,128)S(1)}, f32[2,16,8,512]{3,2,1,0:T(8,128)}, u32[]{:S(2)}) copy-start(f32[2,16,8,512]{3,2,1,0:T(8,128)} %shard_map.95.field_ref) | copy-start | bytes 1572868
  60.0 5.5 %collective-permute-start.3 = (f32[2,2,16,512]{3,2,1,0:T(8,128)}, f32[2,2,16,512]{3,2,1,0:T(8,128)S(1)}, u32[]{:S(2)}, u32[]{:S(2)}) collective-permute-start(f32[2,2,16,512]{3,2,1,0:T(8,128)} %shard_map.96), channel_id=1, source_target_pairs={{0,8},{8,16},{16,24},{24,0},{1,9},{9,17},{17,25},{25,1},{2,10},{10... | collective-permute-start | bytes 393224 | tf_op jit(solution)/shard_map/ppermute | solution.py:144
  60.0 6.6 %collective-permute-start.4 = (f32[2,2,16,512]{3,2,1,0:T(8,128)}, f32[2,2,16,512]{3,2,1,0:T(8,128)S(1)}, u32[]{:S(2)}, u32[]{:S(2)}) collective-permute-start(f32[2,2,16,512]{3,2,1,0:T(8,128)} %shard_map.96), channel_id=1, source_target_pairs={{0,16},{8,24},{16,0},{24,8},{1,17},{9,25},{17,1},{25,9},{2,18},{10... | collective-permute-start | bytes 393224 | tf_op jit(solution)/shard_map/ppermute | solution.py:144
  60.9 6.1 %collective-permute-start.5 = (f32[2,2,16,512]{3,2,1,0:T(8,128)}, f32[2,2,16,512]{3,2,1,0:T(8,128)S(1)}, u32[]{:S(2)}, u32[]{:S(2)}) collective-permute-start(f32[2,2,16,512]{3,2,1,0:T(8,128)} %shard_map.96), channel_id=1, source_target_pairs={{0,24},{8,0},{16,8},{24,16},{1,25},{9,1},{17,9},{25,17},{2,26},{10... | collective-permute-start | bytes 393224 | tf_op jit(solution)/shard_map/ppermute | solution.py:144
  103.0 19.7 %copy-start.1 = (f32[2,16,8,512]{3,2,1,0:T(8,128)S(1)}, f32[2,16,8,512]{3,2,1,0:T(8,128)}, u32[]{:S(2)}) copy-start(f32[2,16,8,512]{3,2,1,0:T(8,128)} %multiply_add_fusion.1.field_ref) | copy-start | bytes 1572868
  108.7 5.5 %collective-permute-start.6 = (f32[2,2,16,512]{3,2,1,0:T(8,128)}, f32[2,2,16,512]{3,2,1,0:T(8,128)S(1)}, u32[]{:S(2)}, u32[]{:S(2)}) collective-permute-start(f32[2,2,16,512]{3,2,1,0:T(8,128)} %shard_map.98), channel_id=1, source_target_pairs={{0,8},{8,16},{16,24},{24,0},{1,9},{9,17},{17,25},{25,1},{2,10},{10... | collective-permute-start | bytes 393224 | tf_op jit(solution)/shard_map/ppermute | solution.py:144
  108.7 6.6 %collective-permute-start.7 = (f32[2,2,16,512]{3,2,1,0:T(8,128)}, f32[2,2,16,512]{3,2,1,0:T(8,128)S(1)}, u32[]{:S(2)}, u32[]{:S(2)}) collective-permute-start(f32[2,2,16,512]{3,2,1,0:T(8,128)} %shard_map.98), channel_id=1, source_target_pairs={{0,16},{8,24},{16,0},{24,8},{1,17},{9,25},{17,1},{25,9},{2,18},{10... | collective-permute-start | bytes 393224 | tf_op jit(solution)/shard_map/ppermute | solution.py:144
  109.3 6.4 %collective-permute-start.8 = (f32[2,2,16,512]{3,2,1,0:T(8,128)}, f32[2,2,16,512]{3,2,1,0:T(8,128)S(1)}, u32[]{:S(2)}, u32[]{:S(2)}) collective-permute-start(f32[2,2,16,512]{3,2,1,0:T(8,128)} %shard_map.98), channel_id=1, source_target_pairs={{0,24},{8,0},{16,8},{24,16},{1,25},{9,1},{17,9},{25,17},{2,26},{10... | collective-permute-start | bytes 393224 | tf_op jit(solution)/shard_map/ppermute | solution.py:144
  137.5 19.0 %all-to-all-start.4 = ((f32[32,2,4,1,512]{4,2,1,3,0:T(4,128)}), f32[32,2,4,1,512]{4,2,1,3,0:T(4,128)S(1)}, u32[]{:S(2)}, u32[]{:S(2)}) async-start(f32[32,2,4,1,512]{4,2,1,3,0:T(4,128)} %copy.123), calls=%async_computation.4 | async-start | bytes 1048576 | tf_op jit(solution)/shard_map/all_to_all | solution.py:219

commit v3 on v2

--- a/solution.py
+++ b/solution.py
@@ -177,11 +177,16 @@
         sent = sent.transpose(0, 4, 2, 5, 3, 1, 6).reshape(
             tiles * groups, slots, own_levels, lat_rows, share, nlon
         )
-        got = lax.all_to_all(sent, ("tile", "mem"), 0, 0, tiled=True)
-        pert = got.reshape(tiles, groups, slots, own_levels, lat_rows, share, nlon)
-        pert = pert.transpose(2, 3, 0, 4, 1, 5, 6).reshape(
-            slots, own_levels, tiles * lat_rows, groups * share, nlon
-        )
+        pert_levels = []
+        for level in range(own_levels):
+            got = lax.all_to_all(sent[:, :, level : level + 1], ("tile", "mem"), 0, 0, tiled=True)
+            got = got.reshape(tiles, groups, slots, 1, lat_rows, share, nlon)
+            pert_levels.append(
+                got.transpose(2, 3, 0, 4, 1, 5, 6).reshape(
+                    slots, 1, tiles * lat_rows, groups * share, nlon
+                )
+            )
+        pert = jnp.concatenate(pert_levels, axis=1) if own_levels > 1 else pert_levels[0]
     else:
         pert = lax.all_to_all(
             perturbations.astype(jnp.float32).transpose(1, 3, 2, 0, 4),
@@ -191,24 +196,51 @@
             tiled=True,
         )
         pert = lax.all_to_all(pert, "tile", split_axis=3, concat_axis=2, tiled=True)
+        pert_levels = [pert[:, level : level + 1] for level in range(own_levels)]
 
     rates = jnp.stack([lat_own, lon_own])
 
-    def forward(control):
-        partial = local_call(
-            forward_kernel,
-            (slots, own_levels, control.shape[1], nlon),
-            rates,
-            mask,
-            pert,
-            control,
-        )
+    def forward(control, by_level=False):
+        if by_level:
+            parts = [
+                local_call(
+                    forward_kernel,
+                    (slots, 1, control.shape[1], nlon),
+                    rates[:, level : level + 1],
+                    mask,
+                    pert_levels[level],
+                    control[level : level + 1],
+                )
+                for level in range(own_levels)
+            ]
+            partial = jnp.concatenate(parts, axis=1) if own_levels > 1 else parts[0]
+        else:
+            partial = local_call(
+                forward_kernel,
+                (slots, own_levels, control.shape[1], nlon),
+                rates,
+                mask,
+                pert,
+                control,
+            )
         return sum_over_tile_by_permutes(partial)
 
-    def adjoint(diag, state):
-        return local_call(
-            adjoint_kernel, pert.shape[1:], rates, mask, pert, diag, state
-        )
+    def adjoint(diag, state, by_level=False):
+        if not by_level:
+            return local_call(adjoint_kernel, pert.shape[1:], rates, mask, pert, diag, state)
+        parts = [
+            local_call(
+                adjoint_kernel,
+                (1,) + pert.shape[2:],
+                rates[:, level : level + 1],
+                mask,
+                pert_levels[level],
+                diag[:, level : level + 1],
+                state[:, level : level + 1],
+            )
+            for level in range(own_levels)
+        ]
+        return jnp.concatenate(parts, axis=0) if own_levels > 1 else parts[0]
 
     def to_output(control):
         if share and local_members % tiles == 0:
@@ -248,13 +280,13 @@
     first_grad, obs_diag = both[0], both[1]
     me = lax.axis_index("tile")
 
-    residual = adjoint(first_grad, jnp.ones_like(first_grad))
+    residual = adjoint(first_grad, jnp.ones_like(first_grad), by_level=True)
     direction = residual
     control = jnp.zeros_like(residual)
     increment = jnp.zeros(state_shape, jnp.float32)
     norm_now = None
     for step in range(ITERS):
-        state = forward(direction)
+        state = forward(direction, by_level=step == 0)
         image = direction + adjoint(obs_diag, state)
         if norm_now is None:
             sums = global_sum(jnp.stack([jnp.sum(residual * residual), jnp.sum(direction * image)]))

time: 159 us -> 162 us (1.019)
  waiting for transfers between devices: 48.8 us -> 42.5 us
  Pallas kernels: 27.6 us -> 30.5 us
  starting transfers between devices: 16 us -> 18.7 us
  local copies, waits for them, and re-layouts: 11.8 us -> 13.7 us
    all_to_all x1 -> x2, waiting for transfers between devices: 24.7 us -> 19.1 us  [body(): lax.all_to_all(sent[:, :, level:level + 1], ('tile', 'mem'), 0, 0, tiled=...]
    slice x0 -> x5, local copies, waits for them, and re-layouts: none -> 3.67 us  [the longest x3 2.37 us: body(): sent[:, :, level:level + 1]]
    pallas_call x5 -> x7, Pallas kernels: 27.6 us -> 30.5 us  [local_call(): pl.pallas_call(kernel, out_shape=jax.ShapeDtypeStruct(out_shape, jnp.floa...]
    all_to_all x1 -> x2, starting transfers between devices: 6.12 us -> 8.73 us  [body(): lax.all_to_all(sent[:, :, level:level + 1], ('tile', 'mem'), 0, 0, tiled=...]
    concatenate x0 -> x2, other arithmetic: none -> 1.96 us  [the longest x1 1.04 us: body(): jnp.concatenate(pert_levels, axis=1)]
    reshape x3 -> x2, local copies, waits for them, and re-layouts: 2.68 us -> 1.02 us  [body(): sent.transpose(0, 4, 2, 5, 3, 1, 6)]
  transfers between devices with their start and end apart: 11 -> 12, of which waited for: 8 -> 9; matrix products, arithmetic and copies ran while one was open for 5% -> 7% of each run, Pallas kernels for 0% -> 4%
where the time goes in v3:
time: 162 us; the launch traced here: 161 us
  waiting for transfers between devices  42.5 us (26%)
  Pallas kernels  30.5 us (19%)
  blocking collectives  28.4 us (18%)
  other arithmetic  19.5 us (12%)
  starting transfers between devices  18.7 us (12%)
  local copies, waits for them, and re-layouts  13.7 us (8%)
  between operations  5.09 us (3%)
  matrix products  2.47 us (2%)
    pallas_call x7, Pallas kernels, local_call(): pl.pallas_call(kernel, out_shape=jax.ShapeDtypeStruct(out_shape, jnp.floa...  30.5 us
    all_to_all x3, blocking collectives, global_sum(): return jnp.sum(lax.all_to_all(spread, axes, 0, 0, tiled=True), axis=0)  28.4 us
    all_to_all x2, waiting for transfers between devices, body(): lax.all_to_all(sent[:, :, level:level + 1], ('tile', 'mem'), 0, 0, tiled=...  19.1 us
    all_to_all x1, waiting for transfers between devices, to_output(): got = lax.all_to_all(sent, ('tile', 'mem'), 0, 0, tiled=True)  14.8 us
    all_to_all x2, starting transfers between devices, body(): lax.all_to_all(sent[:, :, level:level + 1], ('tile', 'mem'), 0, 0, tiled=...  8.73 us
    ppermute x6, waiting for transfers between devices, sum_over_tile_by_permutes(): lax.ppermute(block, 'tile', [(i, (i + k) % count) for i in range(count)])  8.58 us
    ppermute x6, starting transfers between devices, sum_over_tile_by_permutes(): lax.ppermute(block, 'tile', [(i, (i + k) % count) for i in range(count)])  4.12 us
  transfers between devices with their start and end apart: 12, of which 9 were waited for; matrix products, arithmetic and copies ran while one was open for 7% of the time, Pallas kernels for 4%

profile of v3, /device:TPU:0, one launch (start us, length us, event | category | flops | bytes accessed | tf_op | source)
XLA Modules:
  0.0 160.9 jit_solution(11499486250835019688)
XLA Ops:
  0.6 0.6 compare_reduce_fusion.1
  1.3 0.6 compare_reduce_fusion
  1.9 0.7 add_select_fusion.1
  3.0 2.5 %fusion.6 = f32[64,128,2]{1,0,2:T(8,128)S(1)} fusion(f32[4096,128]{0,1:T(8,128)S(1)} %fusion.5, f32[4096,2]{0,1:T(2,128)S(1)} %pad_maximum_fusion.4, s32[4096]{0:T(1024)S(1)} %get-tuple-element.44), kind=kOutput, calls=%fused_computation.7 | convolution fusion | flops 806617088 | bytes 2211840 | tf_op jit(solution)/shard_map/dot_general | solution.py:97
  5.6 0.7 fusion.17
  6.3 0.7 fusion.18
  7.1 2.4 %collective-permute-start = (f32[9,4,512]{2,1,0:T(4,128)S(1)}, f32[9,4,512]{2,1,0:T(4,128)S(1)}, u32[]{:S(2)}, u32[]{:S(2)}) collective-permute-start(f32[9,4,512]{2,1,0:T(4,128)S(1)} %pad_maximum_fusion.3), channel_id=1, source_target_pairs={{0,24},{8,0},{16,8},{24,16},{1,25},{9,1},{17,9},{25,17},{2,26},{10... | collective-permute-start | bytes 221192 | tf_op jit(solution)/shard_map/ppermute | solution.py:120
  9.5 0.6 collective-permute-start.1
  10.3 0.4 copy.125
  10.8 0.6 copy.153
  11.5 1.1 copy.127
  12.6 5.9 %all-to-all-start = ((f32[32,2,1,4,1,512]{5,3,2,1,4,0:T(4,128)}), f32[32,2,1,4,1,512]{5,3,2,1,4,0:T(4,128)S(1)}, u32[]{:S(2)}, u32[]{:S(2)}) async-start(f32[32,2,1,4,1,512]{5,3,2,1,4,0:T(4,128)} %copy.127), calls=%async_computation | async-start | bytes 1048576 | tf_op jit(solution)/shard_map/all_to_all | solution.py:182
  18.7 0.6 fusion.21
  19.4 1.1 copy.130
  20.8 14.1 %all-to-all-done = f32[32,2,1,4,1,512]{5,3,2,1,4,0:T(4,128)S(1)} async-done(((f32[32,2,1,4,1,512]{5,3,2,1,4,0:T(4,128)}), f32[32,2,1,4,1,512]{5,3,2,1,4,0:T(4,128)S(1)}, u32[]{:S(2)}, u32[]{:S(2)}) %all-to-all-start) | async-done | bytes 524320 | tf_op jit(solution)/shard_map/all_to_all | solution.py:182
  34.9 2.8 %all-to-all-start.1 = ((f32[32,2,1,4,1,512]{5,3,2,1,4,0:T(4,128)}), f32[32,2,1,4,1,512]{5,3,2,1,4,0:T(4,128)S(1)}, u32[]{:S(2)}, u32[]{:S(2)}) async-start(f32[32,2,1,4,1,512]{5,3,2,1,4,0:T(4,128)} %copy.130), calls=%async_computation.1 | async-start | bytes 1048576 | tf_op jit(solution)/shard_map/all_to_all | solution.py:182
  38.0 0.7 squeeze.26.diag_ref
  38.7 0.8 compare_select_fusion.2.mask_ref
  39.5 0.7 fusion.20
  40.1 0.3 copy.157
  40.5 0.8 copy.129
  41.3 0.6 broadcast_5_state_ref.2.state_ref
  41.9 3.5 %shard_map.95.field_ref = f32[1,16,8,512]{3,2,1,0:T(8,128)} custom-call(f32[2,1]{1,0:T(2,128)} %get-tuple-element.46.rates_ref, f32[16,1,512]{2,1,0:T(1,128)} %compare_select_fusion.2.mask_ref, f32[2,1,16,8,512]{4,3,2,1,0:T(8,128)} %bitcast.96, f32[2,1,16,512]{3,2,1,0:T(8,128)} %get-tuple-element.42.diag_ref, f32[2,1,16,512]{3,2,1,0:T(8,128)} %broadcast_5_state_ref.2.state_ref), custom_call_target="tpu_custom_call" | custom-call | flops 22020096 | bytes 688128 | tf_op jit(solution)/shard_map/pallas_call | solution.py:71
  45.4 3.6 %shard_map.97 = f32[2,1,16,512]{3,2,1,0:T(8,128)} custom-call(f32[2,1]{1,0:T(2,128)} %get-tuple-element.46.rates_ref, f32[16,1,512]{2,1,0:T(1,128)} %compare_select_fusion.2.mask_ref, f32[2,1,16,8,512]{4,3,2,1,0:T(8,128)} %bitcast.97, f32[1,16,8,512]{3,2,1,0:T(8,128)} %shard_map.95.field_ref), custom_call_target="tpu_custom_call" | custom-call | flops 26214400 | bytes 819200 | tf_op jit(solution)/shard_map/pallas_call | solution.py:71
  49.0 4.9 %all-to-all-done.1 = f32[32,2,1,4,1,512]{5,3,2,1,4,0:T(4,128)S(1)} async-done(((f32[32,2,1,4,1,512]{5,3,2,1,4,0:T(4,128)}), f32[32,2,1,4,1,512]{5,3,2,1,4,0:T(4,128)S(1)}, u32[]{:S(2)}, u32[]{:S(2)}) %all-to-all-start.1) | async-done | bytes 524320 | tf_op jit(solution)/shard_map/all_to_all | solution.py:182
  54.2 0.8 copy.132
  55.1 3.5 %shard_map.96.field_ref = f32[1,16,8,512]{3,2,1,0:T(8,128)} custom-call(f32[2,1]{1,0:T(2,128)} %get-tuple-element.47.rates_ref, f32[16,1,512]{2,1,0:T(1,128)} %compare_select_fusion.2.mask_ref, f32[2,1,16,8,512]{4,3,2,1,0:T(8,128)} %bitcast.99, f32[2,1,16,512]{3,2,1,0:T(8,128)} %get-tuple-element.43.diag_ref, f32[2,1,16,512]{3,2,1,0:T(8,128)} %broadcast_5_state_ref.2.state_ref), custom_call_target="tpu_custom_call" | custom-call | flops 22020096 | bytes 688128 | tf_op jit(solution)/shard_map/pallas_call | solution.py:71
  58.6 3.6 %shard_map.98 = f32[2,1,16,512]{3,2,1,0:T(8,128)} custom-call(f32[2,1]{1,0:T(2,128)} %get-tuple-element.47.rates_ref, f32[16,1,512]{2,1,0:T(1,128)} %compare_select_fusion.2.mask_ref, f32[2,1,16,8,512]{4,3,2,1,0:T(8,128)} %bitcast.100, f32[1,16,8,512]{3,2,1,0:T(8,128)} %shard_map.96.field_ref), custom_call_target="tpu_custom_call" | custom-call | flops 26214400 | bytes 819200 | tf_op jit(solution)/shard_map/pallas_call | solution.py:71
  62.1 0.9 pad_maximum_fusion.2
  63.2 0.8 collective-permute-start.4
  64.0 1.2 collective-permute-start.5
  65.2 1.0 pad_maximum_fusion.pert_ref
  66.2 2.1 %collective-permute-done.3 = f32[2,2,16,512]{3,2,1,0:T(8,128)S(1)} collective-permute-done((f32[2,2,16,512]{3,2,1,0:T(8,128)S(1)}, f32[2,2,16,512]{3,2,1,0:T(8,128)S(1)}, u32[]{:S(2)}, u32[]{:S(2)}) %collective-permute-start.3) | collective-permute-done | bytes 131104 | tf_op jit(solution)/shard_map/ppermute | solution.py:144
  68.3 1.2 collective-permute-done.4
  69.8 0.7 add_add_fusion.1.state_ref
  70.5 5.4 %shard_map.99 = f32[2,16,8,512]{3,2,1,0:T(8,128)} custom-call(f32[2,2]{1,0:T(2,128)} %copy-done.9, f32[16,1,512]{2,1,0:T(1,128)} %compare_select_fusion.2.mask_ref, f32[2,2,16,8,512]{4,3,2,1,0:T(8,128)} %pad_maximum_fusion.pert_ref, f32[2,2,16,512]{3,2,1,0:T(8,128)} %squeeze.26.diag_ref, f32[2,2,16,512]{3,2,1,0:T(8,128)} %add_add_fusion.1.state_ref), custom_call_target="tpu_custom_call" | custom-call | flops 42991616 | bytes 1343488 | tf_op jit(solution)/shard_map/pallas_call | solution.py:71
  75.9 1.9 %multiply_reduce_fusion.2 = (f32[]{:T(128)}, f32[]{:T(128)}) fusion(f32[1,16,8,512]{3,2,1,0:T(8,128)S(1)} %copy-done.2, f32[1,16,8,512]{3,2,1,0:T(8,128)S(1)} %copy-done.1, f32[2,16,8,512]{3,2,1,0:T(8,128)} %shard_map.99), kind=kLoop, calls=%fused_computation.24 | loop fusion | flops 786430 | bytes 1048584 | tf_op jit(solution)/shard_map/reduce_sum | solution.py:292
  77.9 1.3 pad_maximum_fusion.6
  79.2 10.5 %all_to_all.33 = f32[32,1,2]{2,1,0:T(1,128)S(1)} all-to-all(f32[32,1,2]{2,1,0:T(1,128)S(1)} %broadcast_in_dim.32), channel_id=1, replica_groups=mesh['tile'=4,'mem'=8] {'tile','mem'}, dimensions={0} | all-to-all | bytes 512 | tf_op jit(solution)/shard_map/all_to_all | solution.py:88
  89.7 0.6 fusion.22
  91.6 1.8 %multiply_reduce_fusion = f32[]{:T(128)} fusion(f32[]{:T(128)S(6)} %div.25, f32[1,16,8,512]{3,2,1,0:T(8,128)S(1)} %copy-done.2, f32[1,16,8,512]{3,2,1,0:T(8,128)S(1)} %copy-done.1, f32[2,16,8,512]{3,2,1,0:T(8,128)} %shard_map.99), kind=kLoop, calls=%fused_computation.21 | loop fusion | flops 786431 | bytes 1048584 | tf_op jit(solution)/shard_map/reduce_sum | solution.py:302
  93.4 0.6 broadcast_in_dim.33
  94.0 8.8 %all_to_all.34 = f32[32,1,1]{2,1,0:T(1,128)S(1)} all-to-all(f32[32,1,1]{2,1,0:T(1,128)S(1)} %broadcast_in_dim.33), channel_id=1, replica_groups=mesh['tile'=4,'mem'=8] {'tile','mem'}, dimensions={0} | all-to-all | bytes 256 | tf_op jit(solution)/shard_map/all_to_all | solution.py:88
  102.8 0.7 reduce_sum.67
  104.9 0.9 multiply_add_fusion.1.field_ref
  105.8 5.6 %shard_map.100 = f32[2,2,16,512]{3,2,1,0:T(8,128)} custom-call(f32[2,2]{1,0:T(2,128)} %copy-done.9, f32[16,1,512]{2,1,0:T(1,128)} %compare_select_fusion.2.mask_ref, f32[2,2,16,8,512]{4,3,2,1,0:T(8,128)} %pad_maximum_fusion.pert_ref, f32[2,16,8,512]{3,2,1,0:T(8,128)} %multiply_add_fusion.1.field_ref), custom_call_target="tpu_custom_call" | custom-call | flops 51380224 | bytes 1605632 | tf_op jit(solution)/shard_map/pallas_call | solution.py:71
  111.4 0.6 collective-permute-start.7
  112.0 1.4 collective-permute-start.8
  113.4 3.4 %collective-permute-done.6 = f32[2,2,16,512]{3,2,1,0:T(8,128)S(1)} collective-permute-done((f32[2,2,16,512]{3,2,1,0:T(8,128)}, f32[2,2,16,512]{3,2,1,0:T(8,128)S(1)}, u32[]{:S(2)}, u32[]{:S(2)}) %collective-permute-start.6) | collective-permute-done | bytes 131104 | tf_op jit(solution)/shard_map/ppermute | solution.py:144
  116.8 1.1 collective-permute-done.7
  117.9 0.5 collective-permute-done.8
  118.4 1.6 add_add_fusion.state_ref
  120.0 5.4 %shard_map.101 = f32[2,16,8,512]{3,2,1,0:T(8,128)} custom-call(f32[2,2]{1,0:T(2,128)} %copy-done.9, f32[16,1,512]{2,1,0:T(1,128)} %compare_select_fusion.2.mask_ref, f32[2,2,16,8,512]{4,3,2,1,0:T(8,128)} %pad_maximum_fusion.pert_ref, f32[2,2,16,512]{3,2,1,0:T(8,128)} %squeeze.26.diag_ref, f32[2,2,16,512]{3,2,1,0:T(8,128)} %add_add_fusion.state_ref), custom_call_target="tpu_custom_call" | custom-call | flops 42991616 | bytes 1343488 | tf_op jit(solution)/shard_map/pallas_call | solution.py:71
  125.4 1.8 %fusion.11 = f32[]{:T(128)} fusion(f32[2,16,8,512]{3,2,1,0:T(8,128)} %shard_map.101, f32[]{:T(128)S(6)} %div.26, f32[2,16,8,512]{3,2,1,0:T(8,128)S(1)} %copy-done, f32[]{:T(128)S(6)} %div.25, f32[1,16,8,512]{3,2,1,0:T(8,128)S(1)} %copy-done.2, f32[1,16,8,512]{3,2,1,0:T(8,128)S(1)} %copy-done.1), kind=kLoop, calls=%fused_computation.13 | loop fusion | flops 1179647 | bytes 1572876 | tf_op jit(solution)/shard_map/reduce_sum | solution.py:295
  127.2 0.7 broadcast_in_dim.34
  127.8 9.1 %all_to_all.35 = f32[32,1,1]{2,1,0:T(1,128)S(1)} all-to-all(f32[32,1,1]{2,1,0:T(1,128)S(1)} %broadcast_in_dim.34), channel_id=1, replica_groups=mesh['tile'=4,'mem'=8] {'tile','mem'}, dimensions={0} | all-to-all | bytes 256 | tf_op jit(solution)/shard_map/all_to_all | solution.py:88
  137.0 0.6 reduce_sum.69
  139.1 1.1 copy.137
  140.3 2.6 %all-to-all-start.5 = ((f32[32,2,4,1,512]{4,2,1,3,0:T(4,128)}), f32[32,2,4,1,512]{4,2,1,3,0:T(4,128)S(1)}, u32[]{:S(2)}, u32[]{:S(2)}) async-start(f32[32,2,4,1,512]{4,2,1,3,0:T(4,128)} %copy.137), calls=%async_computation.5 | async-start | bytes 1048576 | tf_op jit(solution)/shard_map/all_to_all | solution.py:251
  142.9 1.5 multiply_add_fusion.2
  144.4 14.8 %all-to-all-done.5 = f32[32,2,4,1,512]{4,2,1,3,0:T(4,128)S(1)} async-done(((f32[32,2,4,1,512]{4,2,1,3,0:T(4,128)}), f32[32,2,4,1,512]{4,2,1,3,0:T(4,128)S(1)}, u32[]{:S(2)}, u32[]{:S(2)}) %all-to-all-start.5) | async-done | bytes 524320 | tf_op jit(solution)/shard_map/all_to_all | solution.py:251
  159.2 0.3 copy.154
  159.5 0.3 copy.139
  159.9 1.0 copy.140
  (69 shorter events, 2.3 us)
Async XLA Ops:
  0.6 2.3 %copy-start.10 = (f32[1,4096]{1,0:T(1,128)S(1)}, f32[1,4096]{1,0:T(1,128)}, u32[]{:S(2)}) copy-start(f32[1,4096]{1,0:T(1,128)} %param.13) | copy-start | bytes 49156
  0.6 2.3 %copy-start.8 = (f32[1,4096]{1,0:T(1,128)S(1)}, f32[1,4096]{1,0:T(1,128)}, u32[]{:S(2)}) copy-start(f32[1,4096]{1,0:T(1,128)} %param.14) | copy-start | bytes 49156
  2.7 2.9 %copy-start.13 = (s32[4]{0:T(128)S(1)}, s32[4]{0:T(128)}, u32[]{:S(2)}) copy-start(s32[4]{0:T(128)} %param.16) | copy-start | bytes 52
  2.7 3.6 %copy-start.14 = (s32[4]{0:T(128)S(1)}, s32[4]{0:T(128)}, u32[]{:S(2)}) copy-start(s32[4]{0:T(128)} %param.17) | copy-start | bytes 52
  2.9 7.4 %copy-start.7 = (bf16[4,2,4,16,512]{4,3,2,1,0:T(8,128)(2,1)S(1)}, bf16[4,2,4,16,512]{4,3,2,1,0:T(8,128)(2,1)}, u32[]{:S(2)}) copy-start(bf16[4,2,4,16,512]{4,3,2,1,0:T(8,128)(2,1)} %param.12) | copy-start | bytes 1572868
  7.1 13.4 %collective-permute-start = (f32[9,4,512]{2,1,0:T(4,128)S(1)}, f32[9,4,512]{2,1,0:T(4,128)S(1)}, u32[]{:S(2)}, u32[]{:S(2)}) collective-permute-start(f32[9,4,512]{2,1,0:T(4,128)S(1)} %pad_maximum_fusion.3), channel_id=1, source_target_pairs={{0,24},{8,0},{16,8},{24,16},{1,25},{9,1},{17,9},{25,17},{2,26},{10... | collective-permute-start | bytes 221192 | tf_op jit(solution)/shard_map/ppermute | solution.py:120
  9.5 11.0 %collective-permute-start.1 = (f32[9,4,512]{2,1,0:T(4,128)S(1)}, f32[9,4,512]{2,1,0:T(4,128)S(1)}, u32[]{:S(2)}, u32[]{:S(2)}) collective-permute-start(f32[9,4,512]{2,1,0:T(4,128)S(1)} %pad_maximum_fusion.3), channel_id=1, source_target_pairs={{0,16},{8,24},{16,0},{24,8},{1,17},{9,25},{17,1},{25,9},{2,18},{10... | collective-permute-start | bytes 221192 | tf_op jit(solution)/shard_map/ppermute | solution.py:120
  10.2 10.4 %collective-permute-start.2 = (f32[9,4,512]{2,1,0:T(4,128)S(1)}, f32[9,4,512]{2,1,0:T(4,128)S(1)}, u32[]{:S(2)}, u32[]{:S(2)}) collective-permute-start(f32[9,4,512]{2,1,0:T(4,128)S(1)} %pad_maximum_fusion.3), channel_id=1, source_target_pairs={{0,8},{8,16},{16,24},{24,0},{1,9},{9,17},{17,25},{25,1},{2,10},{10... | collective-permute-start | bytes 221192 | tf_op jit(solution)/shard_map/ppermute | solution.py:120
  11.4 7.2 %copy-start.11 = (f32[16]{0:T(128)S(1)}, f32[16]{0:T(128)}, u32[]{:S(2)}) copy-start(f32[16]{0:T(128)} %param.19) | copy-start | bytes 196
  11.4 7.2 %copy-start.12 = (f32[16]{0:T(128)S(1)}, f32[16]{0:T(128)}, u32[]{:S(2)}) copy-start(f32[16]{0:T(128)} %param.18) | copy-start | bytes 196
  12.6 22.3 %all-to-all-start = ((f32[32,2,1,4,1,512]{5,3,2,1,4,0:T(4,128)}), f32[32,2,1,4,1,512]{5,3,2,1,4,0:T(4,128)S(1)}, u32[]{:S(2)}, u32[]{:S(2)}) async-start(f32[32,2,1,4,1,512]{5,3,2,1,4,0:T(4,128)} %copy.127), calls=%async_computation | async-start | bytes 1048576 | tf_op jit(solution)/shard_map/all_to_all | solution.py:182
  18.7 19.1 %copy-start.9 = (f32[2,2]{1,0:T(2,128)}, f32[2,2]{1,0:T(2,128)S(1)}, u32[]{:S(2)}) copy-start(f32[2,2]{1,0:T(2,128)S(1)} %pad_maximum_fusion.5.rates_ref) | copy-start | bytes 52
  34.9 19.0 %all-to-all-start.1 = ((f32[32,2,1,4,1,512]{5,3,2,1,4,0:T(4,128)}), f32[32,2,1,4,1,512]{5,3,2,1,4,0:T(4,128)S(1)}, u32[]{:S(2)}, u32[]{:S(2)}) async-start(f32[32,2,1,4,1,512]{5,3,2,1,4,0:T(4,128)} %copy.130), calls=%async_computation.1 | async-start | bytes 1048576 | tf_op jit(solution)/shard_map/all_to_all | solution.py:182
  49.0 13.2 %copy-start.5 = (f32[2,1,16,512]{3,2,1,0:T(8,128)S(1)}, f32[2,1,16,512]{3,2,1,0:T(8,128)}, u32[]{:S(2)}) copy-start(f32[2,1,16,512]{3,2,1,0:T(8,128)} %shard_map.97) | copy-start | bytes 196612
  49.0 16.2 %copy-start.3 = (f32[2,1,4,4,8,1,512]{6,4,3,2,0,5,1:T(8,128)S(1)}, f32[2,1,4,4,8,1,512]{6,4,3,2,0,5,1:T(8,128)}, u32[]{:S(2)}) copy-start(f32[2,1,4,4,8,1,512]{6,4,3,2,0,5,1:T(8,128)} %copy.129) | copy-start | bytes 1572868
  55.1 10.1 %copy-start.4 = (f32[2,1,4,4,8,1,512]{6,4,3,2,0,5,1:T(8,128)S(1)}, f32[2,1,4,4,8,1,512]{6,4,3,2,0,5,1:T(8,128)}, u32[]{:S(2)}) copy-start(f32[2,1,4,4,8,1,512]{6,4,3,2,0,5,1:T(8,128)} %copy.132) | copy-start | bytes 1572868
  62.1 7.7 %copy-start.6 = (f32[2,1,16,512]{3,2,1,0:T(8,128)S(1)}, f32[2,1,16,512]{3,2,1,0:T(8,128)}, u32[]{:S(2)}) copy-start(f32[2,1,16,512]{3,2,1,0:T(8,128)} %shard_map.98) | copy-start | bytes 196612
  63.1 12.9 %copy-start.1 = (f32[1,16,8,512]{3,2,1,0:T(8,128)S(1)}, f32[1,16,8,512]{3,2,1,0:T(8,128)}, u32[]{:S(2)}) copy-start(f32[1,16,8,512]{3,2,1,0:T(8,128)} %shard_map.95.field_ref) | copy-start | bytes 786436
  63.1 12.9 %copy-start.2 = (f32[1,16,8,512]{3,2,1,0:T(8,128)S(1)}, f32[1,16,8,512]{3,2,1,0:T(8,128)}, u32[]{:S(2)}) copy-start(f32[1,16,8,512]{3,2,1,0:T(8,128)} %shard_map.96.field_ref) | copy-start | bytes 786436
  63.1 5.2 %collective-permute-start.3 = (f32[2,2,16,512]{3,2,1,0:T(8,128)S(1)}, f32[2,2,16,512]{3,2,1,0:T(8,128)S(1)}, u32[]{:S(2)}, u32[]{:S(2)}) collective-permute-start(f32[2,2,16,512]{3,2,1,0:T(8,128)S(1)} %pad_maximum_fusion.2), channel_id=1, source_target_pairs={{0,8},{8,16},{16,24},{24,0},{1,9},{9,17},{17,25},{25,1},{2,10},{10... | collective-permute-start | bytes 393224 | tf_op jit(solution)/shard_map/ppermute | solution.py:144
  63.2 6.4 %collective-permute-start.4 = (f32[2,2,16,512]{3,2,1,0:T(8,128)S(1)}, f32[2,2,16,512]{3,2,1,0:T(8,128)S(1)}, u32[]{:S(2)}, u32[]{:S(2)}) collective-permute-start(f32[2,2,16,512]{3,2,1,0:T(8,128)S(1)} %pad_maximum_fusion.2), channel_id=1, source_target_pairs={{0,16},{8,24},{16,0},{24,8},{1,17},{9,25},{17,1},{25,9},{2,18},{10... | collective-permute-start | bytes 393224 | tf_op jit(solution)/shard_map/ppermute | solution.py:144
  64.0 5.8 %collective-permute-start.5 = (f32[2,2,16,512]{3,2,1,0:T(8,128)S(1)}, f32[2,2,16,512]{3,2,1,0:T(8,128)S(1)}, u32[]{:S(2)}, u32[]{:S(2)}) collective-permute-start(f32[2,2,16,512]{3,2,1,0:T(8,128)S(1)} %pad_maximum_fusion.2), channel_id=1, source_target_pairs={{0,24},{8,0},{16,8},{24,16},{1,25},{9,1},{17,9},{25,17},{2,26},{10... | collective-permute-start | bytes 393224 | tf_op jit(solution)/shard_map/ppermute | solution.py:144
  75.9 28.9 %copy-start = (f32[2,16,8,512]{3,2,1,0:T(8,128)S(1)}, f32[2,16,8,512]{3,2,1,0:T(8,128)}, u32[]{:S(2)}) copy-start(f32[2,16,8,512]{3,2,1,0:T(8,128)} %shard_map.99) | copy-start | bytes 1572868
  111.4 5.5 %collective-permute-start.6 = (f32[2,2,16,512]{3,2,1,0:T(8,128)}, f32[2,2,16,512]{3,2,1,0:T(8,128)S(1)}, u32[]{:S(2)}, u32[]{:S(2)}) collective-permute-start(f32[2,2,16,512]{3,2,1,0:T(8,128)} %shard_map.100), channel_id=1, source_target_pairs={{0,8},{8,16},{16,24},{24,0},{1,9},{9,17},{17,25},{25,1},{2,10},{10... | collective-permute-start | bytes 393224 | tf_op jit(solution)/shard_map/ppermute | solution.py:144
  111.4 6.6 %collective-permute-start.7 = (f32[2,2,16,512]{3,2,1,0:T(8,128)}, f32[2,2,16,512]{3,2,1,0:T(8,128)S(1)}, u32[]{:S(2)}, u32[]{:S(2)}) collective-permute-start(f32[2,2,16,512]{3,2,1,0:T(8,128)} %shard_map.100), channel_id=1, source_target_pairs={{0,16},{8,24},{16,0},{24,8},{1,17},{9,25},{17,1},{25,9},{2,18},{10... | collective-permute-start | bytes 393224 | tf_op jit(solution)/shard_map/ppermute | solution.py:144
  112.0 6.4 %collective-permute-start.8 = (f32[2,2,16,512]{3,2,1,0:T(8,128)}, f32[2,2,16,512]{3,2,1,0:T(8,128)S(1)}, u32[]{:S(2)}, u32[]{:S(2)}) collective-permute-start(f32[2,2,16,512]{3,2,1,0:T(8,128)} %shard_map.100), channel_id=1, source_target_pairs={{0,24},{8,0},{16,8},{24,16},{1,25},{9,1},{17,9},{25,17},{2,26},{10... | collective-permute-start | bytes 393224 | tf_op jit(solution)/shard_map/ppermute | solution.py:144
  140.3 19.0 %all-to-all-start.5 = ((f32[32,2,4,1,512]{4,2,1,3,0:T(4,128)}), f32[32,2,4,1,512]{4,2,1,3,0:T(4,128)S(1)}, u32[]{:S(2)}, u32[]{:S(2)}) async-start(f32[32,2,4,1,512]{4,2,1,3,0:T(4,128)} %copy.137), calls=%async_computation.5 | async-start | bytes 1048576 | tf_op jit(solution)/shard_map/all_to_all | solution.py:251

commit v4 on v2

--- a/solution.py
+++ b/solution.py
@@ -45,13 +45,17 @@
     return now
 
 
-def adjoint_kernel(rates_ref, mask_ref, pert_ref, diag_ref, state_ref, out_ref):
+def adjoint_kernel(rates_ref, mask_ref, pert_ref, diag_ref, *refs):
+    pieces, out_ref = refs[:-1], refs[-1]
     slots, levels = pert_ref.shape[:2]
     mask = mask_ref[...]
     for level in range(levels):
         field = None
         for slot in range(slots):
-            grad = diag_ref[slot, level] * state_ref[slot, level]
+            state = pieces[0][slot, level]
+            for piece in pieces[1:]:
+                state = state + piece[slot, level]
+            grad = diag_ref[slot, level] * state
             term = pert_ref[slot, level] * grad[:, None, :]
             field = term if field is None else field + term
         out_ref[level] = smooth_level(rates_ref, mask, field, level)
@@ -137,12 +141,12 @@
     return total
 
 
-def sum_over_tile_by_permutes(block):
-    count = lax.axis_size("tile")
-    total = block
-    for k in range(1, count):
-        total = total + lax.ppermute(block, "tile", [(i, (i + k) % count) for i in range(count)])
-    return total
+def pieces_over_tile(block):
+    count = lax.axis_size("tile")
+    return [block] + [
+        lax.ppermute(block, "tile", [(i, (i + k) % count) for i in range(count)])
+        for k in range(1, count)
+    ]
 
 
 def reduce_rows(block, dim):
@@ -203,12 +207,10 @@
             pert,
             control,
         )
-        return sum_over_tile_by_permutes(partial)
-
-    def adjoint(diag, state):
-        return local_call(
-            adjoint_kernel, pert.shape[1:], rates, mask, pert, diag, state
-        )
+        return pieces_over_tile(partial)
+
+    def adjoint(diag, pieces):
+        return local_call(adjoint_kernel, pert.shape[1:], rates, mask, pert, diag, *pieces)
 
     def to_output(control):
         if share and local_members % tiles == 0:
@@ -248,7 +250,7 @@
     first_grad, obs_diag = both[0], both[1]
     me = lax.axis_index("tile")
 
-    residual = adjoint(first_grad, jnp.ones_like(first_grad))
+    residual = adjoint(first_grad, [jnp.ones_like(first_grad)])
     direction = residual
     control = jnp.zeros_like(residual)
     increment = jnp.zeros(state_shape, jnp.float32)
@@ -263,7 +265,10 @@
             curvature = global_sum(jnp.sum(direction * image))
         alpha = norm_now / curvature
         control = control + alpha * direction
-        own_state = lax.dynamic_slice_in_dim(state, me * lat_rows, lat_rows, axis=2)
+        own_state = None
+        for piece in state:
+            own = lax.dynamic_slice_in_dim(piece, me * lat_rows, lat_rows, axis=2)
+            own_state = own if own_state is None else own_state + own
         increment = increment + alpha * own_state
         if step + 1 < ITERS:
             residual = residual - alpha * image

time: 159 us -> 161 us (1.013)
  waiting for transfers between devices: 48.8 us -> 53.4 us
  local copies, waits for them, and re-layouts: 11.8 us -> 13.9 us
  other arithmetic: 18 us -> 16.1 us
    ppermute x6, waiting for transfers between devices: 9.25 us -> 14 us  [pieces_over_tile(): lax.ppermute(block, 'tile', [(i, (i + k) % count) for i in range(count)])]
    add x2 -> x0, other arithmetic: 3.18 us -> none  [sum_over_tile_by_permutes(): total + lax.ppermute(block, 'tile', [(i, (i + k) % count) for i in range(...]
    unnamed x25 -> x33, local copies, waits for them, and re-layouts: 1.16 us -> 3.36 us
where the time goes in v4:
time: 161 us
  waiting for transfers between devices  53.4 us (33%)
  Pallas kernels  27.8 us (17%)
  blocking collectives  27.3 us (17%)
  other arithmetic  16.1 us (10%)
  starting transfers between devices  14.7 us (9%)
  local copies, waits for them, and re-layouts  13.9 us (9%)
  between operations  4.87 us (3%)
  matrix products  2.47 us (2%)
    pallas_call x5, Pallas kernels, local_call(): pl.pallas_call(kernel, out_shape=jax.ShapeDtypeStruct(out_shape, jnp.floa...  27.8 us
    all_to_all x3, blocking collectives, global_sum(): return jnp.sum(lax.all_to_all(spread, axes, 0, 0, tiled=True), axis=0)  27.3 us
    all_to_all x1, waiting for transfers between devices, body(): got = lax.all_to_all(sent, ('tile', 'mem'), 0, 0, tiled=True)  24.8 us
    all_to_all x1, waiting for transfers between devices, to_output(): got = lax.all_to_all(sent, ('tile', 'mem'), 0, 0, tiled=True)  14.6 us
    ppermute x6, waiting for transfers between devices, pieces_over_tile(): lax.ppermute(block, 'tile', [(i, (i + k) % count) for i in range(count)])  14 us
    all_to_all x1, starting transfers between devices, body(): got = lax.all_to_all(sent, ('tile', 'mem'), 0, 0, tiled=True)  5.78 us
    ppermute x3, starting transfers between devices, gather_rows_by_permutes(): lax.ppermute(block, 'tile', [(i, (i + k) % count) for i in range(count)])  3.51 us
    unnamed x33, local copies, waits for them, and re-layouts  3.36 us
  transfers between devices with their start and end apart: 11, of which 8 were waited for; matrix products, arithmetic and copies ran while one was open for 5% of the time, Pallas kernels for 0%

profile of v4, /device:TPU:0, one launch (start us, length us, event | category | flops | bytes accessed | tf_op | source)
XLA Modules:
  0.0 160.6 jit_solution(12407866155935346399)
XLA Ops:
  0.6 0.6 compare_reduce_fusion.1
  1.3 0.6 compare_reduce_fusion
  1.9 0.7 add_select_fusion.1
  2.7 1.3 fusion.16
  4.0 1.3 fusion.17
  5.3 0.1 copy.106
  5.4 0.2 fusion.5
  5.8 2.5 %fusion.6 = f32[64,128,2]{1,0,2:T(8,128)S(1)} fusion(f32[4096,128]{0,1:T(8,128)S(1)} %fusion.5, f32[4096,2]{0,1:T(2,128)S(1)} %pad_maximum_fusion.1, s32[4096]{0:T(1024)S(1)} %get-tuple-element.41), kind=kOutput, calls=%fused_computation.7 | convolution fusion | flops 806617088 | bytes 2211840 | tf_op jit(solution)/shard_map/dot_general | solution.py:101
  8.3 3.0 %collective-permute-start.1 = (f32[9,4,512]{2,1,0:T(4,128)S(1)}, f32[9,4,512]{2,1,0:T(4,128)S(1)}, u32[]{:S(2)}, u32[]{:S(2)}) collective-permute-start(f32[9,4,512]{2,1,0:T(4,128)S(1)} %pad_maximum_fusion), channel_id=1, source_target_pairs={{0,16},{8,24},{16,0},{24,8},{1,17},{9,25},{17,1},{25,9},{2,18},{10... | collective-permute-start | bytes 221192 | tf_op jit(solution)/shard_map/ppermute | solution.py:124
  11.3 0.5 collective-permute-start.2
  11.9 0.4 copy.114
  12.3 0.6 copy.139
  12.9 1.7 %copy.116 = f32[32,2,2,4,1,512]{5,3,2,1,4,0:T(4,128)} copy(f32[32,2,2,4,1,512]{5,0,3,2,1,4:T(8,128)S(1)} %bitcast.95) | data formatting | bytes 2097152 | tf_op jit(solution)/shard_map/reshape | solution.py:181
  14.6 5.8 %all-to-all-start = ((f32[32,2,2,4,1,512]{5,3,2,1,4,0:T(4,128)}), f32[32,2,2,4,1,512]{5,3,2,1,4,0:T(4,128)S(1)}, u32[]{:S(2)}, u32[]{:S(2)}) async-start(f32[32,2,2,4,1,512]{5,3,2,1,4,0:T(4,128)} %copy.116), calls=%async_computation | async-start | bytes 2097152 | tf_op jit(solution)/shard_map/all_to_all | solution.py:184
  20.4 0.1 dynamic-slice_bitcast_fusion
  20.5 0.5 pad_maximum_fusion.2.rates_ref
  21.3 0.1 reshape.296
  21.4 0.1 copy.133
  21.5 0.7 squeeze.25.diag_ref
  22.2 0.8 compare_select_fusion.2.mask_ref
  23.0 24.8 %all-to-all-done = f32[32,2,2,4,1,512]{5,3,2,1,4,0:T(4,128)S(1)} async-done(((f32[32,2,2,4,1,512]{5,3,2,1,4,0:T(4,128)}), f32[32,2,2,4,1,512]{5,3,2,1,4,0:T(4,128)S(1)}, u32[]{:S(2)}, u32[]{:S(2)}) %all-to-all-start) | async-done | bytes 1048608 | tf_op jit(solution)/shard_map/all_to_all | solution.py:184
  47.8 0.6 copy.138
  48.4 1.1 copy.118
  49.4 0.7 broadcast_in_dim.35.refs_0_
  50.1 5.4 %shard_map.95.field_ref = f32[2,16,8,512]{3,2,1,0:T(8,128)} custom-call(f32[2,2]{1,0:T(2,128)} %pad_maximum_fusion.2.rates_ref, f32[16,1,512]{2,1,0:T(1,128)} %compare_select_fusion.2.mask_ref, f32[2,2,16,8,512]{4,3,2,1,0:T(8,128)} %bitcast.90, f32[2,2,16,512]{3,2,1,0:T(8,128)} %squeeze.25.diag_ref, f32[2,2,16,512]{3,2,1,0:T(8,128)} %broadcast_in_dim.35.refs_0_), custom_call_target="tpu_custom_call" | custom-call | flops 42991616 | bytes 1343488 | tf_op jit(solution)/shard_map/pallas_call | solution.py:75
  55.5 5.6 %shard_map.96.refs_0_ = f32[2,2,16,512]{3,2,1,0:T(8,128)} custom-call(f32[2,2]{1,0:T(2,128)} %pad_maximum_fusion.2.rates_ref, f32[16,1,512]{2,1,0:T(1,128)} %compare_select_fusion.2.mask_ref, f32[2,2,16,8,512]{4,3,2,1,0:T(8,128)} %bitcast.91, f32[2,16,8,512]{3,2,1,0:T(8,128)} %shard_map.95.field_ref), custom_call_target="tpu_custom_call" | custom-call | flops 51380224 | bytes 1605632 | tf_op jit(solution)/shard_map/pallas_call | solution.py:75
  61.2 0.5 collective-permute-start.5
  61.6 0.8 collective-permute-start.4
  62.5 0.7 squeeze.26.diag_ref
  63.2 2.6 %collective-permute-done.5.refs_3_ = f32[2,2,16,512]{3,2,1,0:T(8,128)S(1)} collective-permute-done((f32[2,2,16,512]{3,2,1,0:T(8,128)}, f32[2,2,16,512]{3,2,1,0:T(8,128)S(1)}, u32[]{:S(2)}, u32[]{:S(2)}) %collective-permute-start.5) | collective-permute-done | bytes 131104 | tf_op jit(solution)/shard_map/ppermute | solution.py:147
  65.7 3.8 %collective-permute-done.4.refs_2_ = f32[2,2,16,512]{3,2,1,0:T(8,128)S(1)} collective-permute-done((f32[2,2,16,512]{3,2,1,0:T(8,128)}, f32[2,2,16,512]{3,2,1,0:T(8,128)S(1)}, u32[]{:S(2)}, u32[]{:S(2)}) %collective-permute-start.4) | collective-permute-done | bytes 131104 | tf_op jit(solution)/shard_map/ppermute | solution.py:147
  69.6 0.3 collective-permute-done.3.refs_1_
  69.8 0.4 copy-done.4
  70.2 0.6 copy-done.5
  70.9 5.5 %shard_map.97 = f32[2,16,8,512]{3,2,1,0:T(8,128)} custom-call(f32[2,2]{1,0:T(2,128)} %pad_maximum_fusion.2.rates_ref, f32[16,1,512]{2,1,0:T(1,128)} %compare_select_fusion.2.mask_ref, f32[2,2,16,8,512]{4,3,2,1,0:T(8,128)} %bitcast.92, f32[2,2,16,512]{3,2,1,0:T(8,128)} %squeeze.26.diag_ref, f32[2,2,16,512]{3,2,1,0:T(8,128)} %shard_map.96.refs_0_, ...), custom_call_target="tpu_custom_call" | custom-call | flops 55574528 | bytes 1736704 | tf_op jit(solution)/shard_map/pallas_call | solution.py:75
  76.4 1.8 %multiply_reduce_fusion.2 = (f32[]{:T(128)}, f32[]{:T(128)}, f32[2,16,8,512]{3,2,1,0:T(8,128)S(1)}) fusion(f32[2,16,8,512]{3,2,1,0:T(8,128)S(1)} %copy-done, f32[2,16,8,512]{3,2,1,0:T(8,128)} %shard_map.97), kind=kLoop, calls=%fused_computation.21 | loop fusion | flops 655358 | bytes 1572872 | tf_op jit(solution)/shard_map/reduce_sum | solution.py:262
  78.2 1.4 pad_maximum_fusion.3
  79.6 9.7 %all_to_all.28 = f32[32,1,2]{2,1,0:T(1,128)S(1)} all-to-all(f32[32,1,2]{2,1,0:T(1,128)S(1)} %broadcast_in_dim.36), channel_id=1, replica_groups=mesh['tile'=4,'mem'=8] {'tile','mem'}, dimensions={0} | all-to-all | bytes 512 | tf_op jit(solution)/shard_map/all_to_all | solution.py:92
  89.4 0.6 fusion.18
  91.3 0.8 multiply_reduce_fusion
  92.1 0.7 broadcast_in_dim.37
  92.7 8.8 %all_to_all.29 = f32[32,1,1]{2,1,0:T(1,128)S(1)} all-to-all(f32[32,1,1]{2,1,0:T(1,128)S(1)} %broadcast_in_dim.37), channel_id=1, replica_groups=mesh['tile'=4,'mem'=8] {'tile','mem'}, dimensions={0} | all-to-all | bytes 256 | tf_op jit(solution)/shard_map/all_to_all | solution.py:92
  101.5 0.6 reduce_sum.67
  103.5 0.9 multiply_add_fusion.1.field_ref
  104.4 5.6 %shard_map.98.refs_0_ = f32[2,2,16,512]{3,2,1,0:T(8,128)} custom-call(f32[2,2]{1,0:T(2,128)} %pad_maximum_fusion.2.rates_ref, f32[16,1,512]{2,1,0:T(1,128)} %compare_select_fusion.2.mask_ref, f32[2,2,16,8,512]{4,3,2,1,0:T(8,128)} %bitcast.93, f32[2,16,8,512]{3,2,1,0:T(8,128)} %multiply_add_fusion.1.field_ref), custom_call_target="tpu_custom_call" | custom-call | flops 51380224 | bytes 1605632 | tf_op jit(solution)/shard_map/pallas_call | solution.py:75
  110.0 1.5 collective-permute-start.7
  111.5 2.6 %collective-permute-done.8.refs_3_ = f32[2,2,16,512]{3,2,1,0:T(8,128)S(1)} collective-permute-done((f32[2,2,16,512]{3,2,1,0:T(8,128)}, f32[2,2,16,512]{3,2,1,0:T(8,128)S(1)}, u32[]{:S(2)}, u32[]{:S(2)}) %collective-permute-start.8) | collective-permute-done | bytes 131104 | tf_op jit(solution)/shard_map/ppermute | solution.py:147
  114.1 4.7 %collective-permute-done.7.refs_2_ = f32[2,2,16,512]{3,2,1,0:T(8,128)S(1)} collective-permute-done((f32[2,2,16,512]{3,2,1,0:T(8,128)}, f32[2,2,16,512]{3,2,1,0:T(8,128)S(1)}, u32[]{:S(2)}, u32[]{:S(2)}) %collective-permute-start.7) | collective-permute-done | bytes 131104 | tf_op jit(solution)/shard_map/ppermute | solution.py:147
  118.7 0.1 collective-permute-done.6.refs_1_
  118.8 0.5 copy-done.7
  119.4 0.6 copy-done.8
  120.0 5.5 %shard_map.99 = f32[2,16,8,512]{3,2,1,0:T(8,128)} custom-call(f32[2,2]{1,0:T(2,128)} %pad_maximum_fusion.2.rates_ref, f32[16,1,512]{2,1,0:T(1,128)} %compare_select_fusion.2.mask_ref, f32[2,2,16,8,512]{4,3,2,1,0:T(8,128)} %bitcast.94, f32[2,2,16,512]{3,2,1,0:T(8,128)} %squeeze.26.diag_ref, f32[2,2,16,512]{3,2,1,0:T(8,128)} %shard_map.98.refs_0_, ...), custom_call_target="tpu_custom_call" | custom-call | flops 55574528 | bytes 1736704 | tf_op jit(solution)/shard_map/pallas_call | solution.py:75
  125.6 1.8 %fusion.11 = f32[]{:T(128)} fusion(f32[2,16,8,512]{3,2,1,0:T(8,128)S(1)} %copy-done.1, f32[2,16,8,512]{3,2,1,0:T(8,128)} %shard_map.99), kind=kLoop, calls=%fused_computation.13 | loop fusion | flops 393215 | bytes 1048580 | tf_op jit(solution)/shard_map/reduce_sum | solution.py:265
  127.3 0.7 broadcast_in_dim.38
  128.0 8.8 %all_to_all.30 = f32[32,1,1]{2,1,0:T(1,128)S(1)} all-to-all(f32[32,1,1]{2,1,0:T(1,128)S(1)} %broadcast_in_dim.38), channel_id=1, replica_groups=mesh['tile'=4,'mem'=8] {'tile','mem'}, dimensions={0} | all-to-all | bytes 256 | tf_op jit(solution)/shard_map/all_to_all | solution.py:92
  136.8 0.6 reduce_sum.69
  138.8 0.1 multiply_add_fusion
  138.9 1.1 copy.123
  140.0 2.6 %all-to-all-start.4 = ((f32[32,2,4,1,512]{4,2,1,3,0:T(4,128)}), f32[32,2,4,1,512]{4,2,1,3,0:T(4,128)S(1)}, u32[]{:S(2)}, u32[]{:S(2)}) async-start(f32[32,2,4,1,512]{4,2,1,3,0:T(4,128)} %copy.123), calls=%async_computation.4 | async-start | bytes 1048576 | tf_op jit(solution)/shard_map/all_to_all | solution.py:221
  142.7 1.7 %multiply_add_fusion.2 = f32[2,2,4,512]{3,2,1,0:T(4,128)} fusion(f32[2,2,16,512]{3,2,1,0:T(8,128)} %copy-done.6, s32[]{:T(128)S(6)} %select_n.77, f32[2,2,16,512]{3,2,1,0:T(8,128)} %copy-done.7, f32[2,2,16,512]{3,2,1,0:T(8,128)} %copy-done.8, f32[2,2,16,512]{3,2,1,0:T(8,128)} %shard_map.98.refs_0_, f32[2,2,16,512]{3,2,1,0:T(8,128)} %copy-done.3, ...), kind=kLoop, calls=%fused_computation.39 | loop fusion | flops 73728 | bytes 294924 | tf_op jit(solution)/shard_map/add | solution.py:272
  144.4 14.6 %all-to-all-done.4 = f32[32,2,4,1,512]{4,2,1,3,0:T(4,128)S(1)} async-done(((f32[32,2,4,1,512]{4,2,1,3,0:T(4,128)}), f32[32,2,4,1,512]{4,2,1,3,0:T(4,128)S(1)}, u32[]{:S(2)}, u32[]{:S(2)}) %all-to-all-start.4) | async-done | bytes 524320 | tf_op jit(solution)/shard_map/all_to_all | solution.py:221
  159.0 0.3 copy.140
  159.3 0.3 copy.125
  159.7 1.0 copy.126
  (51 shorter events, 0.5 us)
Async XLA Ops:
  0.6 5.1 %copy-start.9 = (f32[1,4096]{1,0:T(1,128)S(1)}, f32[1,4096]{1,0:T(1,128)}, u32[]{:S(2)}) copy-start(f32[1,4096]{1,0:T(1,128)} %param.14) | copy-start | bytes 49156
  0.6 5.1 %copy-start.10 = (f32[1,4096]{1,0:T(1,128)S(1)}, f32[1,4096]{1,0:T(1,128)}, u32[]{:S(2)}) copy-start(f32[1,4096]{1,0:T(1,128)} %param.13) | copy-start | bytes 49156
  5.4 6.4 %copy-start.2 = (bf16[4,2,4,16,512]{4,3,2,1,0:T(8,128)(2,1)S(1)}, bf16[4,2,4,16,512]{4,3,2,1,0:T(8,128)(2,1)}, u32[]{:S(2)}) copy-start(bf16[4,2,4,16,512]{4,3,2,1,0:T(8,128)(2,1)} %param.12) | copy-start | bytes 1572868
  8.3 12.7 %collective-permute-start.1 = (f32[9,4,512]{2,1,0:T(4,128)S(1)}, f32[9,4,512]{2,1,0:T(4,128)S(1)}, u32[]{:S(2)}, u32[]{:S(2)}) collective-permute-start(f32[9,4,512]{2,1,0:T(4,128)S(1)} %pad_maximum_fusion), channel_id=1, source_target_pairs={{0,16},{8,24},{16,0},{24,8},{1,17},{9,25},{17,1},{25,9},{2,18},{10... | collective-permute-start | bytes 221192 | tf_op jit(solution)/shard_map/ppermute | solution.py:124
  11.3 9.7 %collective-permute-start = (f32[9,4,512]{2,1,0:T(4,128)S(1)}, f32[9,4,512]{2,1,0:T(4,128)S(1)}, u32[]{:S(2)}, u32[]{:S(2)}) collective-permute-start(f32[9,4,512]{2,1,0:T(4,128)S(1)} %pad_maximum_fusion), channel_id=1, source_target_pairs={{0,24},{8,0},{16,8},{24,16},{1,25},{9,1},{17,9},{25,17},{2,26},{10... | collective-permute-start | bytes 221192 | tf_op jit(solution)/shard_map/ppermute | solution.py:124
  11.3 9.8 %collective-permute-start.2 = (f32[9,4,512]{2,1,0:T(4,128)S(1)}, f32[9,4,512]{2,1,0:T(4,128)S(1)}, u32[]{:S(2)}, u32[]{:S(2)}) collective-permute-start(f32[9,4,512]{2,1,0:T(4,128)S(1)} %pad_maximum_fusion), channel_id=1, source_target_pairs={{0,8},{8,16},{16,24},{24,0},{1,9},{9,17},{17,25},{25,1},{2,10},{10... | collective-permute-start | bytes 221192 | tf_op jit(solution)/shard_map/ppermute | solution.py:124
  12.9 7.5 %copy-start.11 = (f32[16]{0:T(128)S(1)}, f32[16]{0:T(128)}, u32[]{:S(2)}) copy-start(f32[16]{0:T(128)} %param.19) | copy-start | bytes 196
  12.9 7.5 %copy-start.12 = (f32[16]{0:T(128)S(1)}, f32[16]{0:T(128)}, u32[]{:S(2)}) copy-start(f32[16]{0:T(128)} %param.18) | copy-start | bytes 196
  14.6 33.2 %all-to-all-start = ((f32[32,2,2,4,1,512]{5,3,2,1,4,0:T(4,128)}), f32[32,2,2,4,1,512]{5,3,2,1,4,0:T(4,128)S(1)}, u32[]{:S(2)}, u32[]{:S(2)}) async-start(f32[32,2,2,4,1,512]{5,3,2,1,4,0:T(4,128)} %copy.116), calls=%async_computation | async-start | bytes 2097152 | tf_op jit(solution)/shard_map/all_to_all | solution.py:184
  55.5 20.9 %copy-start = (f32[2,16,8,512]{3,2,1,0:T(8,128)S(1)}, f32[2,16,8,512]{3,2,1,0:T(8,128)}, u32[]{:S(2)}) copy-start(f32[2,16,8,512]{3,2,1,0:T(8,128)} %shard_map.95.field_ref) | copy-start | bytes 1572868
  61.2 4.6 %collective-permute-start.5 = (f32[2,2,16,512]{3,2,1,0:T(8,128)}, f32[2,2,16,512]{3,2,1,0:T(8,128)S(1)}, u32[]{:S(2)}, u32[]{:S(2)}) collective-permute-start(f32[2,2,16,512]{3,2,1,0:T(8,128)} %shard_map.96.refs_0_), channel_id=1, source_target_pairs={{0,24},{8,0},{16,8},{24,16},{1,25},{9,1},{17,9},{25,17},{2,26},{10... | collective-permute-start | bytes 393224 | tf_op jit(solution)/shard_map/ppermute | solution.py:147
  61.6 7.9 %collective-permute-start.4 = (f32[2,2,16,512]{3,2,1,0:T(8,128)}, f32[2,2,16,512]{3,2,1,0:T(8,128)S(1)}, u32[]{:S(2)}, u32[]{:S(2)}) collective-permute-start(f32[2,2,16,512]{3,2,1,0:T(8,128)} %shard_map.96.refs_0_), channel_id=1, source_target_pairs={{0,16},{8,24},{16,0},{24,8},{1,17},{9,25},{17,1},{25,9},{2,18},{10... | collective-permute-start | bytes 393224 | tf_op jit(solution)/shard_map/ppermute | solution.py:147
  62.5 7.4 %collective-permute-start.3 = (f32[2,2,16,512]{3,2,1,0:T(8,128)}, f32[2,2,16,512]{3,2,1,0:T(8,128)S(1)}, u32[]{:S(2)}, u32[]{:S(2)}) collective-permute-start(f32[2,2,16,512]{3,2,1,0:T(8,128)} %shard_map.96.refs_0_), channel_id=1, source_target_pairs={{0,8},{8,16},{16,24},{24,0},{1,9},{9,17},{17,25},{25,1},{2,10},{10... | collective-permute-start | bytes 393224 | tf_op jit(solution)/shard_map/ppermute | solution.py:147
  65.7 4.1 %copy-start.3 = (f32[2,2,16,512]{3,2,1,0:T(8,128)}, f32[2,2,16,512]{3,2,1,0:T(8,128)S(1)}, u32[]{:S(2)}) copy-start(f32[2,2,16,512]{3,2,1,0:T(8,128)S(1)} %collective-permute-done.5.refs_3_) | copy-start | bytes 393220
  69.6 0.7 copy-start.4
  70.2 0.6 copy-start.5
  104.4 21.2 %copy-start.1 = (f32[2,16,8,512]{3,2,1,0:T(8,128)S(1)}, f32[2,16,8,512]{3,2,1,0:T(8,128)}, u32[]{:S(2)}) copy-start(f32[2,16,8,512]{3,2,1,0:T(8,128)} %multiply_add_fusion.1.field_ref) | copy-start | bytes 1572868
  110.0 4.1 %collective-permute-start.8 = (f32[2,2,16,512]{3,2,1,0:T(8,128)}, f32[2,2,16,512]{3,2,1,0:T(8,128)S(1)}, u32[]{:S(2)}, u32[]{:S(2)}) collective-permute-start(f32[2,2,16,512]{3,2,1,0:T(8,128)} %shard_map.98.refs_0_), channel_id=1, source_target_pairs={{0,24},{8,0},{16,8},{24,16},{1,25},{9,1},{17,9},{25,17},{2,26},{10... | collective-permute-start | bytes 393224 | tf_op jit(solution)/shard_map/ppermute | solution.py:147
  110.0 8.7 %collective-permute-start.7 = (f32[2,2,16,512]{3,2,1,0:T(8,128)}, f32[2,2,16,512]{3,2,1,0:T(8,128)S(1)}, u32[]{:S(2)}, u32[]{:S(2)}) collective-permute-start(f32[2,2,16,512]{3,2,1,0:T(8,128)} %shard_map.98.refs_0_), channel_id=1, source_target_pairs={{0,16},{8,24},{16,0},{24,8},{1,17},{9,25},{17,1},{25,9},{2,18},{10... | collective-permute-start | bytes 393224 | tf_op jit(solution)/shard_map/ppermute | solution.py:147
  111.5 7.4 %collective-permute-start.6 = (f32[2,2,16,512]{3,2,1,0:T(8,128)}, f32[2,2,16,512]{3,2,1,0:T(8,128)S(1)}, u32[]{:S(2)}, u32[]{:S(2)}) collective-permute-start(f32[2,2,16,512]{3,2,1,0:T(8,128)} %shard_map.98.refs_0_), channel_id=1, source_target_pairs={{0,8},{8,16},{16,24},{24,0},{1,9},{9,17},{17,25},{25,1},{2,10},{10... | collective-permute-start | bytes 393224 | tf_op jit(solution)/shard_map/ppermute | solution.py:147
  114.1 4.8 %copy-start.6 = (f32[2,2,16,512]{3,2,1,0:T(8,128)}, f32[2,2,16,512]{3,2,1,0:T(8,128)S(1)}, u32[]{:S(2)}) copy-start(f32[2,2,16,512]{3,2,1,0:T(8,128)S(1)} %collective-permute-done.8.refs_3_) | copy-start | bytes 393220
  118.7 0.6 copy-start.7
  119.4 0.6 copy-start.8
  140.0 19.0 %all-to-all-start.4 = ((f32[32,2,4,1,512]{4,2,1,3,0:T(4,128)}), f32[32,2,4,1,512]{4,2,1,3,0:T(4,128)S(1)}, u32[]{:S(2)}, u32[]{:S(2)}) async-start(f32[32,2,4,1,512]{4,2,1,3,0:T(4,128)} %copy.123), calls=%async_computation.4 | async-start | bytes 1048576 | tf_op jit(solution)/shard_map/all_to_all | solution.py:221

commit v5 on v2

--- a/solution.py
+++ b/solution.py
@@ -255,15 +255,20 @@
     norm_now = None
     for step in range(ITERS):
         state = forward(direction)
-        image = direction + adjoint(obs_diag, state)
+        own_state = lax.dynamic_slice_in_dim(state, me * lat_rows, lat_rows, axis=2)
+        if step + 1 < ITERS:
+            image = direction + adjoint(obs_diag, state)
+            dot = jnp.sum(direction * image)
+        else:
+            own_diag = lax.dynamic_slice_in_dim(obs_diag, me * lat_rows, lat_rows, axis=2)
+            dot = jnp.sum(direction * direction) + jnp.sum(own_diag * own_state * own_state)
         if norm_now is None:
-            sums = global_sum(jnp.stack([jnp.sum(residual * residual), jnp.sum(direction * image)]))
+            sums = global_sum(jnp.stack([jnp.sum(residual * residual), dot]))
             norm_now, curvature = sums[0], sums[1]
         else:
-            curvature = global_sum(jnp.sum(direction * image))
+            curvature = global_sum(dot)
         alpha = norm_now / curvature
         control = control + alpha * direction
-        own_state = lax.dynamic_slice_in_dim(state, me * lat_rows, lat_rows, axis=2)
         increment = increment + alpha * own_state
         if step + 1 < ITERS:
             residual = residual - alpha * image

time: 159 us -> 153 us (0.962)
  Pallas kernels: 27.6 us -> 22.1 us
    pallas_call x5 -> x4, Pallas kernels: 27.6 us -> 22.1 us  [local_call(): pl.pallas_call(kernel, out_shape=jax.ShapeDtypeStruct(out_shape, jnp.floa...]
    add x2 -> x1, other arithmetic: 3.18 us -> 1.6 us  [sum_over_tile_by_permutes(): total + lax.ppermute(block, 'tile', [(i, (i + k) % count) for i in range(...]
    reduce_sum x2 -> x3, other arithmetic: 3.66 us -> 4.94 us  [the longest x1 1.88 us: body(): sums = global_sum(jnp.stack([jnp.sum(residual * residual), dot]))]
where the time goes in v5:
time: 153 us; the launch traced here: 152 us
  waiting for transfers between devices  48.8 us (32%)
  blocking collectives  28.4 us (19%)
  Pallas kernels  22.1 us (14%)
  other arithmetic  16.7 us (11%)
  starting transfers between devices  16 us (10%)
  local copies, waits for them, and re-layouts  11.2 us (7%)
  between operations  6.06 us (4%)
  matrix products  2.47 us (2%)
    all_to_all x3, blocking collectives, global_sum(): return jnp.sum(lax.all_to_all(spread, axes, 0, 0, tiled=True), axis=0)  28.4 us
    all_to_all x1, waiting for transfers between devices, body(): got = lax.all_to_all(sent, ('tile', 'mem'), 0, 0, tiled=True)  24.7 us
    pallas_call x4, Pallas kernels, local_call(): pl.pallas_call(kernel, out_shape=jax.ShapeDtypeStruct(out_shape, jnp.floa...  22.1 us
    all_to_all x1, waiting for transfers between devices, to_output(): got = lax.all_to_all(sent, ('tile', 'mem'), 0, 0, tiled=True)  14.9 us
    ppermute x6, waiting for transfers between devices, sum_over_tile_by_permutes(): lax.ppermute(block, 'tile', [(i, (i + k) % count) for i in range(count)])  9.25 us
    all_to_all x1, starting transfers between devices, body(): got = lax.all_to_all(sent, ('tile', 'mem'), 0, 0, tiled=True)  6.12 us
    ppermute x6, starting transfers between devices, sum_over_tile_by_permutes(): lax.ppermute(block, 'tile', [(i, (i + k) % count) for i in range(count)])  4.08 us
    ppermute x3, starting transfers between devices, gather_rows_by_permutes(): lax.ppermute(block, 'tile', [(i, (i + k) % count) for i in range(count)])  3.23 us
  transfers between devices with their start and end apart: 11, of which 8 were waited for; matrix products, arithmetic and copies ran while one was open for 5% of the time, Pallas kernels for 0%

profile of v5, /device:TPU:0, one launch (start us, length us, event | category | flops | bytes accessed | tf_op | source)
XLA Modules:
  0.0 151.8 jit_solution(1226096673633180400)
XLA Ops:
  0.6 0.6 compare_reduce_fusion.1
  1.3 0.6 compare_reduce_fusion
  1.9 0.7 add_select_fusion.1
  2.7 0.0 copy-start.7
  2.7 0.2 fusion.5
  2.9 0.0 copy-start.2
  3.0 2.5 %fusion.6 = f32[64,128,2]{1,0,2:T(8,128)S(1)} fusion(f32[4096,128]{0,1:T(8,128)S(1)} %fusion.5, f32[4096,2]{0,1:T(2,128)S(1)} %pad_maximum_fusion.1, s32[4096]{0:T(1024)S(1)} %get-tuple-element.45), kind=kOutput, calls=%fused_computation.7 | convolution fusion | flops 806617088 | bytes 2211840 | tf_op jit(solution)/shard_map/dot_general | solution.py:97
  5.6 0.7 fusion.16
  6.3 0.7 fusion.17
  7.0 0.1 copy.106
  7.1 2.4 %collective-permute-start = (f32[9,4,512]{2,1,0:T(4,128)S(1)}, f32[9,4,512]{2,1,0:T(4,128)S(1)}, u32[]{:S(2)}, u32[]{:S(2)}) collective-permute-start(f32[9,4,512]{2,1,0:T(4,128)S(1)} %pad_maximum_fusion), channel_id=1, source_target_pairs={{0,24},{8,0},{16,8},{24,16},{1,25},{9,1},{17,9},{25,17},{2,26},{10... | collective-permute-start | bytes 221192 | tf_op jit(solution)/shard_map/ppermute | solution.py:120
  9.5 0.6 collective-permute-start.1
  10.2 0.2 collective-permute-start.2
  10.3 0.4 copy.114
  10.8 0.6 copy.139
  11.4 1.7 %copy.116 = f32[32,2,2,4,1,512]{5,3,2,1,4,0:T(4,128)} copy(f32[32,2,2,4,1,512]{5,0,3,2,1,4:T(8,128)S(1)} %bitcast.94) | data formatting | bytes 2097152 | tf_op jit(solution)/shard_map/reshape | solution.py:177
  13.1 6.1 %all-to-all-start = ((f32[32,2,2,4,1,512]{5,3,2,1,4,0:T(4,128)}), f32[32,2,2,4,1,512]{5,3,2,1,4,0:T(4,128)S(1)}, u32[]{:S(2)}, u32[]{:S(2)}) async-start(f32[32,2,2,4,1,512]{5,3,2,1,4,0:T(4,128)} %copy.116), calls=%async_computation | async-start | bytes 2097152 | tf_op jit(solution)/shard_map/all_to_all | solution.py:180
  19.3 0.1 dynamic-slice_bitcast_fusion
  19.3 0.6 pad_maximum_fusion.2.rates_ref
  20.1 0.7 squeeze.25.diag_ref
  20.9 0.1 reshape.296
  21.0 0.1 copy.133
  21.1 0.8 compare_select_fusion.2.mask_ref
  21.9 24.7 %all-to-all-done = f32[32,2,2,4,1,512]{5,3,2,1,4,0:T(4,128)S(1)} async-done(((f32[32,2,2,4,1,512]{5,3,2,1,4,0:T(4,128)}), f32[32,2,2,4,1,512]{5,3,2,1,4,0:T(4,128)S(1)}, u32[]{:S(2)}, u32[]{:S(2)}) %all-to-all-start) | async-done | bytes 1048608 | tf_op jit(solution)/shard_map/all_to_all | solution.py:180
  46.6 0.6 copy.138
  47.2 1.1 copy.118
  48.3 0.7 broadcast_in_dim.35.state_ref
  49.0 5.4 %shard_map.95.field_ref = f32[2,16,8,512]{3,2,1,0:T(8,128)} custom-call(f32[2,2]{1,0:T(2,128)} %pad_maximum_fusion.2.rates_ref, f32[16,1,512]{2,1,0:T(1,128)} %compare_select_fusion.2.mask_ref, f32[2,2,16,8,512]{4,3,2,1,0:T(8,128)} %bitcast.90, f32[2,2,16,512]{3,2,1,0:T(8,128)} %squeeze.25.diag_ref, f32[2,2,16,512]{3,2,1,0:T(8,128)} %broadcast_in_dim.35.state_ref), custom_call_target="tpu_custom_call" | custom-call | flops 42991616 | bytes 1343488 | tf_op jit(solution)/shard_map/pallas_call | solution.py:71
  54.4 5.7 %shard_map.96 = f32[2,2,16,512]{3,2,1,0:T(8,128)} custom-call(f32[2,2]{1,0:T(2,128)} %pad_maximum_fusion.2.rates_ref, f32[16,1,512]{2,1,0:T(1,128)} %compare_select_fusion.2.mask_ref, f32[2,2,16,8,512]{4,3,2,1,0:T(8,128)} %bitcast.91, f32[2,16,8,512]{3,2,1,0:T(8,128)} %shard_map.95.field_ref), custom_call_target="tpu_custom_call" | custom-call | flops 51380224 | bytes 1605632 | tf_op jit(solution)/shard_map/pallas_call | solution.py:71
  60.0 0.9 collective-permute-start.4
  60.9 1.2 collective-permute-start.5
  62.0 0.7 squeeze.26.diag_ref
  62.7 2.7 %collective-permute-done.3 = f32[2,2,16,512]{3,2,1,0:T(8,128)S(1)} collective-permute-done((f32[2,2,16,512]{3,2,1,0:T(8,128)}, f32[2,2,16,512]{3,2,1,0:T(8,128)S(1)}, u32[]{:S(2)}, u32[]{:S(2)}) %collective-permute-start.3) | collective-permute-done | bytes 131104 | tf_op jit(solution)/shard_map/ppermute | solution.py:144
  65.5 1.1 collective-permute-done.4
  66.6 0.4 collective-permute-done.5
  67.0 1.6 %add_add_fusion.state_ref = f32[2,2,16,512]{3,2,1,0:T(8,128)} fusion(f32[2,2,16,512]{3,2,1,0:T(8,128)S(1)} %collective-permute-done.5, f32[2,2,16,512]{3,2,1,0:T(8,128)S(1)} %collective-permute-done.4, f32[2,2,16,512]{3,2,1,0:T(8,128)} %shard_map.96, f32[2,2,16,512]{3,2,1,0:T(8,128)S(1)} %collective-permute-done.3), kind=kLoop, calls=%fused_computation.25 | loop fusion | flops 98304 | bytes 655360 | tf_op jit(solution)/shard_map/add | solution.py:144
  68.6 5.4 %shard_map.97 = f32[2,16,8,512]{3,2,1,0:T(8,128)} custom-call(f32[2,2]{1,0:T(2,128)} %pad_maximum_fusion.2.rates_ref, f32[16,1,512]{2,1,0:T(1,128)} %compare_select_fusion.2.mask_ref, f32[2,2,16,8,512]{4,3,2,1,0:T(8,128)} %bitcast.92, f32[2,2,16,512]{3,2,1,0:T(8,128)} %squeeze.26.diag_ref, f32[2,2,16,512]{3,2,1,0:T(8,128)} %add_add_fusion.state_ref), custom_call_target="tpu_custom_call" | custom-call | flops 42991616 | bytes 1343488 | tf_op jit(solution)/shard_map/pallas_call | solution.py:71
  74.1 1.9 %multiply_reduce_fusion.3 = (f32[]{:T(128)}, f32[]{:T(128)}, f32[2,16,8,512]{3,2,1,0:T(8,128)S(1)}) fusion(f32[2,16,8,512]{3,2,1,0:T(8,128)S(1)} %copy-done, f32[2,16,8,512]{3,2,1,0:T(8,128)} %shard_map.97), kind=kLoop, calls=%fused_computation.20 | loop fusion | flops 655358 | bytes 1572872 | tf_op jit(solution)/shard_map/reduce_sum | solution.py:266
  75.9 1.4 pad_maximum_fusion.3
  77.4 10.4 %all_to_all.28 = f32[32,1,2]{2,1,0:T(1,128)S(1)} all-to-all(f32[32,1,2]{2,1,0:T(1,128)S(1)} %broadcast_in_dim.36), channel_id=1, replica_groups=mesh['tile'=4,'mem'=8] {'tile','mem'}, dimensions={0} | all-to-all | bytes 512 | tf_op jit(solution)/shard_map/all_to_all | solution.py:88
  87.8 0.1 reduce_sum.74
  87.9 0.6 fusion.18
  89.7 0.8 multiply_reduce_fusion.1
  90.5 0.7 broadcast_in_dim.37
  91.1 8.8 %all_to_all.29 = f32[32,1,1]{2,1,0:T(1,128)S(1)} all-to-all(f32[32,1,1]{2,1,0:T(1,128)S(1)} %broadcast_in_dim.37), channel_id=1, replica_groups=mesh['tile'=4,'mem'=8] {'tile','mem'}, dimensions={0} | all-to-all | bytes 256 | tf_op jit(solution)/shard_map/all_to_all | solution.py:88
  99.9 0.7 reduce_sum.76
  101.8 1.5 %multiply_reduce_fusion = (f32[]{:T(128)}, f32[2,16,8,512]{3,2,1,0:T(8,128)}) fusion(f32[2,16,8,512]{3,2,1,0:T(8,128)S(1)} %copy-done, f32[]{:T(128)S(6)} %div.26, f32[2,16,8,512]{3,2,1,0:T(8,128)S(1)} %get-tuple-element.42, f32[]{:T(128)S(6)} %div.25), kind=kLoop, calls=%fused_computation.15 | loop fusion | flops 786431 | bytes 1572876 | tf_op jit(solution)/shard_map/reduce_sum | solution.py:264
  103.4 5.6 %shard_map.98 = f32[2,2,16,512]{3,2,1,0:T(8,128)} custom-call(f32[2,2]{1,0:T(2,128)} %pad_maximum_fusion.2.rates_ref, f32[16,1,512]{2,1,0:T(1,128)} %compare_select_fusion.2.mask_ref, f32[2,2,16,8,512]{4,3,2,1,0:T(8,128)} %bitcast.93, f32[2,16,8,512]{3,2,1,0:T(8,128)} %get-tuple-element.41.field_ref), custom_call_target="tpu_custom_call" | custom-call | flops 51380224 | bytes 1605632 | tf_op jit(solution)/shard_map/pallas_call | solution.py:71
  109.0 0.6 collective-permute-start.7
  109.6 1.4 collective-permute-start.8
  111.1 3.4 %collective-permute-done.6 = f32[2,2,16,512]{3,2,1,0:T(8,128)S(1)} collective-permute-done((f32[2,2,16,512]{3,2,1,0:T(8,128)}, f32[2,2,16,512]{3,2,1,0:T(8,128)S(1)}, u32[]{:S(2)}, u32[]{:S(2)}) %collective-permute-start.6) | collective-permute-done | bytes 131104 | tf_op jit(solution)/shard_map/ppermute | solution.py:144
  114.5 1.1 collective-permute-done.7
  115.6 0.5 collective-permute-done.8
  116.0 1.5 fusion.12
  118.8 9.1 %all_to_all.30 = f32[32,1,1]{2,1,0:T(1,128)S(1)} all-to-all(f32[32,1,1]{2,1,0:T(1,128)S(1)} %broadcast_in_dim.38), channel_id=1, replica_groups=mesh['tile'=4,'mem'=8] {'tile','mem'}, dimensions={0} | all-to-all | bytes 256 | tf_op jit(solution)/shard_map/all_to_all | solution.py:88
  128.0 0.6 reduce_sum.79
  129.9 0.1 multiply_add_fusion
  130.1 1.1 copy.123
  131.2 2.6 %all-to-all-start.4 = ((f32[32,2,4,1,512]{4,2,1,3,0:T(4,128)}), f32[32,2,4,1,512]{4,2,1,3,0:T(4,128)S(1)}, u32[]{:S(2)}, u32[]{:S(2)}) async-start(f32[32,2,4,1,512]{4,2,1,3,0:T(4,128)} %copy.123), calls=%async_computation.4 | async-start | bytes 1048576 | tf_op jit(solution)/shard_map/all_to_all | solution.py:219
  133.8 1.5 multiply_add_fusion.2
  135.3 14.9 %all-to-all-done.4 = f32[32,2,4,1,512]{4,2,1,3,0:T(4,128)S(1)} async-done(((f32[32,2,4,1,512]{4,2,1,3,0:T(4,128)}), f32[32,2,4,1,512]{4,2,1,3,0:T(4,128)S(1)}, u32[]{:S(2)}, u32[]{:S(2)}) %all-to-all-start.4) | async-done | bytes 524320 | tf_op jit(solution)/shard_map/all_to_all | solution.py:219
  150.2 0.3 copy.140
  150.5 0.3 copy.125
  150.8 1.0 copy.126
  (43 shorter events, 0.5 us)
Async XLA Ops:
  0.6 2.3 %copy-start.4 = (f32[1,4096]{1,0:T(1,128)S(1)}, f32[1,4096]{1,0:T(1,128)}, u32[]{:S(2)}) copy-start(f32[1,4096]{1,0:T(1,128)} %param.13) | copy-start | bytes 49156
  0.6 2.3 %copy-start.3 = (f32[1,4096]{1,0:T(1,128)S(1)}, f32[1,4096]{1,0:T(1,128)}, u32[]{:S(2)}) copy-start(f32[1,4096]{1,0:T(1,128)} %param.14) | copy-start | bytes 49156
  2.7 2.9 %copy-start.7 = (s32[4]{0:T(128)S(1)}, s32[4]{0:T(128)}, u32[]{:S(2)}) copy-start(s32[4]{0:T(128)} %param.16) | copy-start | bytes 52
  2.7 3.6 %copy-start.8 = (s32[4]{0:T(128)S(1)}, s32[4]{0:T(128)}, u32[]{:S(2)}) copy-start(s32[4]{0:T(128)} %param.17) | copy-start | bytes 52
  2.9 7.4 %copy-start.2 = (bf16[4,2,4,16,512]{4,3,2,1,0:T(8,128)(2,1)S(1)}, bf16[4,2,4,16,512]{4,3,2,1,0:T(8,128)(2,1)}, u32[]{:S(2)}) copy-start(bf16[4,2,4,16,512]{4,3,2,1,0:T(8,128)(2,1)} %param.12) | copy-start | bytes 1572868
  7.1 12.8 %collective-permute-start = (f32[9,4,512]{2,1,0:T(4,128)S(1)}, f32[9,4,512]{2,1,0:T(4,128)S(1)}, u32[]{:S(2)}, u32[]{:S(2)}) collective-permute-start(f32[9,4,512]{2,1,0:T(4,128)S(1)} %pad_maximum_fusion), channel_id=1, source_target_pairs={{0,24},{8,0},{16,8},{24,16},{1,25},{9,1},{17,9},{25,17},{2,26},{10... | collective-permute-start | bytes 221192 | tf_op jit(solution)/shard_map/ppermute | solution.py:120
  9.5 10.4 %collective-permute-start.1 = (f32[9,4,512]{2,1,0:T(4,128)S(1)}, f32[9,4,512]{2,1,0:T(4,128)S(1)}, u32[]{:S(2)}, u32[]{:S(2)}) collective-permute-start(f32[9,4,512]{2,1,0:T(4,128)S(1)} %pad_maximum_fusion), channel_id=1, source_target_pairs={{0,16},{8,24},{16,0},{24,8},{1,17},{9,25},{17,1},{25,9},{2,18},{10... | collective-permute-start | bytes 221192 | tf_op jit(solution)/shard_map/ppermute | solution.py:120
  10.2 9.8 %collective-permute-start.2 = (f32[9,4,512]{2,1,0:T(4,128)S(1)}, f32[9,4,512]{2,1,0:T(4,128)S(1)}, u32[]{:S(2)}, u32[]{:S(2)}) collective-permute-start(f32[9,4,512]{2,1,0:T(4,128)S(1)} %pad_maximum_fusion), channel_id=1, source_target_pairs={{0,8},{8,16},{16,24},{24,0},{1,9},{9,17},{17,25},{25,1},{2,10},{10... | collective-permute-start | bytes 221192 | tf_op jit(solution)/shard_map/ppermute | solution.py:120
  11.4 7.9 %copy-start.5 = (f32[16]{0:T(128)S(1)}, f32[16]{0:T(128)}, u32[]{:S(2)}) copy-start(f32[16]{0:T(128)} %param.19) | copy-start | bytes 196
  11.4 7.9 %copy-start.6 = (f32[16]{0:T(128)S(1)}, f32[16]{0:T(128)}, u32[]{:S(2)}) copy-start(f32[16]{0:T(128)} %param.18) | copy-start | bytes 196
  13.1 33.5 %all-to-all-start = ((f32[32,2,2,4,1,512]{5,3,2,1,4,0:T(4,128)}), f32[32,2,2,4,1,512]{5,3,2,1,4,0:T(4,128)S(1)}, u32[]{:S(2)}, u32[]{:S(2)}) async-start(f32[32,2,2,4,1,512]{5,3,2,1,4,0:T(4,128)} %copy.116), calls=%async_computation | async-start | bytes 2097152 | tf_op jit(solution)/shard_map/all_to_all | solution.py:180
  54.4 19.7 %copy-start = (f32[2,16,8,512]{3,2,1,0:T(8,128)S(1)}, f32[2,16,8,512]{3,2,1,0:T(8,128)}, u32[]{:S(2)}) copy-start(f32[2,16,8,512]{3,2,1,0:T(8,128)} %shard_map.95.field_ref) | copy-start | bytes 1572868
  60.0 5.5 %collective-permute-start.3 = (f32[2,2,16,512]{3,2,1,0:T(8,128)}, f32[2,2,16,512]{3,2,1,0:T(8,128)S(1)}, u32[]{:S(2)}, u32[]{:S(2)}) collective-permute-start(f32[2,2,16,512]{3,2,1,0:T(8,128)} %shard_map.96), channel_id=1, source_target_pairs={{0,8},{8,16},{16,24},{24,0},{1,9},{9,17},{17,25},{25,1},{2,10},{10... | collective-permute-start | bytes 393224 | tf_op jit(solution)/shard_map/ppermute | solution.py:144
  60.0 6.6 %collective-permute-start.4 = (f32[2,2,16,512]{3,2,1,0:T(8,128)}, f32[2,2,16,512]{3,2,1,0:T(8,128)S(1)}, u32[]{:S(2)}, u32[]{:S(2)}) collective-permute-start(f32[2,2,16,512]{3,2,1,0:T(8,128)} %shard_map.96), channel_id=1, source_target_pairs={{0,16},{8,24},{16,0},{24,8},{1,17},{9,25},{17,1},{25,9},{2,18},{10... | collective-permute-start | bytes 393224 | tf_op jit(solution)/shard_map/ppermute | solution.py:144
  60.9 6.1 %collective-permute-start.5 = (f32[2,2,16,512]{3,2,1,0:T(8,128)}, f32[2,2,16,512]{3,2,1,0:T(8,128)S(1)}, u32[]{:S(2)}, u32[]{:S(2)}) collective-permute-start(f32[2,2,16,512]{3,2,1,0:T(8,128)} %shard_map.96), channel_id=1, source_target_pairs={{0,24},{8,0},{16,8},{24,16},{1,25},{9,1},{17,9},{25,17},{2,26},{10... | collective-permute-start | bytes 393224 | tf_op jit(solution)/shard_map/ppermute | solution.py:144
  103.4 26.6 %copy-start.1 = (f32[2,16,8,512]{3,2,1,0:T(8,128)S(1)}, f32[2,16,8,512]{3,2,1,0:T(8,128)}, u32[]{:S(2)}) copy-start(f32[2,16,8,512]{3,2,1,0:T(8,128)} %get-tuple-element.41.field_ref) | copy-start | bytes 1572868
  109.0 5.5 %collective-permute-start.6 = (f32[2,2,16,512]{3,2,1,0:T(8,128)}, f32[2,2,16,512]{3,2,1,0:T(8,128)S(1)}, u32[]{:S(2)}, u32[]{:S(2)}) collective-permute-start(f32[2,2,16,512]{3,2,1,0:T(8,128)} %shard_map.98), channel_id=1, source_target_pairs={{0,8},{8,16},{16,24},{24,0},{1,9},{9,17},{17,25},{25,1},{2,10},{10... | collective-permute-start | bytes 393224 | tf_op jit(solution)/shard_map/ppermute | solution.py:144
  109.0 6.6 %collective-permute-start.7 = (f32[2,2,16,512]{3,2,1,0:T(8,128)}, f32[2,2,16,512]{3,2,1,0:T(8,128)S(1)}, u32[]{:S(2)}, u32[]{:S(2)}) collective-permute-start(f32[2,2,16,512]{3,2,1,0:T(8,128)} %shard_map.98), channel_id=1, source_target_pairs={{0,16},{8,24},{16,0},{24,8},{1,17},{9,25},{17,1},{25,9},{2,18},{10... | collective-permute-start | bytes 393224 | tf_op jit(solution)/shard_map/ppermute | solution.py:144
  109.6 6.4 %collective-permute-start.8 = (f32[2,2,16,512]{3,2,1,0:T(8,128)}, f32[2,2,16,512]{3,2,1,0:T(8,128)S(1)}, u32[]{:S(2)}, u32[]{:S(2)}) collective-permute-start(f32[2,2,16,512]{3,2,1,0:T(8,128)} %shard_map.98), channel_id=1, source_target_pairs={{0,24},{8,0},{16,8},{24,16},{1,25},{9,1},{17,9},{25,17},{2,26},{10... | collective-permute-start | bytes 393224 | tf_op jit(solution)/shard_map/ppermute | solution.py:144
  131.2 19.0 %all-to-all-start.4 = ((f32[32,2,4,1,512]{4,2,1,3,0:T(4,128)}), f32[32,2,4,1,512]{4,2,1,3,0:T(4,128)S(1)}, u32[]{:S(2)}, u32[]{:S(2)}) async-start(f32[32,2,4,1,512]{4,2,1,3,0:T(4,128)} %copy.123), calls=%async_computation.4 | async-start | bytes 1048576 | tf_op jit(solution)/shard_map/all_to_all | solution.py:219

commit v6 on v5

--- a/solution.py
+++ b/solution.py
@@ -253,8 +253,12 @@
     control = jnp.zeros_like(residual)
     increment = jnp.zeros(state_shape, jnp.float32)
     norm_now = None
+    ahead = None
     for step in range(ITERS):
-        state = forward(direction)
+        if ahead is None:
+            state = forward(direction)
+        else:
+            state = ahead[0] + ahead[1] * ahead[2]
         own_state = lax.dynamic_slice_in_dim(state, me * lat_rows, lat_rows, axis=2)
         if step + 1 < ITERS:
             image = direction + adjoint(obs_diag, state)
@@ -272,8 +276,12 @@
         increment = increment + alpha * own_state
         if step + 1 < ITERS:
             residual = residual - alpha * image
+            from_residual = forward(residual) if step + 2 == ITERS else None
             norm_next = global_sum(jnp.sum(residual * residual))
-            direction = residual + norm_next / norm_now * direction
+            beta = norm_next / norm_now
+            direction = residual + beta * direction
+            if from_residual is not None:
+                ahead = (from_residual, beta, state)
             norm_now = norm_next
     control = to_output(control)
     increment = increment.transpose(0, 2, 1, 3).reshape(slots, lat_rows, shard_cols)

time: 153 us -> 150 us (0.980)
  blocking collectives: 28.4 us -> 12.9 us
  starting transfers between devices: 16 us -> 23.1 us
  waiting for transfers between devices: 48.8 us -> 53.9 us
    all_to_all x3 -> x1, blocking collectives: 28.4 us -> 12.9 us  [global_sum(): return jnp.sum(lax.all_to_all(spread, axes, 0, 0, tiled=True), axis=0)]
    all_to_all x0 -> x2, waiting for transfers between devices: none -> 7.04 us  [global_sum(): return jnp.sum(lax.all_to_all(spread, axes, 0, 0, tiled=True), axis=0)]
    all_to_all x0 -> x2, starting transfers between devices: none -> 6 us  [global_sum(): return jnp.sum(lax.all_to_all(spread, axes, 0, 0, tiled=True), axis=0)]
    ppermute x6, waiting for transfers between devices: 9.25 us -> 6.45 us  [sum_over_tile_by_permutes(): lax.ppermute(block, 'tile', [(i, (i + k) % count) for i in range(count)])]
  transfers between devices with their start and end apart: 11 -> 13, of which waited for: 8 -> 8; matrix products, arithmetic and copies ran while one was open for 5% -> 5% of each run, Pallas kernels for 0% -> 4%
where the time goes in v6:
time: 150 us; the launch traced here: 149 us
  waiting for transfers between devices  53.9 us (36%)
  starting transfers between devices  23.1 us (15%)
  Pallas kernels  22.1 us (15%)
  other arithmetic  15.8 us (11%)
  blocking collectives  12.9 us (9%)
  local copies, waits for them, and re-layouts  12.4 us (8%)
  between operations  6.35 us (4%)
  matrix products  2.47 us (2%)
    all_to_all x1, waiting for transfers between devices, body(): got = lax.all_to_all(sent, ('tile', 'mem'), 0, 0, tiled=True)  24.7 us
    pallas_call x4, Pallas kernels, local_call(): pl.pallas_call(kernel, out_shape=jax.ShapeDtypeStruct(out_shape, jnp.floa...  22.1 us
    all_to_all x1, waiting for transfers between devices, to_output(): got = lax.all_to_all(sent, ('tile', 'mem'), 0, 0, tiled=True)  15.7 us
    all_to_all x1, blocking collectives, global_sum(): return jnp.sum(lax.all_to_all(spread, axes, 0, 0, tiled=True), axis=0)  12.9 us
    all_to_all x2, waiting for transfers between devices, global_sum(): return jnp.sum(lax.all_to_all(spread, axes, 0, 0, tiled=True), axis=0)  7.04 us
    ppermute x6, waiting for transfers between devices, sum_over_tile_by_permutes(): lax.ppermute(block, 'tile', [(i, (i + k) % count) for i in range(count)])  6.45 us
    all_to_all x1, starting transfers between devices, body(): got = lax.all_to_all(sent, ('tile', 'mem'), 0, 0, tiled=True)  6.12 us
    all_to_all x2, starting transfers between devices, global_sum(): return jnp.sum(lax.all_to_all(spread, axes, 0, 0, tiled=True), axis=0)  6 us
  transfers between devices with their start and end apart: 13, of which 8 were waited for; matrix products, arithmetic and copies ran while one was open for 5% of the time, Pallas kernels for 4%

profile of v6, /device:TPU:0, one launch (start us, length us, event | category | flops | bytes accessed | tf_op | source)
XLA Modules:
  0.0 149.0 jit_solution(5582993634950314573)
XLA Ops:
  0.6 0.6 compare_reduce_fusion.1
  1.3 0.6 compare_reduce_fusion
  1.9 0.7 add_select_fusion.1
  2.7 0.2 fusion.5
  3.0 2.5 %fusion.6 = f32[64,128,2]{1,0,2:T(8,128)S(1)} fusion(f32[4096,128]{0,1:T(8,128)S(1)} %fusion.5, f32[4096,2]{0,1:T(2,128)S(1)} %pad_maximum_fusion.1, s32[4096]{0:T(1024)S(1)} %get-tuple-element.45), kind=kOutput, calls=%fused_computation.7 | convolution fusion | flops 806617088 | bytes 2211840 | tf_op jit(solution)/shard_map/dot_general | solution.py:97
  5.6 0.7 fusion.17
  6.3 0.7 fusion.18
  7.0 0.1 copy.106
  7.1 2.4 %collective-permute-start = (f32[9,4,512]{2,1,0:T(4,128)S(1)}, f32[9,4,512]{2,1,0:T(4,128)S(1)}, u32[]{:S(2)}, u32[]{:S(2)}) collective-permute-start(f32[9,4,512]{2,1,0:T(4,128)S(1)} %pad_maximum_fusion), channel_id=1, source_target_pairs={{0,24},{8,0},{16,8},{24,16},{1,25},{9,1},{17,9},{25,17},{2,26},{10... | collective-permute-start | bytes 221192 | tf_op jit(solution)/shard_map/ppermute | solution.py:120
  9.5 0.6 collective-permute-start.1
  10.2 0.2 collective-permute-start.2
  10.3 0.4 copy.114
  10.8 0.6 copy.139
  11.4 1.7 %copy.116 = f32[32,2,2,4,1,512]{5,3,2,1,4,0:T(4,128)} copy(f32[32,2,2,4,1,512]{5,0,3,2,1,4:T(8,128)S(1)} %bitcast.94) | data formatting | bytes 2097152 | tf_op jit(solution)/shard_map/reshape | solution.py:177
  13.0 6.1 %all-to-all-start = ((f32[32,2,2,4,1,512]{5,3,2,1,4,0:T(4,128)}), f32[32,2,2,4,1,512]{5,3,2,1,4,0:T(4,128)S(1)}, u32[]{:S(2)}, u32[]{:S(2)}) async-start(f32[32,2,2,4,1,512]{5,3,2,1,4,0:T(4,128)} %copy.116), calls=%async_computation | async-start | bytes 2097152 | tf_op jit(solution)/shard_map/all_to_all | solution.py:180
  19.3 0.1 dynamic-slice_bitcast_fusion
  19.3 0.6 pad_maximum_fusion.2.rates_ref
  20.1 0.7 squeeze.25.diag_ref
  20.8 0.1 reshape.296
  21.0 0.1 copy.133
  21.0 0.8 compare_select_fusion.2.mask_ref
  21.9 24.7 %all-to-all-done = f32[32,2,2,4,1,512]{5,3,2,1,4,0:T(4,128)S(1)} async-done(((f32[32,2,2,4,1,512]{5,3,2,1,4,0:T(4,128)}), f32[32,2,2,4,1,512]{5,3,2,1,4,0:T(4,128)S(1)}, u32[]{:S(2)}, u32[]{:S(2)}) %all-to-all-start) | async-done | bytes 1048608 | tf_op jit(solution)/shard_map/all_to_all | solution.py:180
  46.6 0.6 copy.138
  47.2 1.1 copy.118
  48.3 0.7 broadcast_in_dim.35.state_ref
  48.9 5.4 %shard_map.95.field_ref = f32[2,16,8,512]{3,2,1,0:T(8,128)} custom-call(f32[2,2]{1,0:T(2,128)} %pad_maximum_fusion.2.rates_ref, f32[16,1,512]{2,1,0:T(1,128)} %compare_select_fusion.2.mask_ref, f32[2,2,16,8,512]{4,3,2,1,0:T(8,128)} %bitcast.90, f32[2,2,16,512]{3,2,1,0:T(8,128)} %squeeze.25.diag_ref, f32[2,2,16,512]{3,2,1,0:T(8,128)} %broadcast_in_dim.35.state_ref), custom_call_target="tpu_custom_call" | custom-call | flops 42991616 | bytes 1343488 | tf_op jit(solution)/shard_map/pallas_call | solution.py:71
  54.3 5.6 %shard_map.96 = f32[2,2,16,512]{3,2,1,0:T(8,128)} custom-call(f32[2,2]{1,0:T(2,128)} %pad_maximum_fusion.2.rates_ref, f32[16,1,512]{2,1,0:T(1,128)} %compare_select_fusion.2.mask_ref, f32[2,2,16,8,512]{4,3,2,1,0:T(8,128)} %bitcast.91, f32[2,16,8,512]{3,2,1,0:T(8,128)} %shard_map.95.field_ref), custom_call_target="tpu_custom_call" | custom-call | flops 51380224 | bytes 1605632 | tf_op jit(solution)/shard_map/pallas_call | solution.py:71
  60.0 0.9 collective-permute-start.4
  60.8 1.2 collective-permute-start.5
  62.0 0.7 squeeze.26.diag_ref
  62.7 2.7 %collective-permute-done.3 = f32[2,2,16,512]{3,2,1,0:T(8,128)S(1)} collective-permute-done((f32[2,2,16,512]{3,2,1,0:T(8,128)}, f32[2,2,16,512]{3,2,1,0:T(8,128)S(1)}, u32[]{:S(2)}, u32[]{:S(2)}) %collective-permute-start.3) | collective-permute-done | bytes 131104 | tf_op jit(solution)/shard_map/ppermute | solution.py:144
  65.4 1.1 collective-permute-done.4
  66.5 0.4 collective-permute-done.5
  67.0 1.6 %add_add_fusion.state_ref = f32[2,2,16,512]{3,2,1,0:T(8,128)} fusion(f32[2,2,16,512]{3,2,1,0:T(8,128)S(1)} %collective-permute-done.5, f32[2,2,16,512]{3,2,1,0:T(8,128)S(1)} %collective-permute-done.4, f32[2,2,16,512]{3,2,1,0:T(8,128)} %shard_map.96, f32[2,2,16,512]{3,2,1,0:T(8,128)S(1)} %collective-permute-done.3), kind=kLoop, calls=%fused_computation.25 | loop fusion | flops 98304 | bytes 655360 | tf_op jit(solution)/shard_map/add | solution.py:144
  68.6 5.4 %shard_map.97 = f32[2,16,8,512]{3,2,1,0:T(8,128)} custom-call(f32[2,2]{1,0:T(2,128)} %pad_maximum_fusion.2.rates_ref, f32[16,1,512]{2,1,0:T(1,128)} %compare_select_fusion.2.mask_ref, f32[2,2,16,8,512]{4,3,2,1,0:T(8,128)} %bitcast.92, f32[2,2,16,512]{3,2,1,0:T(8,128)} %squeeze.26.diag_ref, f32[2,2,16,512]{3,2,1,0:T(8,128)} %add_add_fusion.state_ref), custom_call_target="tpu_custom_call" | custom-call | flops 42991616 | bytes 1343488 | tf_op jit(solution)/shard_map/pallas_call | solution.py:71
  74.0 1.9 %multiply_reduce_fusion.3 = (f32[]{:T(128)}, f32[]{:T(128)}, f32[2,16,8,512]{3,2,1,0:T(8,128)S(1)}) fusion(f32[2,16,8,512]{3,2,1,0:T(8,128)S(1)} %copy-done, f32[2,16,8,512]{3,2,1,0:T(8,128)} %shard_map.97), kind=kLoop, calls=%fused_computation.20 | loop fusion | flops 655358 | bytes 1572872 | tf_op jit(solution)/shard_map/reduce_sum | solution.py:270
  75.9 1.4 pad_maximum_fusion.3
  77.2 0.6 broadcast_in_dim.36
  77.8 3.5 %all-to-all-start.1 = ((f32[32,1,2]{2,1,0:T(1,128)}), f32[32,1,2]{2,1,0:T(1,128)S(1)}, u32[]{:S(2)}, u32[]{:S(2)}) async-start(f32[32,1,2]{2,1,0:T(1,128)} %broadcast_in_dim.36), calls=%async_computation.1 | async-start | bytes 32768 | tf_op jit(solution)/shard_map/all_to_all | solution.py:88
  81.4 7.0 %all-to-all-done.1 = f32[32,1,2]{2,1,0:T(1,128)S(1)} async-done(((f32[32,1,2]{2,1,0:T(1,128)}), f32[32,1,2]{2,1,0:T(1,128)S(1)}, u32[]{:S(2)}, u32[]{:S(2)}) %all-to-all-start.1) | async-done | bytes 288 | tf_op jit(solution)/shard_map/all_to_all | solution.py:88
  88.4 0.1 reduce_sum.74
  88.5 0.6 fusion.20
  90.4 1.6 %multiply_reduce_fusion.1 = (f32[]{:T(128)}, f32[2,16,8,512]{3,2,1,0:T(8,128)}) fusion(f32[2,16,8,512]{3,2,1,0:T(8,128)S(1)} %copy-done, f32[2,16,8,512]{3,2,1,0:T(8,128)S(1)} %get-tuple-element.42, f32[]{:T(128)S(6)} %div.25), kind=kLoop, calls=%fused_computation.17 | loop fusion | flops 524287 | bytes 1572872 | tf_op jit(solution)/shard_map/reduce_sum | solution.py:280
  92.0 1.3 broadcast_in_dim.37
  93.3 2.5 %all-to-all-start.2 = ((f32[32,1,1]{2,1,0:T(1,128)}), f32[32,1,1]{2,1,0:T(1,128)S(1)}, u32[]{:S(2)}, u32[]{:S(2)}) async-start(f32[32,1,1]{2,1,0:T(1,128)} %broadcast_in_dim.37), calls=%async_computation.2 | async-start | bytes 32768 | tf_op jit(solution)/shard_map/all_to_all | solution.py:88
  95.8 5.6 %shard_map.98 = f32[2,2,16,512]{3,2,1,0:T(8,128)} custom-call(f32[2,2]{1,0:T(2,128)} %pad_maximum_fusion.2.rates_ref, f32[16,1,512]{2,1,0:T(1,128)} %compare_select_fusion.2.mask_ref, f32[2,2,16,8,512]{4,3,2,1,0:T(8,128)} %bitcast.93, f32[2,16,8,512]{3,2,1,0:T(8,128)} %get-tuple-element.41.field_ref), custom_call_target="tpu_custom_call" | custom-call | flops 51380224 | bytes 1605632 | tf_op jit(solution)/shard_map/pallas_call | solution.py:71
  101.4 0.1 collective-permute-start.6
  101.5 1.7 %collective-permute-start.7 = (f32[2,2,16,512]{3,2,1,0:T(8,128)}, f32[2,2,16,512]{3,2,1,0:T(8,128)S(1)}, u32[]{:S(2)}, u32[]{:S(2)}) collective-permute-start(f32[2,2,16,512]{3,2,1,0:T(8,128)} %shard_map.98), channel_id=1, source_target_pairs={{0,16},{8,24},{16,0},{24,8},{1,17},{9,25},{17,1},{25,9},{2,18},{10... | collective-permute-start | bytes 393224 | tf_op jit(solution)/shard_map/ppermute | solution.py:144
  103.2 1.3 collective-permute-start.8
  104.5 0.6 reduce_sum.76
  106.5 0.8 multiply_reduce_fusion
  107.3 0.7 collective-permute-done.7
  108.0 1.4 collective-permute-done.8
  109.5 1.5 %fusion.12 = (f32[]{:T(128)}, f32[2,2,4,512]{3,2,1,0:T(4,128)S(1)}) fusion(f32[2,2,16,512]{3,2,1,0:T(8,128)} %squeeze.26.diag_ref, s32[]{:T(128)S(6)} %select_n.72, f32[2,2,16,512]{3,2,1,0:T(8,128)S(1)} %copy-done.2, f32[]{:T(128)S(6)} %div.26, f32[2,2,16,512]{3,2,1,0:T(8,128)S(1)} %collective-permute-done.8, ...), kind=kLoop, calls=%fused_computation.38 | loop fusion | flops 65535 | bytes 229388 | tf_op jit(solution)/shard_map/reduce_sum | solution.py:268
  112.2 12.9 %all_to_all.28 = f32[32,1,1]{2,1,0:T(1,128)S(1)} all-to-all(f32[32,1,1]{2,1,0:T(1,128)S(1)} %broadcast_in_dim.38), channel_id=1, replica_groups=mesh['tile'=4,'mem'=8] {'tile','mem'}, dimensions={0} | all-to-all | bytes 256 | tf_op jit(solution)/shard_map/all_to_all | solution.py:88
  125.1 0.6 reduce_sum.79
  127.1 0.1 multiply_add_fusion
  127.3 1.1 copy.123
  128.4 2.6 %all-to-all-start.4 = ((f32[32,2,4,1,512]{4,2,1,3,0:T(4,128)}), f32[32,2,4,1,512]{4,2,1,3,0:T(4,128)S(1)}, u32[]{:S(2)}, u32[]{:S(2)}) async-start(f32[32,2,4,1,512]{4,2,1,3,0:T(4,128)} %copy.123), calls=%async_computation.4 | async-start | bytes 1048576 | tf_op jit(solution)/shard_map/all_to_all | solution.py:219
  131.0 0.6 multiply_add_fusion.2
  131.7 15.7 %all-to-all-done.4 = f32[32,2,4,1,512]{4,2,1,3,0:T(4,128)S(1)} async-done(((f32[32,2,4,1,512]{4,2,1,3,0:T(4,128)}), f32[32,2,4,1,512]{4,2,1,3,0:T(4,128)S(1)}, u32[]{:S(2)}, u32[]{:S(2)}) %all-to-all-start.4) | async-done | bytes 524320 | tf_op jit(solution)/shard_map/all_to_all | solution.py:219
  147.4 0.3 copy.140
  147.7 0.3 copy.125
  148.0 1.0 copy.126
  (47 shorter events, 0.5 us)
Async XLA Ops:
  0.6 2.3 %copy-start.5 = (f32[1,4096]{1,0:T(1,128)S(1)}, f32[1,4096]{1,0:T(1,128)}, u32[]{:S(2)}) copy-start(f32[1,4096]{1,0:T(1,128)} %param.13) | copy-start | bytes 49156
  0.6 2.3 %copy-start.4 = (f32[1,4096]{1,0:T(1,128)S(1)}, f32[1,4096]{1,0:T(1,128)}, u32[]{:S(2)}) copy-start(f32[1,4096]{1,0:T(1,128)} %param.14) | copy-start | bytes 49156
  2.7 2.9 %copy-start.8 = (s32[4]{0:T(128)S(1)}, s32[4]{0:T(128)}, u32[]{:S(2)}) copy-start(s32[4]{0:T(128)} %param.16) | copy-start | bytes 52
  2.7 3.6 %copy-start.9 = (s32[4]{0:T(128)S(1)}, s32[4]{0:T(128)}, u32[]{:S(2)}) copy-start(s32[4]{0:T(128)} %param.17) | copy-start | bytes 52
  2.9 7.4 %copy-start.3 = (bf16[4,2,4,16,512]{4,3,2,1,0:T(8,128)(2,1)S(1)}, bf16[4,2,4,16,512]{4,3,2,1,0:T(8,128)(2,1)}, u32[]{:S(2)}) copy-start(bf16[4,2,4,16,512]{4,3,2,1,0:T(8,128)(2,1)} %param.12) | copy-start | bytes 1572868
  7.1 12.8 %collective-permute-start = (f32[9,4,512]{2,1,0:T(4,128)S(1)}, f32[9,4,512]{2,1,0:T(4,128)S(1)}, u32[]{:S(2)}, u32[]{:S(2)}) collective-permute-start(f32[9,4,512]{2,1,0:T(4,128)S(1)} %pad_maximum_fusion), channel_id=1, source_target_pairs={{0,24},{8,0},{16,8},{24,16},{1,25},{9,1},{17,9},{25,17},{2,26},{10... | collective-permute-start | bytes 221192 | tf_op jit(solution)/shard_map/ppermute | solution.py:120
  9.5 10.4 %collective-permute-start.1 = (f32[9,4,512]{2,1,0:T(4,128)S(1)}, f32[9,4,512]{2,1,0:T(4,128)S(1)}, u32[]{:S(2)}, u32[]{:S(2)}) collective-permute-start(f32[9,4,512]{2,1,0:T(4,128)S(1)} %pad_maximum_fusion), channel_id=1, source_target_pairs={{0,16},{8,24},{16,0},{24,8},{1,17},{9,25},{17,1},{25,9},{2,18},{10... | collective-permute-start | bytes 221192 | tf_op jit(solution)/shard_map/ppermute | solution.py:120
  10.2 9.8 %collective-permute-start.2 = (f32[9,4,512]{2,1,0:T(4,128)S(1)}, f32[9,4,512]{2,1,0:T(4,128)S(1)}, u32[]{:S(2)}, u32[]{:S(2)}) collective-permute-start(f32[9,4,512]{2,1,0:T(4,128)S(1)} %pad_maximum_fusion), channel_id=1, source_target_pairs={{0,8},{8,16},{16,24},{24,0},{1,9},{9,17},{17,25},{25,1},{2,10},{10... | collective-permute-start | bytes 221192 | tf_op jit(solution)/shard_map/ppermute | solution.py:120
  11.4 7.9 %copy-start.6 = (f32[16]{0:T(128)S(1)}, f32[16]{0:T(128)}, u32[]{:S(2)}) copy-start(f32[16]{0:T(128)} %param.19) | copy-start | bytes 196
  11.4 7.9 %copy-start.7 = (f32[16]{0:T(128)S(1)}, f32[16]{0:T(128)}, u32[]{:S(2)}) copy-start(f32[16]{0:T(128)} %param.18) | copy-start | bytes 196
  13.0 33.5 %all-to-all-start = ((f32[32,2,2,4,1,512]{5,3,2,1,4,0:T(4,128)}), f32[32,2,2,4,1,512]{5,3,2,1,4,0:T(4,128)S(1)}, u32[]{:S(2)}, u32[]{:S(2)}) async-start(f32[32,2,2,4,1,512]{5,3,2,1,4,0:T(4,128)} %copy.116), calls=%async_computation | async-start | bytes 2097152 | tf_op jit(solution)/shard_map/all_to_all | solution.py:180
  54.3 19.6 %copy-start = (f32[2,16,8,512]{3,2,1,0:T(8,128)S(1)}, f32[2,16,8,512]{3,2,1,0:T(8,128)}, u32[]{:S(2)}) copy-start(f32[2,16,8,512]{3,2,1,0:T(8,128)} %shard_map.95.field_ref) | copy-start | bytes 1572868
  60.0 5.5 %collective-permute-start.3 = (f32[2,2,16,512]{3,2,1,0:T(8,128)}, f32[2,2,16,512]{3,2,1,0:T(8,128)S(1)}, u32[]{:S(2)}, u32[]{:S(2)}) collective-permute-start(f32[2,2,16,512]{3,2,1,0:T(8,128)} %shard_map.96), channel_id=1, source_target_pairs={{0,8},{8,16},{16,24},{24,0},{1,9},{9,17},{17,25},{25,1},{2,10},{10... | collective-permute-start | bytes 393224 | tf_op jit(solution)/shard_map/ppermute | solution.py:144
  60.0 6.6 %collective-permute-start.4 = (f32[2,2,16,512]{3,2,1,0:T(8,128)}, f32[2,2,16,512]{3,2,1,0:T(8,128)S(1)}, u32[]{:S(2)}, u32[]{:S(2)}) collective-permute-start(f32[2,2,16,512]{3,2,1,0:T(8,128)} %shard_map.96), channel_id=1, source_target_pairs={{0,16},{8,24},{16,0},{24,8},{1,17},{9,25},{17,1},{25,9},{2,18},{10... | collective-permute-start | bytes 393224 | tf_op jit(solution)/shard_map/ppermute | solution.py:144
  60.8 6.1 %collective-permute-start.5 = (f32[2,2,16,512]{3,2,1,0:T(8,128)}, f32[2,2,16,512]{3,2,1,0:T(8,128)S(1)}, u32[]{:S(2)}, u32[]{:S(2)}) collective-permute-start(f32[2,2,16,512]{3,2,1,0:T(8,128)} %shard_map.96), channel_id=1, source_target_pairs={{0,24},{8,0},{16,8},{24,16},{1,25},{9,1},{17,9},{25,17},{2,26},{10... | collective-permute-start | bytes 393224 | tf_op jit(solution)/shard_map/ppermute | solution.py:144
  77.8 10.6 %all-to-all-start.1 = ((f32[32,1,2]{2,1,0:T(1,128)}), f32[32,1,2]{2,1,0:T(1,128)S(1)}, u32[]{:S(2)}, u32[]{:S(2)}) async-start(f32[32,1,2]{2,1,0:T(1,128)} %broadcast_in_dim.36), calls=%async_computation.1 | async-start | bytes 32768 | tf_op jit(solution)/shard_map/all_to_all | solution.py:88
  90.4 19.0 %copy-start.2 = (f32[2,2,16,512]{3,2,1,0:T(8,128)S(1)}, f32[2,2,16,512]{3,2,1,0:T(8,128)}, u32[]{:S(2)}) copy-start(f32[2,2,16,512]{3,2,1,0:T(8,128)} %add_add_fusion.state_ref) | copy-start | bytes 393220
  92.0 14.5 %copy-start.1 = (f32[2,16,8,512]{3,2,1,0:T(8,128)S(1)}, f32[2,16,8,512]{3,2,1,0:T(8,128)}, u32[]{:S(2)}) copy-start(f32[2,16,8,512]{3,2,1,0:T(8,128)} %get-tuple-element.41.field_ref) | copy-start | bytes 1572868
  93.3 11.2 %all-to-all-start.2 = ((f32[32,1,1]{2,1,0:T(1,128)}), f32[32,1,1]{2,1,0:T(1,128)S(1)}, u32[]{:S(2)}, u32[]{:S(2)}) async-start(f32[32,1,1]{2,1,0:T(1,128)} %broadcast_in_dim.37), calls=%async_computation.2 | async-start | bytes 32768 | tf_op jit(solution)/shard_map/all_to_all | solution.py:88
  101.4 5.9 %collective-permute-start.6 = (f32[2,2,16,512]{3,2,1,0:T(8,128)}, f32[2,2,16,512]{3,2,1,0:T(8,128)S(1)}, u32[]{:S(2)}, u32[]{:S(2)}) collective-permute-start(f32[2,2,16,512]{3,2,1,0:T(8,128)} %shard_map.98), channel_id=1, source_target_pairs={{0,8},{8,16},{16,24},{24,0},{1,9},{9,17},{17,25},{25,1},{2,10},{10... | collective-permute-start | bytes 393224 | tf_op jit(solution)/shard_map/ppermute | solution.py:144
  101.5 6.5 %collective-permute-start.7 = (f32[2,2,16,512]{3,2,1,0:T(8,128)}, f32[2,2,16,512]{3,2,1,0:T(8,128)S(1)}, u32[]{:S(2)}, u32[]{:S(2)}) collective-permute-start(f32[2,2,16,512]{3,2,1,0:T(8,128)} %shard_map.98), channel_id=1, source_target_pairs={{0,16},{8,24},{16,0},{24,8},{1,17},{9,25},{17,1},{25,9},{2,18},{10... | collective-permute-start | bytes 393224 | tf_op jit(solution)/shard_map/ppermute | solution.py:144
  103.2 6.3 %collective-permute-start.8 = (f32[2,2,16,512]{3,2,1,0:T(8,128)}, f32[2,2,16,512]{3,2,1,0:T(8,128)S(1)}, u32[]{:S(2)}, u32[]{:S(2)}) collective-permute-start(f32[2,2,16,512]{3,2,1,0:T(8,128)} %shard_map.98), channel_id=1, source_target_pairs={{0,24},{8,0},{16,8},{24,16},{1,25},{9,1},{17,9},{25,17},{2,26},{10... | collective-permute-start | bytes 393224 | tf_op jit(solution)/shard_map/ppermute | solution.py:144
  128.4 19.0 %all-to-all-start.4 = ((f32[32,2,4,1,512]{4,2,1,3,0:T(4,128)}), f32[32,2,4,1,512]{4,2,1,3,0:T(4,128)S(1)}, u32[]{:S(2)}, u32[]{:S(2)}) async-start(f32[32,2,4,1,512]{4,2,1,3,0:T(4,128)} %copy.123), calls=%async_computation.4 | async-start | bytes 1048576 | tf_op jit(solution)/shard_map/all_to_all | solution.py:219

commit v7 on v6

--- a/solution.py
+++ b/solution.py
@@ -260,12 +260,10 @@
         else:
             state = ahead[0] + ahead[1] * ahead[2]
         own_state = lax.dynamic_slice_in_dim(state, me * lat_rows, lat_rows, axis=2)
+        own_diag = lax.dynamic_slice_in_dim(obs_diag, me * lat_rows, lat_rows, axis=2)
+        dot = jnp.sum(direction * direction) + jnp.sum(own_diag * own_state * own_state)
         if step + 1 < ITERS:
             image = direction + adjoint(obs_diag, state)
-            dot = jnp.sum(direction * image)
-        else:
-            own_diag = lax.dynamic_slice_in_dim(obs_diag, me * lat_rows, lat_rows, axis=2)
-            dot = jnp.sum(direction * direction) + jnp.sum(own_diag * own_state * own_state)
         if norm_now is None:
             sums = global_sum(jnp.stack([jnp.sum(residual * residual), dot]))
             norm_now, curvature = sums[0], sums[1]

time: 150 us -> 146 us (0.973)
  waiting for transfers between devices: 53.9 us -> 48.3 us
  starting transfers between devices: 23.1 us -> 25.1 us
    all_to_all x2, waiting for transfers between devices: 7.04 us -> 1.47 us  [global_sum(): return jnp.sum(lax.all_to_all(spread, axes, 0, 0, tiled=True), axis=0)]
    all_to_all x2, starting transfers between devices: 6 us -> 7.9 us  [global_sum(): return jnp.sum(lax.all_to_all(spread, axes, 0, 0, tiled=True), axis=0)]
  transfers between devices with their start and end apart: 13 -> 13, of which waited for: 8 -> 8; matrix products, arithmetic and copies ran while one was open for 5% -> 6% of each run, Pallas kernels for 4% -> 8%
where the time goes in v7:
time: 146 us
  waiting for transfers between devices  48.3 us (33%)
  starting transfers between devices  25.1 us (17%)
  Pallas kernels  22.1 us (15%)
  other arithmetic  15.2 us (10%)
  blocking collectives  12.8 us (9%)
  local copies, waits for them, and re-layouts  11.8 us (8%)
  between operations  7.76 us (5%)
  matrix products  2.48 us (2%)
    all_to_all x1, waiting for transfers between devices, body(): got = lax.all_to_all(sent, ('tile', 'mem'), 0, 0, tiled=True)  24.6 us
    pallas_call x4, Pallas kernels, local_call(): pl.pallas_call(kernel, out_shape=jax.ShapeDtypeStruct(out_shape, jnp.floa...  22.1 us
    all_to_all x1, waiting for transfers between devices, to_output(): got = lax.all_to_all(sent, ('tile', 'mem'), 0, 0, tiled=True)  15.7 us
    all_to_all x1, blocking collectives, global_sum(): return jnp.sum(lax.all_to_all(spread, axes, 0, 0, tiled=True), axis=0)  12.8 us
    all_to_all x2, starting transfers between devices, global_sum(): return jnp.sum(lax.all_to_all(spread, axes, 0, 0, tiled=True), axis=0)  7.9 us
    ppermute x6, waiting for transfers between devices, sum_over_tile_by_permutes(): lax.ppermute(block, 'tile', [(i, (i + k) % count) for i in range(count)])  6.46 us
    all_to_all x1, starting transfers between devices, body(): got = lax.all_to_all(sent, ('tile', 'mem'), 0, 0, tiled=True)  6.12 us
    ppermute x6, starting transfers between devices, sum_over_tile_by_permutes(): lax.ppermute(block, 'tile', [(i, (i + k) % count) for i in range(count)])  5.26 us
  transfers between devices with their start and end apart: 13, of which 8 were waited for; matrix products, arithmetic and copies ran while one was open for 6% of the time, Pallas kernels for 8%

profile of v7, /device:TPU:0, one launch (start us, length us, event | category | flops | bytes accessed | tf_op | source)
XLA Modules:
  0.0 145.6 jit_solution(12427111112959342035)
XLA Ops:
  0.6 0.6 compare_reduce_fusion.1
  1.3 0.6 compare_reduce_fusion
  1.9 0.7 add_select_fusion.1
  2.7 0.2 fusion.5
  3.0 2.5 %fusion.6 = f32[64,128,2]{1,0,2:T(8,128)S(1)} fusion(f32[4096,128]{0,1:T(8,128)S(1)} %fusion.5, f32[4096,2]{0,1:T(2,128)S(1)} %pad_maximum_fusion.1, s32[4096]{0:T(1024)S(1)} %get-tuple-element.42), kind=kOutput, calls=%fused_computation.7 | convolution fusion | flops 806617088 | bytes 2211840 | tf_op jit(solution)/shard_map/dot_general | solution.py:97
  5.6 0.7 fusion.18
  6.3 0.7 fusion.19
  7.0 0.1 copy.106
  7.1 2.4 %collective-permute-start = (f32[9,4,512]{2,1,0:T(4,128)S(1)}, f32[9,4,512]{2,1,0:T(4,128)S(1)}, u32[]{:S(2)}, u32[]{:S(2)}) collective-permute-start(f32[9,4,512]{2,1,0:T(4,128)S(1)} %pad_maximum_fusion), channel_id=1, source_target_pairs={{0,24},{8,0},{16,8},{24,16},{1,25},{9,1},{17,9},{25,17},{2,26},{10... | collective-permute-start | bytes 221192 | tf_op jit(solution)/shard_map/ppermute | solution.py:120
  9.5 0.6 collective-permute-start.1
  10.2 0.2 collective-permute-start.2
  10.3 0.4 copy.114
  10.8 0.6 copy.139
  11.4 1.6 %copy.116 = f32[32,2,2,4,1,512]{5,3,2,1,4,0:T(4,128)} copy(f32[32,2,2,4,1,512]{5,0,3,2,1,4:T(8,128)S(1)} %bitcast.94) | data formatting | bytes 2097152 | tf_op jit(solution)/shard_map/reshape | solution.py:177
  13.0 6.1 %all-to-all-start = ((f32[32,2,2,4,1,512]{5,3,2,1,4,0:T(4,128)}), f32[32,2,2,4,1,512]{5,3,2,1,4,0:T(4,128)S(1)}, u32[]{:S(2)}, u32[]{:S(2)}) async-start(f32[32,2,2,4,1,512]{5,3,2,1,4,0:T(4,128)} %copy.116), calls=%async_computation | async-start | bytes 2097152 | tf_op jit(solution)/shard_map/all_to_all | solution.py:180
  19.3 0.1 dynamic-slice_bitcast_fusion
  19.3 0.6 pad_maximum_fusion.2.rates_ref
  20.1 0.7 squeeze.25.diag_ref
  20.8 0.1 reshape.296
  21.0 0.1 copy.133
  21.1 0.8 compare_select_fusion.2.mask_ref
  21.9 24.6 %all-to-all-done = f32[32,2,2,4,1,512]{5,3,2,1,4,0:T(4,128)S(1)} async-done(((f32[32,2,2,4,1,512]{5,3,2,1,4,0:T(4,128)}), f32[32,2,2,4,1,512]{5,3,2,1,4,0:T(4,128)S(1)}, u32[]{:S(2)}, u32[]{:S(2)}) %all-to-all-start) | async-done | bytes 1048608 | tf_op jit(solution)/shard_map/all_to_all | solution.py:180
  46.6 0.6 copy.138
  47.2 1.1 copy.118
  48.3 0.7 broadcast_in_dim.35.state_ref
  48.9 5.4 %shard_map.95.field_ref = f32[2,16,8,512]{3,2,1,0:T(8,128)} custom-call(f32[2,2]{1,0:T(2,128)} %pad_maximum_fusion.2.rates_ref, f32[16,1,512]{2,1,0:T(1,128)} %compare_select_fusion.2.mask_ref, f32[2,2,16,8,512]{4,3,2,1,0:T(8,128)} %bitcast.90, f32[2,2,16,512]{3,2,1,0:T(8,128)} %squeeze.25.diag_ref, f32[2,2,16,512]{3,2,1,0:T(8,128)} %broadcast_in_dim.35.state_ref), custom_call_target="tpu_custom_call" | custom-call | flops 42991616 | bytes 1343488 | tf_op jit(solution)/shard_map/pallas_call | solution.py:71
  54.4 5.6 %shard_map.96 = f32[2,2,16,512]{3,2,1,0:T(8,128)} custom-call(f32[2,2]{1,0:T(2,128)} %pad_maximum_fusion.2.rates_ref, f32[16,1,512]{2,1,0:T(1,128)} %compare_select_fusion.2.mask_ref, f32[2,2,16,8,512]{4,3,2,1,0:T(8,128)} %bitcast.91, f32[2,16,8,512]{3,2,1,0:T(8,128)} %shard_map.95.field_ref), custom_call_target="tpu_custom_call" | custom-call | flops 51380224 | bytes 1605632 | tf_op jit(solution)/shard_map/pallas_call | solution.py:71
  60.0 0.9 collective-permute-start.4
  60.9 1.2 collective-permute-start.5
  62.0 0.7 multiply_reduce_fusion.2
  62.8 2.7 %collective-permute-done.3 = f32[2,2,16,512]{3,2,1,0:T(8,128)S(1)} collective-permute-done((f32[2,2,16,512]{3,2,1,0:T(8,128)}, f32[2,2,16,512]{3,2,1,0:T(8,128)S(1)}, u32[]{:S(2)}, u32[]{:S(2)}) %collective-permute-start.3) | collective-permute-done | bytes 131104 | tf_op jit(solution)/shard_map/ppermute | solution.py:144
  65.5 1.1 collective-permute-done.4
  66.6 0.4 collective-permute-done.5
  67.0 0.9 add_add_fusion.state_ref
  68.0 0.7 fusion.12
  70.0 0.7 pad_maximum_fusion.3
  70.7 0.6 broadcast_in_dim.36
  71.3 3.7 %all-to-all-start.1 = ((f32[32,1,2]{2,1,0:T(1,128)}), f32[32,1,2]{2,1,0:T(1,128)S(1)}, u32[]{:S(2)}, u32[]{:S(2)}) async-start(f32[32,1,2]{2,1,0:T(1,128)} %broadcast_in_dim.36), calls=%async_computation.1 | async-start | bytes 32768 | tf_op jit(solution)/shard_map/all_to_all | solution.py:88
  75.1 5.4 %shard_map.97 = f32[2,16,8,512]{3,2,1,0:T(8,128)} custom-call(f32[2,2]{1,0:T(2,128)} %pad_maximum_fusion.2.rates_ref, f32[16,1,512]{2,1,0:T(1,128)} %compare_select_fusion.2.mask_ref, f32[2,2,16,8,512]{4,3,2,1,0:T(8,128)} %bitcast.92, f32[2,2,16,512]{3,2,1,0:T(8,128)} %copy-done.4, f32[2,2,16,512]{3,2,1,0:T(8,128)} %copy-done.2), custom_call_target="tpu_custom_call" | custom-call | flops 42991616 | bytes 1343488 | tf_op jit(solution)/shard_map/pallas_call | solution.py:71
  80.5 1.5 %all-to-all-done.1 = f32[32,1,2]{2,1,0:T(1,128)S(1)} async-done(((f32[32,1,2]{2,1,0:T(1,128)}), f32[32,1,2]{2,1,0:T(1,128)S(1)}, u32[]{:S(2)}, u32[]{:S(2)}) %all-to-all-start.1) | async-done | bytes 288 | tf_op jit(solution)/shard_map/all_to_all | solution.py:88
  81.9 0.1 reduce_sum.78
  82.0 0.6 fusion.21
  84.0 2.6 %multiply_reduce_fusion.1 = (f32[]{:T(128)}, f32[2,16,8,512]{3,2,1,0:T(8,128)}) fusion(f32[2,16,8,512]{3,2,1,0:T(8,128)S(1)} %copy-done, f32[2,16,8,512]{3,2,1,0:T(8,128)} %shard_map.97, f32[]{:T(128)S(6)} %div.25), kind=kLoop, calls=%fused_computation.17 | loop fusion | flops 655359 | bytes 1572872 | tf_op jit(solution)/shard_map/reduce_sum | solution.py:278
  86.6 1.3 broadcast_in_dim.37
  88.0 4.2 %all-to-all-start.2 = ((f32[32,1,1]{2,1,0:T(1,128)}), f32[32,1,1]{2,1,0:T(1,128)S(1)}, u32[]{:S(2)}, u32[]{:S(2)}) async-start(f32[32,1,1]{2,1,0:T(1,128)} %broadcast_in_dim.37), calls=%async_computation.2 | async-start | bytes 32768 | tf_op jit(solution)/shard_map/all_to_all | solution.py:88
  92.1 5.6 %shard_map.98 = f32[2,2,16,512]{3,2,1,0:T(8,128)} custom-call(f32[2,2]{1,0:T(2,128)} %pad_maximum_fusion.2.rates_ref, f32[16,1,512]{2,1,0:T(1,128)} %compare_select_fusion.2.mask_ref, f32[2,2,16,8,512]{4,3,2,1,0:T(8,128)} %bitcast.93, f32[2,16,8,512]{3,2,1,0:T(8,128)} %get-tuple-element.39.field_ref), custom_call_target="tpu_custom_call" | custom-call | flops 51380224 | bytes 1605632 | tf_op jit(solution)/shard_map/pallas_call | solution.py:71
  97.7 0.3 collective-permute-start.6
  98.0 1.7 %collective-permute-start.7 = (f32[2,2,16,512]{3,2,1,0:T(8,128)}, f32[2,2,16,512]{3,2,1,0:T(8,128)S(1)}, u32[]{:S(2)}, u32[]{:S(2)}) collective-permute-start(f32[2,2,16,512]{3,2,1,0:T(8,128)} %shard_map.98), channel_id=1, source_target_pairs={{0,16},{8,24},{16,0},{24,8},{1,17},{9,25},{17,1},{25,9},{2,18},{10... | collective-permute-start | bytes 393224 | tf_op jit(solution)/shard_map/ppermute | solution.py:144
  99.7 1.3 collective-permute-start.8
  101.0 0.6 reduce_sum.80
  103.0 0.8 multiply_reduce_fusion
  103.7 0.8 collective-permute-done.7
  104.5 1.4 collective-permute-done.8
  106.0 1.6 %fusion.13 = (f32[]{:T(128)}, f32[2,2,4,512]{3,2,1,0:T(4,128)S(1)}) fusion(f32[2,2,16,512]{3,2,1,0:T(8,128)} %copy-done.4, s32[]{:T(128)S(6)} %select_n.73, f32[2,2,16,512]{3,2,1,0:T(8,128)S(1)} %copy-done.3, f32[]{:T(128)S(6)} %div.26, f32[2,2,16,512]{3,2,1,0:T(8,128)S(1)} %collective-permute-done.8, f32[2,2,16,512]{3,2,1,0:T(8,128)S(1)} %collective-permute-done.7, ...), kind=kLoop, calls=%fused_computation.39 | loop fusion | flops 65535 | bytes 229388 | tf_op jit(solution)/shard_map/reduce_sum | solution.py:264
  108.9 12.8 %all_to_all.28 = f32[32,1,1]{2,1,0:T(1,128)S(1)} all-to-all(f32[32,1,1]{2,1,0:T(1,128)S(1)} %broadcast_in_dim.38), channel_id=1, replica_groups=mesh['tile'=4,'mem'=8] {'tile','mem'}, dimensions={0} | all-to-all | bytes 256 | tf_op jit(solution)/shard_map/all_to_all | solution.py:88
  121.7 0.6 reduce_sum.83
  123.7 0.1 multiply_add_fusion
  123.8 1.1 copy.123
  125.0 2.6 %all-to-all-start.4 = ((f32[32,2,4,1,512]{4,2,1,3,0:T(4,128)}), f32[32,2,4,1,512]{4,2,1,3,0:T(4,128)S(1)}, u32[]{:S(2)}, u32[]{:S(2)}) async-start(f32[32,2,4,1,512]{4,2,1,3,0:T(4,128)} %copy.123), calls=%async_computation.4 | async-start | bytes 1048576 | tf_op jit(solution)/shard_map/all_to_all | solution.py:219
  127.6 0.6 multiply_add_fusion.2
  128.2 15.7 %all-to-all-done.4 = f32[32,2,4,1,512]{4,2,1,3,0:T(4,128)S(1)} async-done(((f32[32,2,4,1,512]{4,2,1,3,0:T(4,128)}), f32[32,2,4,1,512]{4,2,1,3,0:T(4,128)S(1)}, u32[]{:S(2)}, u32[]{:S(2)}) %all-to-all-start.4) | async-done | bytes 524320 | tf_op jit(solution)/shard_map/all_to_all | solution.py:219
  143.9 0.3 copy.140
  144.3 0.3 copy.125
  144.6 1.0 copy.126
  (52 shorter events, 0.6 us)
Async XLA Ops:
  0.6 2.3 %copy-start.7 = (f32[1,4096]{1,0:T(1,128)S(1)}, f32[1,4096]{1,0:T(1,128)}, u32[]{:S(2)}) copy-start(f32[1,4096]{1,0:T(1,128)} %param.13) | copy-start | bytes 49156
  0.6 2.3 %copy-start.6 = (f32[1,4096]{1,0:T(1,128)S(1)}, f32[1,4096]{1,0:T(1,128)}, u32[]{:S(2)}) copy-start(f32[1,4096]{1,0:T(1,128)} %param.14) | copy-start | bytes 49156
  2.7 2.9 %copy-start.10 = (s32[4]{0:T(128)S(1)}, s32[4]{0:T(128)}, u32[]{:S(2)}) copy-start(s32[4]{0:T(128)} %param.16) | copy-start | bytes 52
  2.7 3.6 %copy-start.11 = (s32[4]{0:T(128)S(1)}, s32[4]{0:T(128)}, u32[]{:S(2)}) copy-start(s32[4]{0:T(128)} %param.17) | copy-start | bytes 52
  2.9 7.4 %copy-start.5 = (bf16[4,2,4,16,512]{4,3,2,1,0:T(8,128)(2,1)S(1)}, bf16[4,2,4,16,512]{4,3,2,1,0:T(8,128)(2,1)}, u32[]{:S(2)}) copy-start(bf16[4,2,4,16,512]{4,3,2,1,0:T(8,128)(2,1)} %param.12) | copy-start | bytes 1572868
  7.1 12.8 %collective-permute-start = (f32[9,4,512]{2,1,0:T(4,128)S(1)}, f32[9,4,512]{2,1,0:T(4,128)S(1)}, u32[]{:S(2)}, u32[]{:S(2)}) collective-permute-start(f32[9,4,512]{2,1,0:T(4,128)S(1)} %pad_maximum_fusion), channel_id=1, source_target_pairs={{0,24},{8,0},{16,8},{24,16},{1,25},{9,1},{17,9},{25,17},{2,26},{10... | collective-permute-start | bytes 221192 | tf_op jit(solution)/shard_map/ppermute | solution.py:120
  9.5 10.4 %collective-permute-start.1 = (f32[9,4,512]{2,1,0:T(4,128)S(1)}, f32[9,4,512]{2,1,0:T(4,128)S(1)}, u32[]{:S(2)}, u32[]{:S(2)}) collective-permute-start(f32[9,4,512]{2,1,0:T(4,128)S(1)} %pad_maximum_fusion), channel_id=1, source_target_pairs={{0,16},{8,24},{16,0},{24,8},{1,17},{9,25},{17,1},{25,9},{2,18},{10... | collective-permute-start | bytes 221192 | tf_op jit(solution)/shard_map/ppermute | solution.py:120
  10.2 9.8 %collective-permute-start.2 = (f32[9,4,512]{2,1,0:T(4,128)S(1)}, f32[9,4,512]{2,1,0:T(4,128)S(1)}, u32[]{:S(2)}, u32[]{:S(2)}) collective-permute-start(f32[9,4,512]{2,1,0:T(4,128)S(1)} %pad_maximum_fusion), channel_id=1, source_target_pairs={{0,8},{8,16},{16,24},{24,0},{1,9},{9,17},{17,25},{25,1},{2,10},{10... | collective-permute-start | bytes 221192 | tf_op jit(solution)/shard_map/ppermute | solution.py:120
  11.4 7.9 %copy-start.8 = (f32[16]{0:T(128)S(1)}, f32[16]{0:T(128)}, u32[]{:S(2)}) copy-start(f32[16]{0:T(128)} %param.19) | copy-start | bytes 196
  11.4 7.9 %copy-start.9 = (f32[16]{0:T(128)S(1)}, f32[16]{0:T(128)}, u32[]{:S(2)}) copy-start(f32[16]{0:T(128)} %param.18) | copy-start | bytes 196
  13.0 33.5 %all-to-all-start = ((f32[32,2,2,4,1,512]{5,3,2,1,4,0:T(4,128)}), f32[32,2,2,4,1,512]{5,3,2,1,4,0:T(4,128)S(1)}, u32[]{:S(2)}, u32[]{:S(2)}) async-start(f32[32,2,2,4,1,512]{5,3,2,1,4,0:T(4,128)} %copy.116), calls=%async_computation | async-start | bytes 2097152 | tf_op jit(solution)/shard_map/all_to_all | solution.py:180
  21.1 46.8 %copy-start.4 = (f32[2,2,16,512]{3,2,1,0:T(8,128)}, f32[2,2,16,512]{3,2,1,0:T(8,128)S(1)}, u32[]{:S(2)}) copy-start(f32[2,2,16,512]{3,2,1,0:T(8,128)S(1)} %squeeze.26.diag_ref) | copy-start | bytes 393220
  54.4 7.7 %copy-start = (f32[2,16,8,512]{3,2,1,0:T(8,128)S(1)}, f32[2,16,8,512]{3,2,1,0:T(8,128)}, u32[]{:S(2)}) copy-start(f32[2,16,8,512]{3,2,1,0:T(8,128)} %shard_map.95.field_ref) | copy-start | bytes 1572868
  60.0 5.5 %collective-permute-start.3 = (f32[2,2,16,512]{3,2,1,0:T(8,128)}, f32[2,2,16,512]{3,2,1,0:T(8,128)S(1)}, u32[]{:S(2)}, u32[]{:S(2)}) collective-permute-start(f32[2,2,16,512]{3,2,1,0:T(8,128)} %shard_map.96), channel_id=1, source_target_pairs={{0,8},{8,16},{16,24},{24,0},{1,9},{9,17},{17,25},{25,1},{2,10},{10... | collective-permute-start | bytes 393224 | tf_op jit(solution)/shard_map/ppermute | solution.py:144
  60.0 6.6 %collective-permute-start.4 = (f32[2,2,16,512]{3,2,1,0:T(8,128)}, f32[2,2,16,512]{3,2,1,0:T(8,128)S(1)}, u32[]{:S(2)}, u32[]{:S(2)}) collective-permute-start(f32[2,2,16,512]{3,2,1,0:T(8,128)} %shard_map.96), channel_id=1, source_target_pairs={{0,16},{8,24},{16,0},{24,8},{1,17},{9,25},{17,1},{25,9},{2,18},{10... | collective-permute-start | bytes 393224 | tf_op jit(solution)/shard_map/ppermute | solution.py:144
  60.9 6.1 %collective-permute-start.5 = (f32[2,2,16,512]{3,2,1,0:T(8,128)}, f32[2,2,16,512]{3,2,1,0:T(8,128)S(1)}, u32[]{:S(2)}, u32[]{:S(2)}) collective-permute-start(f32[2,2,16,512]{3,2,1,0:T(8,128)} %shard_map.96), channel_id=1, source_target_pairs={{0,24},{8,0},{16,8},{24,16},{1,25},{9,1},{17,9},{25,17},{2,26},{10... | collective-permute-start | bytes 393224 | tf_op jit(solution)/shard_map/ppermute | solution.py:144
  67.9 7.1 %copy-start.2 = (f32[2,2,16,512]{3,2,1,0:T(8,128)}, f32[2,2,16,512]{3,2,1,0:T(8,128)S(1)}, u32[]{:S(2)}) copy-start(f32[2,2,16,512]{3,2,1,0:T(8,128)S(1)} %add_add_fusion.state_ref) | copy-start | bytes 393220
  71.3 10.6 %all-to-all-start.1 = ((f32[32,1,2]{2,1,0:T(1,128)}), f32[32,1,2]{2,1,0:T(1,128)S(1)}, u32[]{:S(2)}, u32[]{:S(2)}) async-start(f32[32,1,2]{2,1,0:T(1,128)} %broadcast_in_dim.36), calls=%async_computation.1 | async-start | bytes 32768 | tf_op jit(solution)/shard_map/all_to_all | solution.py:88
  84.0 22.0 %copy-start.3 = (f32[2,2,16,512]{3,2,1,0:T(8,128)S(1)}, f32[2,2,16,512]{3,2,1,0:T(8,128)}, u32[]{:S(2)}) copy-start(f32[2,2,16,512]{3,2,1,0:T(8,128)} %copy-done.2) | copy-start | bytes 393220
  86.6 16.3 %copy-start.1 = (f32[2,16,8,512]{3,2,1,0:T(8,128)S(1)}, f32[2,16,8,512]{3,2,1,0:T(8,128)}, u32[]{:S(2)}) copy-start(f32[2,16,8,512]{3,2,1,0:T(8,128)} %get-tuple-element.39.field_ref) | copy-start | bytes 1572868
  88.0 13.0 %all-to-all-start.2 = ((f32[32,1,1]{2,1,0:T(1,128)}), f32[32,1,1]{2,1,0:T(1,128)S(1)}, u32[]{:S(2)}, u32[]{:S(2)}) async-start(f32[32,1,1]{2,1,0:T(1,128)} %broadcast_in_dim.37), calls=%async_computation.2 | async-start | bytes 32768 | tf_op jit(solution)/shard_map/all_to_all | solution.py:88
  97.7 6.0 %collective-permute-start.6 = (f32[2,2,16,512]{3,2,1,0:T(8,128)}, f32[2,2,16,512]{3,2,1,0:T(8,128)S(1)}, u32[]{:S(2)}, u32[]{:S(2)}) collective-permute-start(f32[2,2,16,512]{3,2,1,0:T(8,128)} %shard_map.98), channel_id=1, source_target_pairs={{0,8},{8,16},{16,24},{24,0},{1,9},{9,17},{17,25},{25,1},{2,10},{10... | collective-permute-start | bytes 393224 | tf_op jit(solution)/shard_map/ppermute | solution.py:144
  98.0 6.6 %collective-permute-start.7 = (f32[2,2,16,512]{3,2,1,0:T(8,128)}, f32[2,2,16,512]{3,2,1,0:T(8,128)S(1)}, u32[]{:S(2)}, u32[]{:S(2)}) collective-permute-start(f32[2,2,16,512]{3,2,1,0:T(8,128)} %shard_map.98), channel_id=1, source_target_pairs={{0,16},{8,24},{16,0},{24,8},{1,17},{9,25},{17,1},{25,9},{2,18},{10... | collective-permute-start | bytes 393224 | tf_op jit(solution)/shard_map/ppermute | solution.py:144
  99.7 6.3 %collective-permute-start.8 = (f32[2,2,16,512]{3,2,1,0:T(8,128)}, f32[2,2,16,512]{3,2,1,0:T(8,128)S(1)}, u32[]{:S(2)}, u32[]{:S(2)}) collective-permute-start(f32[2,2,16,512]{3,2,1,0:T(8,128)} %shard_map.98), channel_id=1, source_target_pairs={{0,24},{8,0},{16,8},{24,16},{1,25},{9,1},{17,9},{25,17},{2,26},{10... | collective-permute-start | bytes 393224 | tf_op jit(solution)/shard_map/ppermute | solution.py:144
  125.0 19.0 %all-to-all-start.4 = ((f32[32,2,4,1,512]{4,2,1,3,0:T(4,128)}), f32[32,2,4,1,512]{4,2,1,3,0:T(4,128)S(1)}, u32[]{:S(2)}, u32[]{:S(2)}) async-start(f32[32,2,4,1,512]{4,2,1,3,0:T(4,128)} %copy.123), calls=%async_computation.4 | async-start | bytes 1048576 | tf_op jit(solution)/shard_map/all_to_all | solution.py:219

commit v8 on v7

--- a/solution.py
+++ b/solution.py
@@ -194,7 +194,7 @@
 
     rates = jnp.stack([lat_own, lon_own])
 
-    def forward(control):
+    def forward(control, own_rows=False):
         partial = local_call(
             forward_kernel,
             (slots, own_levels, control.shape[1], nlon),
@@ -203,6 +203,8 @@
             pert,
             control,
         )
+        if own_rows:
+            return reduce_rows_by_permutes(partial, 2)
         return sum_over_tile_by_permutes(partial)
 
     def adjoint(diag, state):
@@ -258,8 +260,10 @@
         if ahead is None:
             state = forward(direction)
         else:
-            state = ahead[0] + ahead[1] * ahead[2]
-        own_state = lax.dynamic_slice_in_dim(state, me * lat_rows, lat_rows, axis=2)
+            state = None
+            own_state = ahead[0] + ahead[1] * ahead[2]
+        if state is not None:
+            own_state = lax.dynamic_slice_in_dim(state, me * lat_rows, lat_rows, axis=2)
         own_diag = lax.dynamic_slice_in_dim(obs_diag, me * lat_rows, lat_rows, axis=2)
         dot = jnp.sum(direction * direction) + jnp.sum(own_diag * own_state * own_state)
         if step + 1 < ITERS:
@@ -274,12 +278,12 @@
         increment = increment + alpha * own_state
         if step + 1 < ITERS:
             residual = residual - alpha * image
-            from_residual = forward(residual) if step + 2 == ITERS else None
+            from_residual = forward(residual, own_rows=True) if step + 2 == ITERS else None
             norm_next = global_sum(jnp.sum(residual * residual))
             beta = norm_next / norm_now
             direction = residual + beta * direction
             if from_residual is not None:
-                ahead = (from_residual, beta, state)
+                ahead = (from_residual, beta, own_state)
             norm_now = norm_next
     control = to_output(control)
     increment = increment.transpose(0, 2, 1, 3).reshape(slots, lat_rows, shard_cols)

time: 146 us -> 144 us (0.986)
  blocking collectives: 12.8 us -> 8.81 us
    all_to_all x1, blocking collectives: 12.8 us -> 8.81 us  [global_sum(): return jnp.sum(lax.all_to_all(spread, axes, 0, 0, tiled=True), axis=0)]
    ppermute x0 -> x3, starting transfers between devices: none -> 3.3 us  [reduce_rows_by_permutes(): lax.ppermute(piece, 'tile', [(i, (i + k) % count) for i in range(count)])]
    ppermute x6 -> x3, starting transfers between devices: 5.26 us -> 2.01 us  [sum_over_tile_by_permutes(): lax.ppermute(block, 'tile', [(i, (i + k) % count) for i in range(count)])]
    all_to_all x2, waiting for transfers between devices: 1.47 us -> 4.26 us  [global_sum(): return jnp.sum(lax.all_to_all(spread, axes, 0, 0, tiled=True), axis=0)]
    ppermute x6 -> x3, waiting for transfers between devices: 6.46 us -> 4.24 us  [sum_over_tile_by_permutes(): lax.ppermute(block, 'tile', [(i, (i + k) % count) for i in range(count)])]
  transfers between devices with their start and end apart: 13 -> 13, of which waited for: 8 -> 7; matrix products, arithmetic and copies ran while one was open for 6% -> 6% of each run, Pallas kernels for 8% -> 4%
where the time goes in v8:
time: 144 us; the launch traced here: 143 us
  waiting for transfers between devices  48.8 us (34%)
  starting transfers between devices  25.2 us (18%)
  Pallas kernels  22.1 us (15%)
  other arithmetic  15.1 us (10%)
  local copies, waits for them, and re-layouts  12.6 us (9%)
  blocking collectives  8.81 us (6%)
  between operations  7.68 us (5%)
  matrix products  2.47 us (2%)
    all_to_all x1, waiting for transfers between devices, body(): got = lax.all_to_all(sent, ('tile', 'mem'), 0, 0, tiled=True)  24.6 us
    pallas_call x4, Pallas kernels, local_call(): pl.pallas_call(kernel, out_shape=jax.ShapeDtypeStruct(out_shape, jnp.floa...  22.1 us
    all_to_all x1, waiting for transfers between devices, to_output(): got = lax.all_to_all(sent, ('tile', 'mem'), 0, 0, tiled=True)  15.7 us
    all_to_all x1, blocking collectives, global_sum(): return jnp.sum(lax.all_to_all(spread, axes, 0, 0, tiled=True), axis=0)  8.81 us
    all_to_all x2, starting transfers between devices, global_sum(): return jnp.sum(lax.all_to_all(spread, axes, 0, 0, tiled=True), axis=0)  7.9 us
    all_to_all x1, starting transfers between devices, body(): got = lax.all_to_all(sent, ('tile', 'mem'), 0, 0, tiled=True)  6.12 us
    all_to_all x2, waiting for transfers between devices, global_sum(): return jnp.sum(lax.all_to_all(spread, axes, 0, 0, tiled=True), axis=0)  4.26 us
    ppermute x3, waiting for transfers between devices, sum_over_tile_by_permutes(): lax.ppermute(block, 'tile', [(i, (i + k) % count) for i in range(count)])  4.24 us
  transfers between devices with their start and end apart: 13, of which 7 were waited for; matrix products, arithmetic and copies ran while one was open for 6% of the time, Pallas kernels for 4%

profile of v8, /device:TPU:0, one launch (start us, length us, event | category | flops | bytes accessed | tf_op | source)
XLA Modules:
  0.0 142.8 jit_solution(16370986741476972999)
XLA Ops:
  0.6 0.6 compare_reduce_fusion.1
  1.3 0.6 compare_reduce_fusion
  1.9 0.7 add_select_fusion.1
  2.7 0.2 fusion.5
  3.0 2.5 %fusion.6 = f32[64,128,2]{1,0,2:T(8,128)S(1)} fusion(f32[4096,128]{0,1:T(8,128)S(1)} %fusion.5, f32[4096,2]{0,1:T(2,128)S(1)} %pad_maximum_fusion.1, s32[4096]{0:T(1024)S(1)} %get-tuple-element.45), kind=kOutput, calls=%fused_computation.7 | convolution fusion | flops 806617088 | bytes 2211840 | tf_op jit(solution)/shard_map/dot_general | solution.py:97
  5.6 0.7 fusion.17
  6.3 0.7 fusion.18
  7.0 0.1 copy.106
  7.1 2.4 %collective-permute-start = (f32[9,4,512]{2,1,0:T(4,128)S(1)}, f32[9,4,512]{2,1,0:T(4,128)S(1)}, u32[]{:S(2)}, u32[]{:S(2)}) collective-permute-start(f32[9,4,512]{2,1,0:T(4,128)S(1)} %pad_maximum_fusion), channel_id=1, source_target_pairs={{0,24},{8,0},{16,8},{24,16},{1,25},{9,1},{17,9},{25,17},{2,26},{10... | collective-permute-start | bytes 221192 | tf_op jit(solution)/shard_map/ppermute | solution.py:120
  9.5 0.6 collective-permute-start.1
  10.2 0.2 collective-permute-start.2
  10.3 0.4 copy.114
  10.8 0.6 copy.139
  11.4 1.6 %copy.116 = f32[32,2,2,4,1,512]{5,3,2,1,4,0:T(4,128)} copy(f32[32,2,2,4,1,512]{5,0,3,2,1,4:T(8,128)S(1)} %bitcast.94) | data formatting | bytes 2097152 | tf_op jit(solution)/shard_map/reshape | solution.py:177
  13.0 6.1 %all-to-all-start = ((f32[32,2,2,4,1,512]{5,3,2,1,4,0:T(4,128)}), f32[32,2,2,4,1,512]{5,3,2,1,4,0:T(4,128)S(1)}, u32[]{:S(2)}, u32[]{:S(2)}) async-start(f32[32,2,2,4,1,512]{5,3,2,1,4,0:T(4,128)} %copy.116), calls=%async_computation | async-start | bytes 2097152 | tf_op jit(solution)/shard_map/all_to_all | solution.py:180
  19.3 0.1 dynamic-slice_bitcast_fusion
  19.4 0.6 pad_maximum_fusion.2.rates_ref
  20.2 0.7 squeeze.25.diag_ref
  20.9 0.1 reshape.296
  21.0 0.1 copy.133
  21.1 0.8 compare_select_fusion.2.mask_ref
  22.0 24.6 %all-to-all-done = f32[32,2,2,4,1,512]{5,3,2,1,4,0:T(4,128)S(1)} async-done(((f32[32,2,2,4,1,512]{5,3,2,1,4,0:T(4,128)}), f32[32,2,2,4,1,512]{5,3,2,1,4,0:T(4,128)S(1)}, u32[]{:S(2)}, u32[]{:S(2)}) %all-to-all-start) | async-done | bytes 1048608 | tf_op jit(solution)/shard_map/all_to_all | solution.py:180
  46.6 0.6 copy.138
  47.2 1.1 copy.118
  48.3 0.7 broadcast_in_dim.35.state_ref
  48.9 5.4 %shard_map.95.field_ref = f32[2,16,8,512]{3,2,1,0:T(8,128)} custom-call(f32[2,2]{1,0:T(2,128)} %pad_maximum_fusion.2.rates_ref, f32[16,1,512]{2,1,0:T(1,128)} %compare_select_fusion.2.mask_ref, f32[2,2,16,8,512]{4,3,2,1,0:T(8,128)} %bitcast.90, f32[2,2,16,512]{3,2,1,0:T(8,128)} %squeeze.25.diag_ref, f32[2,2,16,512]{3,2,1,0:T(8,128)} %broadcast_in_dim.35.state_ref), custom_call_target="tpu_custom_call" | custom-call | flops 42991616 | bytes 1343488 | tf_op jit(solution)/shard_map/pallas_call | solution.py:71
  54.3 5.6 %shard_map.96 = f32[2,2,16,512]{3,2,1,0:T(8,128)} custom-call(f32[2,2]{1,0:T(2,128)} %pad_maximum_fusion.2.rates_ref, f32[16,1,512]{2,1,0:T(1,128)} %compare_select_fusion.2.mask_ref, f32[2,2,16,8,512]{4,3,2,1,0:T(8,128)} %bitcast.91, f32[2,16,8,512]{3,2,1,0:T(8,128)} %shard_map.95.field_ref), custom_call_target="tpu_custom_call" | custom-call | flops 51380224 | bytes 1605632 | tf_op jit(solution)/shard_map/pallas_call | solution.py:71
  60.0 0.9 collective-permute-start.4
  60.8 1.2 collective-permute-start.5
  62.0 0.7 multiply_reduce_fusion.2
  62.7 2.7 %collective-permute-done.3 = f32[2,2,16,512]{3,2,1,0:T(8,128)S(1)} collective-permute-done((f32[2,2,16,512]{3,2,1,0:T(8,128)}, f32[2,2,16,512]{3,2,1,0:T(8,128)S(1)}, u32[]{:S(2)}, u32[]{:S(2)}) %collective-permute-start.3) | collective-permute-done | bytes 131104 | tf_op jit(solution)/shard_map/ppermute | solution.py:144
  65.4 1.1 collective-permute-done.4
  66.5 0.4 collective-permute-done.5
  67.0 0.9 add_add_fusion.state_ref
  67.9 0.6 fusion.12
  69.9 0.7 pad_maximum_fusion.3
  70.6 0.6 broadcast_in_dim.36
  71.2 3.7 %all-to-all-start.1 = ((f32[32,1,2]{2,1,0:T(1,128)}), f32[32,1,2]{2,1,0:T(1,128)S(1)}, u32[]{:S(2)}, u32[]{:S(2)}) async-start(f32[32,1,2]{2,1,0:T(1,128)} %broadcast_in_dim.36), calls=%async_computation.1 | async-start | bytes 32768 | tf_op jit(solution)/shard_map/all_to_all | solution.py:88
  74.9 5.4 %shard_map.97 = f32[2,16,8,512]{3,2,1,0:T(8,128)} custom-call(f32[2,2]{1,0:T(2,128)} %pad_maximum_fusion.2.rates_ref, f32[16,1,512]{2,1,0:T(1,128)} %compare_select_fusion.2.mask_ref, f32[2,2,16,8,512]{4,3,2,1,0:T(8,128)} %bitcast.92, f32[2,2,16,512]{3,2,1,0:T(8,128)} %copy-done.4, f32[2,2,16,512]{3,2,1,0:T(8,128)} %copy-done.2), custom_call_target="tpu_custom_call" | custom-call | flops 42991616 | bytes 1343488 | tf_op jit(solution)/shard_map/pallas_call | solution.py:71
  80.4 1.5 %all-to-all-done.1 = f32[32,1,2]{2,1,0:T(1,128)S(1)} async-done(((f32[32,1,2]{2,1,0:T(1,128)}), f32[32,1,2]{2,1,0:T(1,128)S(1)}, u32[]{:S(2)}, u32[]{:S(2)}) %all-to-all-start.1) | async-done | bytes 288 | tf_op jit(solution)/shard_map/all_to_all | solution.py:88
  81.8 0.1 reduce_sum.78
  81.9 0.6 fusion.19
  83.8 2.6 %multiply_reduce_fusion.1 = (f32[]{:T(128)}, f32[2,16,8,512]{3,2,1,0:T(8,128)}) fusion(f32[2,16,8,512]{3,2,1,0:T(8,128)S(1)} %copy-done, f32[2,16,8,512]{3,2,1,0:T(8,128)} %shard_map.97, f32[]{:T(128)S(6)} %div.25), kind=kLoop, calls=%fused_computation.17 | loop fusion | flops 655359 | bytes 1572872 | tf_op jit(solution)/shard_map/reduce_sum | solution.py:282
  86.4 5.6 %shard_map.98 = f32[2,2,16,512]{3,2,1,0:T(8,128)} custom-call(f32[2,2]{1,0:T(2,128)} %pad_maximum_fusion.2.rates_ref, f32[16,1,512]{2,1,0:T(1,128)} %compare_select_fusion.2.mask_ref, f32[2,2,16,8,512]{4,3,2,1,0:T(8,128)} %bitcast.93, f32[2,16,8,512]{3,2,1,0:T(8,128)} %get-tuple-element.39.field_ref), custom_call_target="tpu_custom_call" | custom-call | flops 51380224 | bytes 1605632 | tf_op jit(solution)/shard_map/pallas_call | solution.py:71
  92.1 1.2 broadcast_in_dim.37
  93.3 4.2 %all-to-all-start.2 = ((f32[32,1,1]{2,1,0:T(1,128)}), f32[32,1,1]{2,1,0:T(1,128)S(1)}, u32[]{:S(2)}, u32[]{:S(2)}) async-start(f32[32,1,1]{2,1,0:T(1,128)} %broadcast_in_dim.37), calls=%async_computation.2 | async-start | bytes 32768 | tf_op jit(solution)/shard_map/all_to_all | solution.py:88
  97.5 0.9 constant_dynamic-slice_fusion.4
  98.4 0.3 collective-permute-start.6
  98.7 1.7 %collective-permute-start.7 = (f32[2,2,4,512]{3,2,1,0:T(4,128)S(1)}, f32[2,2,4,512]{3,2,1,0:T(4,128)S(1)}, u32[]{:S(2)}, u32[]{:S(2)}) collective-permute-start(f32[2,2,4,512]{3,2,1,0:T(4,128)S(1)} %get-tuple-element.44), channel_id=1, source_target_pairs={{0,16},{8,24},{16,0},{24,8},{1,17},{9,25},{17,1},{25,9},{2,18},{10... | collective-permute-start | bytes 98312 | tf_op jit(solution)/shard_map/ppermute | solution.py:136
  100.4 1.3 collective-permute-start.8
  101.7 2.8 %all-to-all-done.2 = f32[32,1,1]{2,1,0:T(1,128)S(1)} async-done(((f32[32,1,1]{2,1,0:T(1,128)}), f32[32,1,1]{2,1,0:T(1,128)S(1)}, u32[]{:S(2)}, u32[]{:S(2)}) %all-to-all-start.2) | async-done | bytes 160 | tf_op jit(solution)/shard_map/all_to_all | solution.py:88
  104.5 0.6 reduce_sum.80
  106.5 0.8 multiply_reduce_fusion
  107.3 1.6 %fusion.13 = (f32[]{:T(128)}, f32[2,2,4,512]{3,2,1,0:T(4,128)S(1)}) fusion(f32[2,2,16,512]{3,2,1,0:T(8,128)} %copy-done.4, s32[]{:T(128)S(6)} %select_n.96, f32[2,2,16,512]{3,2,1,0:T(8,128)S(1)} %copy-done.3, f32[]{:T(128)S(6)} %div.26, f32[2,2,4,512]{3,2,1,0:T(4,128)S(1)} %collective-permute-done.8, f32[2,2,4,512]{3,2,1,0:T(4,128)S(1)} %collective-permute-done.7, ...), kind=kLoop, calls=%fused_computation.39 | loop fusion | flops 65535 | bytes 229388 | tf_op jit(solution)/shard_map/reduce_sum | solution.py:268
  110.1 8.8 %all_to_all.28 = f32[32,1,1]{2,1,0:T(1,128)S(1)} all-to-all(f32[32,1,1]{2,1,0:T(1,128)S(1)} %broadcast_in_dim.38), channel_id=1, replica_groups=mesh['tile'=4,'mem'=8] {'tile','mem'}, dimensions={0} | all-to-all | bytes 256 | tf_op jit(solution)/shard_map/all_to_all | solution.py:88
  118.9 0.6 reduce_sum.83
  120.9 0.1 multiply_add_fusion
  121.1 1.1 copy.123
  122.2 2.6 %all-to-all-start.4 = ((f32[32,2,4,1,512]{4,2,1,3,0:T(4,128)}), f32[32,2,4,1,512]{4,2,1,3,0:T(4,128)S(1)}, u32[]{:S(2)}, u32[]{:S(2)}) async-start(f32[32,2,4,1,512]{4,2,1,3,0:T(4,128)} %copy.123), calls=%async_computation.4 | async-start | bytes 1048576 | tf_op jit(solution)/shard_map/all_to_all | solution.py:221
  124.8 0.6 multiply_add_fusion.2
  125.5 15.7 %all-to-all-done.4 = f32[32,2,4,1,512]{4,2,1,3,0:T(4,128)S(1)} async-done(((f32[32,2,4,1,512]{4,2,1,3,0:T(4,128)}), f32[32,2,4,1,512]{4,2,1,3,0:T(4,128)S(1)}, u32[]{:S(2)}, u32[]{:S(2)}) %all-to-all-start.4) | async-done | bytes 524320 | tf_op jit(solution)/shard_map/all_to_all | solution.py:221
  141.2 0.3 copy.140
  141.5 0.3 copy.125
  141.8 1.0 copy.126
  (53 shorter events, 0.6 us)
Async XLA Ops:
  0.6 2.3 %copy-start.7 = (f32[1,4096]{1,0:T(1,128)S(1)}, f32[1,4096]{1,0:T(1,128)}, u32[]{:S(2)}) copy-start(f32[1,4096]{1,0:T(1,128)} %param.13) | copy-start | bytes 49156
  0.6 2.3 %copy-start.6 = (f32[1,4096]{1,0:T(1,128)S(1)}, f32[1,4096]{1,0:T(1,128)}, u32[]{:S(2)}) copy-start(f32[1,4096]{1,0:T(1,128)} %param.14) | copy-start | bytes 49156
  2.7 2.9 %copy-start.10 = (s32[4]{0:T(128)S(1)}, s32[4]{0:T(128)}, u32[]{:S(2)}) copy-start(s32[4]{0:T(128)} %param.16) | copy-start | bytes 52
  2.7 3.6 %copy-start.11 = (s32[4]{0:T(128)S(1)}, s32[4]{0:T(128)}, u32[]{:S(2)}) copy-start(s32[4]{0:T(128)} %param.17) | copy-start | bytes 52
  2.9 7.4 %copy-start.5 = (bf16[4,2,4,16,512]{4,3,2,1,0:T(8,128)(2,1)S(1)}, bf16[4,2,4,16,512]{4,3,2,1,0:T(8,128)(2,1)}, u32[]{:S(2)}) copy-start(bf16[4,2,4,16,512]{4,3,2,1,0:T(8,128)(2,1)} %param.12) | copy-start | bytes 1572868
  7.1 12.9 %collective-permute-start = (f32[9,4,512]{2,1,0:T(4,128)S(1)}, f32[9,4,512]{2,1,0:T(4,128)S(1)}, u32[]{:S(2)}, u32[]{:S(2)}) collective-permute-start(f32[9,4,512]{2,1,0:T(4,128)S(1)} %pad_maximum_fusion), channel_id=1, source_target_pairs={{0,24},{8,0},{16,8},{24,16},{1,25},{9,1},{17,9},{25,17},{2,26},{10... | collective-permute-start | bytes 221192 | tf_op jit(solution)/shard_map/ppermute | solution.py:120
  9.5 10.4 %collective-permute-start.1 = (f32[9,4,512]{2,1,0:T(4,128)S(1)}, f32[9,4,512]{2,1,0:T(4,128)S(1)}, u32[]{:S(2)}, u32[]{:S(2)}) collective-permute-start(f32[9,4,512]{2,1,0:T(4,128)S(1)} %pad_maximum_fusion), channel_id=1, source_target_pairs={{0,16},{8,24},{16,0},{24,8},{1,17},{9,25},{17,1},{25,9},{2,18},{10... | collective-permute-start | bytes 221192 | tf_op jit(solution)/shard_map/ppermute | solution.py:120
  10.2 9.8 %collective-permute-start.2 = (f32[9,4,512]{2,1,0:T(4,128)S(1)}, f32[9,4,512]{2,1,0:T(4,128)S(1)}, u32[]{:S(2)}, u32[]{:S(2)}) collective-permute-start(f32[9,4,512]{2,1,0:T(4,128)S(1)} %pad_maximum_fusion), channel_id=1, source_target_pairs={{0,8},{8,16},{16,24},{24,0},{1,9},{9,17},{17,25},{25,1},{2,10},{10... | collective-permute-start | bytes 221192 | tf_op jit(solution)/shard_map/ppermute | solution.py:120
  11.4 7.9 %copy-start.8 = (f32[16]{0:T(128)S(1)}, f32[16]{0:T(128)}, u32[]{:S(2)}) copy-start(f32[16]{0:T(128)} %param.19) | copy-start | bytes 196
  11.4 7.9 %copy-start.9 = (f32[16]{0:T(128)S(1)}, f32[16]{0:T(128)}, u32[]{:S(2)}) copy-start(f32[16]{0:T(128)} %param.18) | copy-start | bytes 196
  13.0 33.5 %all-to-all-start = ((f32[32,2,2,4,1,512]{5,3,2,1,4,0:T(4,128)}), f32[32,2,2,4,1,512]{5,3,2,1,4,0:T(4,128)S(1)}, u32[]{:S(2)}, u32[]{:S(2)}) async-start(f32[32,2,2,4,1,512]{5,3,2,1,4,0:T(4,128)} %copy.116), calls=%async_computation | async-start | bytes 2097152 | tf_op jit(solution)/shard_map/all_to_all | solution.py:180
  21.1 46.8 %copy-start.4 = (f32[2,2,16,512]{3,2,1,0:T(8,128)}, f32[2,2,16,512]{3,2,1,0:T(8,128)S(1)}, u32[]{:S(2)}) copy-start(f32[2,2,16,512]{3,2,1,0:T(8,128)S(1)} %squeeze.26.diag_ref) | copy-start | bytes 393220
  54.3 7.7 %copy-start = (f32[2,16,8,512]{3,2,1,0:T(8,128)S(1)}, f32[2,16,8,512]{3,2,1,0:T(8,128)}, u32[]{:S(2)}) copy-start(f32[2,16,8,512]{3,2,1,0:T(8,128)} %shard_map.95.field_ref) | copy-start | bytes 1572868
  60.0 5.5 %collective-permute-start.3 = (f32[2,2,16,512]{3,2,1,0:T(8,128)}, f32[2,2,16,512]{3,2,1,0:T(8,128)S(1)}, u32[]{:S(2)}, u32[]{:S(2)}) collective-permute-start(f32[2,2,16,512]{3,2,1,0:T(8,128)} %shard_map.96), channel_id=1, source_target_pairs={{0,8},{8,16},{16,24},{24,0},{1,9},{9,17},{17,25},{25,1},{2,10},{10... | collective-permute-start | bytes 393224 | tf_op jit(solution)/shard_map/ppermute | solution.py:144
  60.0 6.6 %collective-permute-start.4 = (f32[2,2,16,512]{3,2,1,0:T(8,128)}, f32[2,2,16,512]{3,2,1,0:T(8,128)S(1)}, u32[]{:S(2)}, u32[]{:S(2)}) collective-permute-start(f32[2,2,16,512]{3,2,1,0:T(8,128)} %shard_map.96), channel_id=1, source_target_pairs={{0,16},{8,24},{16,0},{24,8},{1,17},{9,25},{17,1},{25,9},{2,18},{10... | collective-permute-start | bytes 393224 | tf_op jit(solution)/shard_map/ppermute | solution.py:144
  60.8 6.1 %collective-permute-start.5 = (f32[2,2,16,512]{3,2,1,0:T(8,128)}, f32[2,2,16,512]{3,2,1,0:T(8,128)S(1)}, u32[]{:S(2)}, u32[]{:S(2)}) collective-permute-start(f32[2,2,16,512]{3,2,1,0:T(8,128)} %shard_map.96), channel_id=1, source_target_pairs={{0,24},{8,0},{16,8},{24,16},{1,25},{9,1},{17,9},{25,17},{2,26},{10... | collective-permute-start | bytes 393224 | tf_op jit(solution)/shard_map/ppermute | solution.py:144
  67.9 7.0 %copy-start.2 = (f32[2,2,16,512]{3,2,1,0:T(8,128)}, f32[2,2,16,512]{3,2,1,0:T(8,128)S(1)}, u32[]{:S(2)}) copy-start(f32[2,2,16,512]{3,2,1,0:T(8,128)S(1)} %add_add_fusion.state_ref) | copy-start | bytes 393220
  71.2 10.6 %all-to-all-start.1 = ((f32[32,1,2]{2,1,0:T(1,128)}), f32[32,1,2]{2,1,0:T(1,128)S(1)}, u32[]{:S(2)}, u32[]{:S(2)}) async-start(f32[32,1,2]{2,1,0:T(1,128)} %broadcast_in_dim.36), calls=%async_computation.1 | async-start | bytes 32768 | tf_op jit(solution)/shard_map/all_to_all | solution.py:88
  83.8 23.5 %copy-start.3 = (f32[2,2,16,512]{3,2,1,0:T(8,128)S(1)}, f32[2,2,16,512]{3,2,1,0:T(8,128)}, u32[]{:S(2)}) copy-start(f32[2,2,16,512]{3,2,1,0:T(8,128)} %copy-done.2) | copy-start | bytes 393220
  86.4 20.1 %copy-start.1 = (f32[2,16,8,512]{3,2,1,0:T(8,128)S(1)}, f32[2,16,8,512]{3,2,1,0:T(8,128)}, u32[]{:S(2)}) copy-start(f32[2,16,8,512]{3,2,1,0:T(8,128)} %get-tuple-element.39.field_ref) | copy-start | bytes 1572868
  93.3 11.2 %all-to-all-start.2 = ((f32[32,1,1]{2,1,0:T(1,128)}), f32[32,1,1]{2,1,0:T(1,128)S(1)}, u32[]{:S(2)}, u32[]{:S(2)}) async-start(f32[32,1,1]{2,1,0:T(1,128)} %broadcast_in_dim.37), calls=%async_computation.2 | async-start | bytes 32768 | tf_op jit(solution)/shard_map/all_to_all | solution.py:88
  98.4 8.8 %collective-permute-start.6 = (f32[2,2,4,512]{3,2,1,0:T(4,128)S(1)}, f32[2,2,4,512]{3,2,1,0:T(4,128)S(1)}, u32[]{:S(2)}, u32[]{:S(2)}) collective-permute-start(f32[2,2,4,512]{3,2,1,0:T(4,128)S(1)} %get-tuple-element.42), channel_id=1, source_target_pairs={{0,8},{8,16},{16,24},{24,0},{1,9},{9,17},{17,25},{25,1},{2,10},{10... | collective-permute-start | bytes 98312 | tf_op jit(solution)/shard_map/ppermute | solution.py:136
  98.7 8.5 %collective-permute-start.7 = (f32[2,2,4,512]{3,2,1,0:T(4,128)S(1)}, f32[2,2,4,512]{3,2,1,0:T(4,128)S(1)}, u32[]{:S(2)}, u32[]{:S(2)}) collective-permute-start(f32[2,2,4,512]{3,2,1,0:T(4,128)S(1)} %get-tuple-element.44), channel_id=1, source_target_pairs={{0,16},{8,24},{16,0},{24,8},{1,17},{9,25},{17,1},{25,9},{2,18},{10... | collective-permute-start | bytes 98312 | tf_op jit(solution)/shard_map/ppermute | solution.py:136
  100.4 6.9 %collective-permute-start.8 = (f32[2,2,4,512]{3,2,1,0:T(4,128)S(1)}, f32[2,2,4,512]{3,2,1,0:T(4,128)S(1)}, u32[]{:S(2)}, u32[]{:S(2)}) collective-permute-start(f32[2,2,4,512]{3,2,1,0:T(4,128)S(1)} %get-tuple-element.43), channel_id=1, source_target_pairs={{0,24},{8,0},{16,8},{24,16},{1,25},{9,1},{17,9},{25,17},{2,26},{10... | collective-permute-start | bytes 98312 | tf_op jit(solution)/shard_map/ppermute | solution.py:136
  122.2 19.0 %all-to-all-start.4 = ((f32[32,2,4,1,512]{4,2,1,3,0:T(4,128)}), f32[32,2,4,1,512]{4,2,1,3,0:T(4,128)S(1)}, u32[]{:S(2)}, u32[]{:S(2)}) async-start(f32[32,2,4,1,512]{4,2,1,3,0:T(4,128)} %copy.123), calls=%async_computation.4 | async-start | bytes 1048576 | tf_op jit(solution)/shard_map/all_to_all | solution.py:221

commit v9 on v8

--- a/solution.py
+++ b/solution.py
@@ -45,13 +45,16 @@
     return now
 
 
-def adjoint_kernel(rates_ref, mask_ref, pert_ref, diag_ref, state_ref, out_ref):
+def adjoint_kernel(rates_ref, mask_ref, pert_ref, diag_ref, *refs):
+    state_refs, out_ref = refs[:-1], refs[-1]
     slots, levels = pert_ref.shape[:2]
     mask = mask_ref[...]
     for level in range(levels):
         field = None
         for slot in range(slots):
-            grad = diag_ref[slot, level] * state_ref[slot, level]
+            grad = diag_ref[slot, level]
+            if state_refs:
+                grad = grad * state_refs[0][slot, level]
             term = pert_ref[slot, level] * grad[:, None, :]
             field = term if field is None else field + term
         out_ref[level] = smooth_level(rates_ref, mask, field, level)
@@ -208,9 +211,8 @@
         return sum_over_tile_by_permutes(partial)
 
     def adjoint(diag, state):
-        return local_call(
-            adjoint_kernel, pert.shape[1:], rates, mask, pert, diag, state
-        )
+        states = () if state is None else (state,)
+        return local_call(adjoint_kernel, pert.shape[1:], rates, mask, pert, diag, *states)
 
     def to_output(control):
         if share and local_members % tiles == 0:
@@ -250,7 +252,7 @@
     first_grad, obs_diag = both[0], both[1]
     me = lax.axis_index("tile")
 
-    residual = adjoint(first_grad, jnp.ones_like(first_grad))
+    residual = adjoint(first_grad, None)
     direction = residual
     control = jnp.zeros_like(residual)
     increment = jnp.zeros(state_shape, jnp.float32)

time: 144 us -> 143 us (level)
  no operation moved by 1% of the time
where the time goes in v9:
time: 143 us; the launch traced here: 142 us
  waiting for transfers between devices  48.8 us (34%)
  starting transfers between devices  25.2 us (18%)
  Pallas kernels  22.1 us (15%)
  other arithmetic  15.1 us (11%)
  local copies, waits for them, and re-layouts  12 us (8%)
  blocking collectives  8.81 us (6%)
  between operations  7.68 us (5%)
  matrix products  2.47 us (2%)
    all_to_all x1, waiting for transfers between devices, body(): got = lax.all_to_all(sent, ('tile', 'mem'), 0, 0, tiled=True)  24.6 us
    pallas_call x4, Pallas kernels, local_call(): pl.pallas_call(kernel, out_shape=jax.ShapeDtypeStruct(out_shape, jnp.floa...  22.1 us
    all_to_all x1, waiting for transfers between devices, to_output(): got = lax.all_to_all(sent, ('tile', 'mem'), 0, 0, tiled=True)  15.7 us
    all_to_all x1, blocking collectives, global_sum(): return jnp.sum(lax.all_to_all(spread, axes, 0, 0, tiled=True), axis=0)  8.81 us
    all_to_all x2, starting transfers between devices, global_sum(): return jnp.sum(lax.all_to_all(spread, axes, 0, 0, tiled=True), axis=0)  7.9 us
    all_to_all x1, starting transfers between devices, body(): got = lax.all_to_all(sent, ('tile', 'mem'), 0, 0, tiled=True)  6.12 us
    all_to_all x2, waiting for transfers between devices, global_sum(): return jnp.sum(lax.all_to_all(spread, axes, 0, 0, tiled=True), axis=0)  4.26 us
    ppermute x3, waiting for transfers between devices, sum_over_tile_by_permutes(): lax.ppermute(block, 'tile', [(i, (i + k) % count) for i in range(count)])  4.24 us
  transfers between devices with their start and end apart: 13, of which 7 were waited for; matrix products, arithmetic and copies ran while one was open for 6% of the time, Pallas kernels for 4%

profile of v9, /device:TPU:0, one launch (start us, length us, event | category | flops | bytes accessed | tf_op | source)
XLA Modules:
  0.0 142.1 jit_solution(8778585747421620819)
XLA Ops:
  0.6 0.6 compare_reduce_fusion.1
  1.3 0.6 compare_reduce_fusion
  1.9 0.7 add_select_fusion.1
  2.7 0.0 copy-start.10
  2.7 0.2 fusion.5
  3.0 2.5 %fusion.6 = f32[64,128,2]{1,0,2:T(8,128)S(1)} fusion(f32[4096,128]{0,1:T(8,128)S(1)} %fusion.5, f32[4096,2]{0,1:T(2,128)S(1)} %pad_maximum_fusion.1, s32[4096]{0:T(1024)S(1)} %get-tuple-element.45), kind=kOutput, calls=%fused_computation.7 | convolution fusion | flops 806617088 | bytes 2211840 | tf_op jit(solution)/shard_map/dot_general | solution.py:100
  5.6 0.7 fusion.17
  6.3 0.7 fusion.18
  7.0 0.1 copy.106
  7.1 2.4 %collective-permute-start = (f32[9,4,512]{2,1,0:T(4,128)S(1)}, f32[9,4,512]{2,1,0:T(4,128)S(1)}, u32[]{:S(2)}, u32[]{:S(2)}) collective-permute-start(f32[9,4,512]{2,1,0:T(4,128)S(1)} %pad_maximum_fusion), channel_id=1, source_target_pairs={{0,24},{8,0},{16,8},{24,16},{1,25},{9,1},{17,9},{25,17},{2,26},{10... | collective-permute-start | bytes 221192 | tf_op jit(solution)/shard_map/ppermute | solution.py:123
  9.5 0.6 collective-permute-start.1
  10.2 0.2 collective-permute-start.2
  10.3 0.4 copy.114
  10.8 0.6 copy.139
  11.4 1.6 %copy.116 = f32[32,2,2,4,1,512]{5,3,2,1,4,0:T(4,128)} copy(f32[32,2,2,4,1,512]{5,0,3,2,1,4:T(8,128)S(1)} %bitcast.94) | data formatting | bytes 2097152 | tf_op jit(solution)/shard_map/reshape | solution.py:180
  13.0 6.1 %all-to-all-start = ((f32[32,2,2,4,1,512]{5,3,2,1,4,0:T(4,128)}), f32[32,2,2,4,1,512]{5,3,2,1,4,0:T(4,128)S(1)}, u32[]{:S(2)}, u32[]{:S(2)}) async-start(f32[32,2,2,4,1,512]{5,3,2,1,4,0:T(4,128)} %copy.116), calls=%async_computation | async-start | bytes 2097152 | tf_op jit(solution)/shard_map/all_to_all | solution.py:183
  19.3 0.1 dynamic-slice_bitcast_fusion
  19.4 0.6 pad_maximum_fusion.2.rates_ref
  20.2 0.7 squeeze.25.diag_ref
  20.9 0.1 reshape.296
  21.0 0.1 copy.133
  21.1 0.8 compare_select_fusion.2.mask_ref
  22.0 24.6 %all-to-all-done = f32[32,2,2,4,1,512]{5,3,2,1,4,0:T(4,128)S(1)} async-done(((f32[32,2,2,4,1,512]{5,3,2,1,4,0:T(4,128)}), f32[32,2,2,4,1,512]{5,3,2,1,4,0:T(4,128)S(1)}, u32[]{:S(2)}, u32[]{:S(2)}) %all-to-all-start) | async-done | bytes 1048608 | tf_op jit(solution)/shard_map/all_to_all | solution.py:183
  46.6 0.6 copy.138
  47.2 1.1 copy.118
  48.3 5.4 %shard_map.95.field_ref = f32[2,16,8,512]{3,2,1,0:T(8,128)} custom-call(f32[2,2]{1,0:T(2,128)} %pad_maximum_fusion.2.rates_ref, f32[16,1,512]{2,1,0:T(1,128)} %compare_select_fusion.2.mask_ref, f32[2,2,16,8,512]{4,3,2,1,0:T(8,128)} %bitcast.90, f32[2,2,16,512]{3,2,1,0:T(8,128)} %squeeze.25.diag_ref), custom_call_target="tpu_custom_call" | custom-call | flops 38797312 | bytes 1212416 | tf_op jit(solution)/shard_map/pallas_call | solution.py:74
  53.6 5.6 %shard_map.96 = f32[2,2,16,512]{3,2,1,0:T(8,128)} custom-call(f32[2,2]{1,0:T(2,128)} %pad_maximum_fusion.2.rates_ref, f32[16,1,512]{2,1,0:T(1,128)} %compare_select_fusion.2.mask_ref, f32[2,2,16,8,512]{4,3,2,1,0:T(8,128)} %bitcast.91, f32[2,16,8,512]{3,2,1,0:T(8,128)} %shard_map.95.field_ref), custom_call_target="tpu_custom_call" | custom-call | flops 51380224 | bytes 1605632 | tf_op jit(solution)/shard_map/pallas_call | solution.py:74
  59.3 0.9 collective-permute-start.4
  60.1 1.2 collective-permute-start.5
  61.3 0.7 multiply_reduce_fusion.2
  62.0 2.7 %collective-permute-done.3 = f32[2,2,16,512]{3,2,1,0:T(8,128)S(1)} collective-permute-done((f32[2,2,16,512]{3,2,1,0:T(8,128)}, f32[2,2,16,512]{3,2,1,0:T(8,128)S(1)}, u32[]{:S(2)}, u32[]{:S(2)}) %collective-permute-start.3) | collective-permute-done | bytes 131104 | tf_op jit(solution)/shard_map/ppermute | solution.py:147
  64.7 1.1 collective-permute-done.4
  65.8 0.4 collective-permute-done.5
  66.3 0.9 add_add_fusion.refs_0_
  67.2 0.6 fusion.12
  69.1 0.7 pad_maximum_fusion.3
  69.9 0.6 broadcast_in_dim.32
  70.5 3.7 %all-to-all-start.1 = ((f32[32,1,2]{2,1,0:T(1,128)}), f32[32,1,2]{2,1,0:T(1,128)S(1)}, u32[]{:S(2)}, u32[]{:S(2)}) async-start(f32[32,1,2]{2,1,0:T(1,128)} %broadcast_in_dim.32), calls=%async_computation.1 | async-start | bytes 32768 | tf_op jit(solution)/shard_map/all_to_all | solution.py:91
  74.2 5.4 %shard_map.97 = f32[2,16,8,512]{3,2,1,0:T(8,128)} custom-call(f32[2,2]{1,0:T(2,128)} %pad_maximum_fusion.2.rates_ref, f32[16,1,512]{2,1,0:T(1,128)} %compare_select_fusion.2.mask_ref, f32[2,2,16,8,512]{4,3,2,1,0:T(8,128)} %bitcast.92, f32[2,2,16,512]{3,2,1,0:T(8,128)} %copy-done.4, f32[2,2,16,512]{3,2,1,0:T(8,128)} %copy-done.2), custom_call_target="tpu_custom_call" | custom-call | flops 42991616 | bytes 1343488 | tf_op jit(solution)/shard_map/pallas_call | solution.py:74
  79.7 1.5 %all-to-all-done.1 = f32[32,1,2]{2,1,0:T(1,128)S(1)} async-done(((f32[32,1,2]{2,1,0:T(1,128)}), f32[32,1,2]{2,1,0:T(1,128)S(1)}, u32[]{:S(2)}, u32[]{:S(2)}) %all-to-all-start.1) | async-done | bytes 288 | tf_op jit(solution)/shard_map/all_to_all | solution.py:91
  81.1 0.1 reduce_sum.78
  81.2 0.6 fusion.19
  83.1 2.6 %multiply_reduce_fusion.1 = (f32[]{:T(128)}, f32[2,16,8,512]{3,2,1,0:T(8,128)}) fusion(f32[2,16,8,512]{3,2,1,0:T(8,128)S(1)} %copy-done, f32[2,16,8,512]{3,2,1,0:T(8,128)} %shard_map.97, f32[]{:T(128)S(6)} %div.25), kind=kLoop, calls=%fused_computation.17 | loop fusion | flops 655359 | bytes 1572872 | tf_op jit(solution)/shard_map/reduce_sum | solution.py:284
  85.7 5.6 %shard_map.98 = f32[2,2,16,512]{3,2,1,0:T(8,128)} custom-call(f32[2,2]{1,0:T(2,128)} %pad_maximum_fusion.2.rates_ref, f32[16,1,512]{2,1,0:T(1,128)} %compare_select_fusion.2.mask_ref, f32[2,2,16,8,512]{4,3,2,1,0:T(8,128)} %bitcast.93, f32[2,16,8,512]{3,2,1,0:T(8,128)} %get-tuple-element.39.field_ref), custom_call_target="tpu_custom_call" | custom-call | flops 51380224 | bytes 1605632 | tf_op jit(solution)/shard_map/pallas_call | solution.py:74
  91.3 1.2 broadcast_in_dim.33
  92.6 4.2 %all-to-all-start.2 = ((f32[32,1,1]{2,1,0:T(1,128)}), f32[32,1,1]{2,1,0:T(1,128)S(1)}, u32[]{:S(2)}, u32[]{:S(2)}) async-start(f32[32,1,1]{2,1,0:T(1,128)} %broadcast_in_dim.33), calls=%async_computation.2 | async-start | bytes 32768 | tf_op jit(solution)/shard_map/all_to_all | solution.py:91
  96.7 0.9 constant_dynamic-slice_fusion.4
  97.7 0.3 collective-permute-start.6
  98.0 1.7 %collective-permute-start.7 = (f32[2,2,4,512]{3,2,1,0:T(4,128)S(1)}, f32[2,2,4,512]{3,2,1,0:T(4,128)S(1)}, u32[]{:S(2)}, u32[]{:S(2)}) collective-permute-start(f32[2,2,4,512]{3,2,1,0:T(4,128)S(1)} %get-tuple-element.44), channel_id=1, source_target_pairs={{0,16},{8,24},{16,0},{24,8},{1,17},{9,25},{17,1},{25,9},{2,18},{10... | collective-permute-start | bytes 98312 | tf_op jit(solution)/shard_map/ppermute | solution.py:139
  99.7 1.3 collective-permute-start.8
  101.0 2.8 %all-to-all-done.2 = f32[32,1,1]{2,1,0:T(1,128)S(1)} async-done(((f32[32,1,1]{2,1,0:T(1,128)}), f32[32,1,1]{2,1,0:T(1,128)S(1)}, u32[]{:S(2)}, u32[]{:S(2)}) %all-to-all-start.2) | async-done | bytes 160 | tf_op jit(solution)/shard_map/all_to_all | solution.py:91
  103.8 0.6 reduce_sum.80
  105.8 0.8 multiply_reduce_fusion
  106.6 1.6 %fusion.13 = (f32[]{:T(128)}, f32[2,2,4,512]{3,2,1,0:T(4,128)S(1)}) fusion(f32[2,2,16,512]{3,2,1,0:T(8,128)} %copy-done.4, s32[]{:T(128)S(6)} %select_n.96, f32[2,2,16,512]{3,2,1,0:T(8,128)S(1)} %copy-done.3, f32[]{:T(128)S(6)} %div.26, f32[2,2,4,512]{3,2,1,0:T(4,128)S(1)} %collective-permute-done.8, f32[2,2,4,512]{3,2,1,0:T(4,128)S(1)} %collective-permute-done.7, ...), kind=kLoop, calls=%fused_computation.39 | loop fusion | flops 65535 | bytes 229388 | tf_op jit(solution)/shard_map/reduce_sum | solution.py:270
  109.4 8.8 %all_to_all.28 = f32[32,1,1]{2,1,0:T(1,128)S(1)} all-to-all(f32[32,1,1]{2,1,0:T(1,128)S(1)} %broadcast_in_dim.34), channel_id=1, replica_groups=mesh['tile'=4,'mem'=8] {'tile','mem'}, dimensions={0} | all-to-all | bytes 256 | tf_op jit(solution)/shard_map/all_to_all | solution.py:91
  118.2 0.6 reduce_sum.83
  120.2 0.1 multiply_add_fusion
  120.4 1.1 copy.123
  121.5 2.6 %all-to-all-start.4 = ((f32[32,2,4,1,512]{4,2,1,3,0:T(4,128)}), f32[32,2,4,1,512]{4,2,1,3,0:T(4,128)S(1)}, u32[]{:S(2)}, u32[]{:S(2)}) async-start(f32[32,2,4,1,512]{4,2,1,3,0:T(4,128)} %copy.123), calls=%async_computation.4 | async-start | bytes 1048576 | tf_op jit(solution)/shard_map/all_to_all | solution.py:223
  124.1 0.6 multiply_add_fusion.2
  124.7 15.7 %all-to-all-done.4 = f32[32,2,4,1,512]{4,2,1,3,0:T(4,128)S(1)} async-done(((f32[32,2,4,1,512]{4,2,1,3,0:T(4,128)}), f32[32,2,4,1,512]{4,2,1,3,0:T(4,128)S(1)}, u32[]{:S(2)}, u32[]{:S(2)}) %all-to-all-start.4) | async-done | bytes 524320 | tf_op jit(solution)/shard_map/all_to_all | solution.py:223
  140.5 0.3 copy.140
  140.8 0.3 copy.125
  141.1 1.0 copy.126
  (52 shorter events, 0.6 us)
Async XLA Ops:
  0.6 2.3 %copy-start.7 = (f32[1,4096]{1,0:T(1,128)S(1)}, f32[1,4096]{1,0:T(1,128)}, u32[]{:S(2)}) copy-start(f32[1,4096]{1,0:T(1,128)} %param.13) | copy-start | bytes 49156
  0.6 2.3 %copy-start.6 = (f32[1,4096]{1,0:T(1,128)S(1)}, f32[1,4096]{1,0:T(1,128)}, u32[]{:S(2)}) copy-start(f32[1,4096]{1,0:T(1,128)} %param.14) | copy-start | bytes 49156
  2.7 2.9 %copy-start.10 = (s32[4]{0:T(128)S(1)}, s32[4]{0:T(128)}, u32[]{:S(2)}) copy-start(s32[4]{0:T(128)} %param.16) | copy-start | bytes 52
  2.7 3.6 %copy-start.11 = (s32[4]{0:T(128)S(1)}, s32[4]{0:T(128)}, u32[]{:S(2)}) copy-start(s32[4]{0:T(128)} %param.17) | copy-start | bytes 52
  2.9 7.4 %copy-start.5 = (bf16[4,2,4,16,512]{4,3,2,1,0:T(8,128)(2,1)S(1)}, bf16[4,2,4,16,512]{4,3,2,1,0:T(8,128)(2,1)}, u32[]{:S(2)}) copy-start(bf16[4,2,4,16,512]{4,3,2,1,0:T(8,128)(2,1)} %param.12) | copy-start | bytes 1572868
  7.1 12.9 %collective-permute-start = (f32[9,4,512]{2,1,0:T(4,128)S(1)}, f32[9,4,512]{2,1,0:T(4,128)S(1)}, u32[]{:S(2)}, u32[]{:S(2)}) collective-permute-start(f32[9,4,512]{2,1,0:T(4,128)S(1)} %pad_maximum_fusion), channel_id=1, source_target_pairs={{0,24},{8,0},{16,8},{24,16},{1,25},{9,1},{17,9},{25,17},{2,26},{10... | collective-permute-start | bytes 221192 | tf_op jit(solution)/shard_map/ppermute | solution.py:123
  9.5 10.4 %collective-permute-start.1 = (f32[9,4,512]{2,1,0:T(4,128)S(1)}, f32[9,4,512]{2,1,0:T(4,128)S(1)}, u32[]{:S(2)}, u32[]{:S(2)}) collective-permute-start(f32[9,4,512]{2,1,0:T(4,128)S(1)} %pad_maximum_fusion), channel_id=1, source_target_pairs={{0,16},{8,24},{16,0},{24,8},{1,17},{9,25},{17,1},{25,9},{2,18},{10... | collective-permute-start | bytes 221192 | tf_op jit(solution)/shard_map/ppermute | solution.py:123
  10.2 9.8 %collective-permute-start.2 = (f32[9,4,512]{2,1,0:T(4,128)S(1)}, f32[9,4,512]{2,1,0:T(4,128)S(1)}, u32[]{:S(2)}, u32[]{:S(2)}) collective-permute-start(f32[9,4,512]{2,1,0:T(4,128)S(1)} %pad_maximum_fusion), channel_id=1, source_target_pairs={{0,8},{8,16},{16,24},{24,0},{1,9},{9,17},{17,25},{25,1},{2,10},{10... | collective-permute-start | bytes 221192 | tf_op jit(solution)/shard_map/ppermute | solution.py:123
  11.4 7.9 %copy-start.8 = (f32[16]{0:T(128)S(1)}, f32[16]{0:T(128)}, u32[]{:S(2)}) copy-start(f32[16]{0:T(128)} %param.19) | copy-start | bytes 196
  11.4 7.9 %copy-start.9 = (f32[16]{0:T(128)S(1)}, f32[16]{0:T(128)}, u32[]{:S(2)}) copy-start(f32[16]{0:T(128)} %param.18) | copy-start | bytes 196
  13.0 33.5 %all-to-all-start = ((f32[32,2,2,4,1,512]{5,3,2,1,4,0:T(4,128)}), f32[32,2,2,4,1,512]{5,3,2,1,4,0:T(4,128)S(1)}, u32[]{:S(2)}, u32[]{:S(2)}) async-start(f32[32,2,2,4,1,512]{5,3,2,1,4,0:T(4,128)} %copy.116), calls=%async_computation | async-start | bytes 2097152 | tf_op jit(solution)/shard_map/all_to_all | solution.py:183
  21.1 46.1 %copy-start.4 = (f32[2,2,16,512]{3,2,1,0:T(8,128)}, f32[2,2,16,512]{3,2,1,0:T(8,128)S(1)}, u32[]{:S(2)}) copy-start(f32[2,2,16,512]{3,2,1,0:T(8,128)S(1)} %squeeze.26.diag_ref) | copy-start | bytes 393220
  53.6 7.7 %copy-start = (f32[2,16,8,512]{3,2,1,0:T(8,128)S(1)}, f32[2,16,8,512]{3,2,1,0:T(8,128)}, u32[]{:S(2)}) copy-start(f32[2,16,8,512]{3,2,1,0:T(8,128)} %shard_map.95.field_ref) | copy-start | bytes 1572868
  59.3 5.5 %collective-permute-start.3 = (f32[2,2,16,512]{3,2,1,0:T(8,128)}, f32[2,2,16,512]{3,2,1,0:T(8,128)S(1)}, u32[]{:S(2)}, u32[]{:S(2)}) collective-permute-start(f32[2,2,16,512]{3,2,1,0:T(8,128)} %shard_map.96), channel_id=1, source_target_pairs={{0,8},{8,16},{16,24},{24,0},{1,9},{9,17},{17,25},{25,1},{2,10},{10... | collective-permute-start | bytes 393224 | tf_op jit(solution)/shard_map/ppermute | solution.py:147
  59.3 6.6 %collective-permute-start.4 = (f32[2,2,16,512]{3,2,1,0:T(8,128)}, f32[2,2,16,512]{3,2,1,0:T(8,128)S(1)}, u32[]{:S(2)}, u32[]{:S(2)}) collective-permute-start(f32[2,2,16,512]{3,2,1,0:T(8,128)} %shard_map.96), channel_id=1, source_target_pairs={{0,16},{8,24},{16,0},{24,8},{1,17},{9,25},{17,1},{25,9},{2,18},{10... | collective-permute-start | bytes 393224 | tf_op jit(solution)/shard_map/ppermute | solution.py:147
  60.1 6.1 %collective-permute-start.5 = (f32[2,2,16,512]{3,2,1,0:T(8,128)}, f32[2,2,16,512]{3,2,1,0:T(8,128)S(1)}, u32[]{:S(2)}, u32[]{:S(2)}) collective-permute-start(f32[2,2,16,512]{3,2,1,0:T(8,128)} %shard_map.96), channel_id=1, source_target_pairs={{0,24},{8,0},{16,8},{24,16},{1,25},{9,1},{17,9},{25,17},{2,26},{10... | collective-permute-start | bytes 393224 | tf_op jit(solution)/shard_map/ppermute | solution.py:147
  67.2 7.0 %copy-start.2 = (f32[2,2,16,512]{3,2,1,0:T(8,128)}, f32[2,2,16,512]{3,2,1,0:T(8,128)S(1)}, u32[]{:S(2)}) copy-start(f32[2,2,16,512]{3,2,1,0:T(8,128)S(1)} %add_add_fusion.refs_0_) | copy-start | bytes 393220
  70.5 10.6 %all-to-all-start.1 = ((f32[32,1,2]{2,1,0:T(1,128)}), f32[32,1,2]{2,1,0:T(1,128)S(1)}, u32[]{:S(2)}, u32[]{:S(2)}) async-start(f32[32,1,2]{2,1,0:T(1,128)} %broadcast_in_dim.32), calls=%async_computation.1 | async-start | bytes 32768 | tf_op jit(solution)/shard_map/all_to_all | solution.py:91
  83.1 23.5 %copy-start.3 = (f32[2,2,16,512]{3,2,1,0:T(8,128)S(1)}, f32[2,2,16,512]{3,2,1,0:T(8,128)}, u32[]{:S(2)}) copy-start(f32[2,2,16,512]{3,2,1,0:T(8,128)} %copy-done.2) | copy-start | bytes 393220
  85.7 20.1 %copy-start.1 = (f32[2,16,8,512]{3,2,1,0:T(8,128)S(1)}, f32[2,16,8,512]{3,2,1,0:T(8,128)}, u32[]{:S(2)}) copy-start(f32[2,16,8,512]{3,2,1,0:T(8,128)} %get-tuple-element.39.field_ref) | copy-start | bytes 1572868
  92.6 11.2 %all-to-all-start.2 = ((f32[32,1,1]{2,1,0:T(1,128)}), f32[32,1,1]{2,1,0:T(1,128)S(1)}, u32[]{:S(2)}, u32[]{:S(2)}) async-start(f32[32,1,1]{2,1,0:T(1,128)} %broadcast_in_dim.33), calls=%async_computation.2 | async-start | bytes 32768 | tf_op jit(solution)/shard_map/all_to_all | solution.py:91
  97.7 8.8 %collective-permute-start.6 = (f32[2,2,4,512]{3,2,1,0:T(4,128)S(1)}, f32[2,2,4,512]{3,2,1,0:T(4,128)S(1)}, u32[]{:S(2)}, u32[]{:S(2)}) collective-permute-start(f32[2,2,4,512]{3,2,1,0:T(4,128)S(1)} %get-tuple-element.42), channel_id=1, source_target_pairs={{0,8},{8,16},{16,24},{24,0},{1,9},{9,17},{17,25},{25,1},{2,10},{10... | collective-permute-start | bytes 98312 | tf_op jit(solution)/shard_map/ppermute | solution.py:139
  98.0 8.5 %collective-permute-start.7 = (f32[2,2,4,512]{3,2,1,0:T(4,128)S(1)}, f32[2,2,4,512]{3,2,1,0:T(4,128)S(1)}, u32[]{:S(2)}, u32[]{:S(2)}) collective-permute-start(f32[2,2,4,512]{3,2,1,0:T(4,128)S(1)} %get-tuple-element.44), channel_id=1, source_target_pairs={{0,16},{8,24},{16,0},{24,8},{1,17},{9,25},{17,1},{25,9},{2,18},{10... | collective-permute-start | bytes 98312 | tf_op jit(solution)/shard_map/ppermute | solution.py:139
  99.7 6.9 %collective-permute-start.8 = (f32[2,2,4,512]{3,2,1,0:T(4,128)S(1)}, f32[2,2,4,512]{3,2,1,0:T(4,128)S(1)}, u32[]{:S(2)}, u32[]{:S(2)}) collective-permute-start(f32[2,2,4,512]{3,2,1,0:T(4,128)S(1)} %get-tuple-element.43), channel_id=1, source_target_pairs={{0,24},{8,0},{16,8},{24,16},{1,25},{9,1},{17,9},{25,17},{2,26},{10... | collective-permute-start | bytes 98312 | tf_op jit(solution)/shard_map/ppermute | solution.py:139
  121.5 19.0 %all-to-all-start.4 = ((f32[32,2,4,1,512]{4,2,1,3,0:T(4,128)}), f32[32,2,4,1,512]{4,2,1,3,0:T(4,128)S(1)}, u32[]{:S(2)}, u32[]{:S(2)}) async-start(f32[32,2,4,1,512]{4,2,1,3,0:T(4,128)} %copy.123), calls=%async_computation.4 | async-start | bytes 1048576 | tf_op jit(solution)/shard_map/all_to_all | solution.py:223
